TPU v7x, 32 devices: a whole 2x2x4 slice. The times are simulated.
32 devices in a mesh: row: 16 (over z, y, core), col: 2 (over x).
Axes of the slice: x: 2, y: 2, z: 4, core: 2. Of those that a mesh axis runs over, the one named last changes fastest.
Arguments:
- acts: bfloat16 [1024, 28672], P('row', 'col'), may hold values from -6 to 6
- grads: bfloat16 [1024, 8192], P('col', 'row'), may hold values from -6 to 6
- basis_in: bfloat16 [28672, 28672], P('row', 'col'), may hold values from -0.03125 to 0.03125
- basis_out: bfloat16 [8192, 8192], P('col', 'row'), may hold values from -0.0625 to 0.0625
- corr: float32 [28672, 8192], P('row', 'col'), may hold values from 0.5 to 2
Outputs:
- new_corr: float32 [28672, 8192], P('row', 'col')
All inputs are finite; a program needn't handle non-finite values.
Results may differ from a plain program's by a relative error of at most 0.0026.
Values may be sent and summed in bfloat16 or wider, within the bound.
No kernel may reach another device: no remote copies, remote signals or barrier semaphores. Data moves between devices by JAX's collectives and lax.ppermute only.
A program may use at most 320 MiB of HBM per device.

v0:
```python
import jax
import jax.numpy as jnp
from jax import lax
from jax.sharding import PartitionSpec as P

SEQ_LEN = 512
SEQS = 2


def rotate_rows(token_rows, basis_tile):
    return lax.dot_general(
        token_rows, basis_tile, (((1,), (1,)), ((), ())), preferred_element_type=jnp.float32
    )


def local(acts, grads, basis_in, basis_out, corr):
    act_partial = rotate_rows(lax.all_gather(acts, "row", axis=0, tiled=True), basis_in)
    act_rot = lax.psum(act_partial, "col").astype(jnp.bfloat16)
    grad_all = lax.all_gather(grads, "col", axis=0, tiled=True)
    grad_share = lax.psum_scatter(
        rotate_rows(grad_all, basis_out), "row", scatter_dimension=0, tiled=True
    ).astype(jnp.bfloat16)
    grad_rot = lax.all_gather(grad_share, "row", axis=0, tiled=True)
    act_seqs = act_rot.reshape(SEQS, SEQ_LEN, act_rot.shape[1])
    grad_seqs = grad_rot.reshape(SEQS, SEQ_LEN, grad_rot.shape[1])
    seq_grad = jnp.einsum("stk,stm->skm", act_seqs, grad_seqs, preferred_element_type=jnp.float32)
    scale_factor = 1.0 / (SEQS * SEQ_LEN)
    return corr + jnp.sum(seq_grad * seq_grad, axis=0) * scale_factor


def solution(mesh):
    return jax.shard_map(
        local,
        mesh=mesh,
        in_specs=(
            P("row", "col"),
            P("col", "row"),
            P("row", "col"),
            P("col", "row"),
            P("row", "col"),
        ),
        out_specs=P("row", "col"),
        check_vma=False,
    )
```

profile of v0, /device:TPU:0, one launch (start us, length us, event | category | flops | bytes accessed | tf_op | source)
XLA Modules:
  0.0 681.3 jit_solution(7208082654567431498)
XLA Ops:
  6.5 0.0 all-gather.6.cloned.1.call-start
  6.5 0.7 all-gather.6.cloned.1.call-update
  7.3 0.0 reduce-scatter.2.cloned.1.call-start
  7.3 25.6 %all-gather.6.cloned.1.call-done = bf16[1024,512]{1,0:T(8,128)(2,1)} async-done(((bf16[512,512]{1,0:T(8,128)(2,1)}), bf16[1024,512]{1,0:T(8,128)(2,1)}) %all-gather.6.cloned.1.call-update) | async-done | bytes 1048592 | tf_op jit(solution)/shard_map/all_gather | solution.py:19
  32.9 13.2 %fusion.1 = f32[1024,4096]{1,0:T(8,128)} fusion(bf16[1024,512]{1,0:T(8,128)(2,1)} %all-gather.6.cloned.1.call-done, bf16[4096,512]{1,0:T(8,128)(2,1)} %param.8), kind=kOutput, calls=%fused_computation.3 | convolution fusion | flops 4294967296 | bytes 22020096 | tf_op jit(solution)/shard_map/dot_general | solution.py:11
  46.1 0.0 reduce-scatter.2.cloned.1.call-update
  46.2 0.0 all-gather.4.cloned.1.call-start
  46.2 0.7 all-gather.4.cloned.1.call-update
  46.9 0.0 all-gather.8.cloned.1.call-start
  46.9 176.7 %reduce-scatter.2.cloned.1.call-done = f32[64,4096]{1,0:T(8,128)} async-done(((f32[1024,4096]{1,0:T(8,128)}), f32[64,4096]{1,0:T(8,128)}) %reduce-scatter.2.cloned.1.call-update) | async-done | bytes 1048592 | tf_op jit(solution)/shard_map/reduce_scatter | solution.py:20
  223.6 2.1 convert_element_type.7
  225.7 0.0 all-gather.8.cloned.1.call-update
  225.7 146.9 %all-gather.4.cloned.1.call-done = bf16[1024,14336]{1,0:T(8,128)(2,1)} async-done(((bf16[64,14336]{1,0:T(8,128)(2,1)}), bf16[1024,14336]{1,0:T(8,128)(2,1)}) %all-gather.4.cloned.1.call-update) | async-done | bytes 29360144 | tf_op jit(solution)/shard_map/all_gather | solution.py:17
  372.7 62.0 %fusion = f32[1024,1792]{1,0:T(8,128)} fusion(bf16[1024,14336]{1,0:T(8,128)(2,1)} %all-gather.4.cloned.1.call-done, bf16[1792,14336]{1,0:T(8,128)(2,1)} %param.7), kind=kOutput, calls=%fused_computation.2 | convolution fusion | flops 52613349376 | bytes 88080384 | tf_op jit(solution)/shard_map/dot_general | solution.py:11
  434.7 172.3 %all-reduce.1 = bf16[1024,1792]{1,0:T(8,128)(2,1)} all-reduce(f32[1024,1792]{1,0:T(8,128)} %fusion), channel_id=1, replica_groups=mesh['row'=16,'col'=2] {'col'}, use_global_device_ids=true, to_apply=%region_0.0 | all-reduce | flops 1835008 | bytes 11010048 | tf_op jit(solution)/shard_map/psum | solution.py:18
  607.0 0.0 all-gather.8.cloned.1.call-done
  607.0 38.0 %multiply_reduce_fusion = f32[1792,4096]{1,0:T(8,128)} fusion(bf16[2,512,1792]{2,1,0:T(8,128)(2,1)} %bitcast.8, bf16[2,512,4096]{2,1,0:T(8,128)(2,1)} %bitcast.9), kind=kOutput, calls=%fused_computation | convolution fusion | flops 15054405632 | bytes 41418752 | tf_op jit(solution)/shard_map/stk,stm->skm/dot_general | solution.py:26
  645.0 29.8 %multiply_add_fusion = f32[1792,4096]{1,0:T(8,128)} fusion(f32[1792,4096]{1,0:T(8,128)} %param.9, f32[1792,4096]{1,0:T(8,128)} %multiply_reduce_fusion), kind=kLoop, calls=%fused_computation.1 | loop fusion | flops 14680064 | bytes 88080384 | tf_op jit(solution)/shard_map/add | solution.py:28
Async XLA Ops:
  6.5 26.4 %all-gather.6.cloned.1.call-start = ((), (), s32[]{:S(2)}) async-start(), calls=%async_computation.2 | async-start | bytes 1572864 | tf_op jit(solution)/shard_map/all_gather | solution.py:19
  7.3 216.4 %reduce-scatter.2.cloned.1.call-start = ((), (), s32[]{:S(2)}) async-start(), calls=%async_computation.3 | async-start | bytes 17825792 | tf_op jit(solution)/shard_map/reduce_scatter | solution.py:20
  46.2 326.5 %all-gather.4.cloned.1.call-start = ((), (), s32[]{:S(2)}) async-start(), calls=%async_computation.1 | async-start | bytes 31195136 | tf_op jit(solution)/shard_map/all_gather | solution.py:17
  46.9 560.1 %all-gather.8.cloned.1.call-start = ((), (), s32[]{:S(2)}) async-start(), calls=%async_computation.4 | async-start | bytes 8912896 | tf_op jit(solution)/shard_map/all_gather | solution.py:23
Sparse Core Ops, SparseCore 0:
  8.9 23.9 all-gather.5
  46.3 177.3 reduce-scatter.1
  225.2 147.3 all-gather.3
  374.7 74.2 all-gather.7
where the time goes:
time: 681 us
  waiting for transfers between devices  351 us (52%)
  blocking collectives  172 us (25%)
  matrix products  113 us (17%)
  other arithmetic  31.8 us (5%)
  between operations  13.1 us (2%)
    reduce_scatter x1, waiting for transfers between devices, local(): lax.psum_scatter(rotate_rows(grad_all, basis_out), 'row', scatter_dimensi...  177 us
    psum x1, blocking collectives, local(): act_rot = lax.psum(act_partial, 'col').astype(jnp.bfloat16)  172 us
    all_gather x1, waiting for transfers between devices, local(): lax.all_gather(acts, 'row', axis=0, tiled=True)  147 us
    dot_general x2, matrix products, rotate_rows(): lax.dot_general(token_rows, basis_tile, (((1,), (1,)), ((), ())), preferr...  75.3 us
    dot_general x1, matrix products, local(): jnp.einsum('stk,stm->skm', act_seqs, grad_seqs, preferred_element_type=jn...  38 us
    add x1, other arithmetic, local(): return corr + jnp.sum(seq_grad * seq_grad, axis=0) * scale_factor  29.8 us
    all_gather x1, waiting for transfers between devices, local(): grad_all = lax.all_gather(grads, 'col', axis=0, tiled=True)  25.6 us
  transfers between devices with their start and end apart: 4, of which 3 were waited for; matrix products, arithmetic and copies ran while one was open for 9% of the time, Pallas kernels for 0%

commit v1 on v0

v1 whole, which is shorter than its diff:
```python
import jax
import jax.numpy as jnp
import numpy as np
from jax import lax
from jax.sharding import Mesh
from jax.sharding import PartitionSpec as P

SEQ_LEN = 512
SEQS = 2
CHUNKS = 2
ROW = ("rchip", "core")


def swap_perm(n):
    return [(i, i ^ 1) for i in range(n)]


def local(acts, grads, basis_in, basis_out, corr):
    n_chip = lax.axis_size("rchip")
    n_row = n_chip * 2
    n_col = lax.axis_size("col")
    tok_dev = acts.shape[0]
    half = tok_dev // CHUNKS
    tokens = tok_dev * n_row

    act_t = []
    for c in range(CHUNKS):
        gathered = lax.all_gather(acts[c * half:(c + 1) * half], ROW, axis=0, tiled=True)
        part = lax.dot_general(
            basis_in, gathered, (((1,), (1,)), ((), ())), preferred_element_type=jnp.float32
        )
        if n_col == 2:
            other = lax.ppermute(part.astype(jnp.bfloat16), "col", swap_perm(2))
            act_t.append((part + other.astype(jnp.float32)).astype(jnp.bfloat16))
        else:
            act_t.append(lax.psum(part, "col").astype(jnp.bfloat16))

    g_all = lax.all_gather(grads, "col", axis=0, tiled=True)
    g_all = g_all.reshape(n_row, CHUNKS, half, g_all.shape[1]).transpose(1, 0, 2, 3)
    g_all = g_all.reshape(tokens, grads.shape[1])
    g_part = lax.dot_general(
        g_all, basis_out, (((1,), (1,)), ((), ())), preferred_element_type=jnp.float32
    )
    core = lax.axis_index("core")
    pair = tokens // 2
    keep = lax.dynamic_slice_in_dim(g_part, core * pair, pair, axis=0)
    send = lax.dynamic_slice_in_dim(g_part, (1 - core) * pair, pair, axis=0)
    summed = keep + lax.ppermute(send, "core", swap_perm(2))
    share = lax.psum_scatter(summed, "rchip", scatter_dimension=0, tiled=True)
    grad_rot = lax.all_gather(share.astype(jnp.bfloat16), ("core", "rchip"), axis=0, tiled=True)

    seg = n_row * half // SEQS
    a = jnp.concatenate(act_t, axis=1).reshape(basis_in.shape[0], CHUNKS, SEQS, seg)
    g = grad_rot.reshape(CHUNKS, SEQS, seg, grad_rot.shape[1])
    seq_grad = jnp.einsum("kcsu,csum->skm", a, g, preferred_element_type=jnp.float32)
    scale_factor = 1.0 / (SEQS * SEQ_LEN)
    return corr + jnp.sum(seq_grad * seq_grad, axis=0) * scale_factor


def solution(mesh):
    devices = np.asarray(mesh.devices)
    n_row, n_col = devices.shape
    inner = Mesh(devices.reshape(n_row // 2, 2, n_col), ("rchip", "core", "col"))
    return jax.shard_map(
        local,
        mesh=inner,
        in_specs=(
            P(ROW, "col"),
            P("col", ROW),
            P(ROW, "col"),
            P("col", ROW),
            P(ROW, "col"),
        ),
        out_specs=P(ROW, "col"),
        check_vma=False,
    )
```

time: 681 us -> 547 us (0.80)
  blocking collectives: 172 us -> 0 us
  other arithmetic: 31.8 us -> 45.9 us
  local copies, waits for them, and re-layouts: 0 us -> 12.7 us
    psum x1 -> x0, blocking collectives: 172 us -> none  [local(): act_rot = lax.psum(act_partial, 'col').astype(jnp.bfloat16)]
    all_gather x3 -> x4, waiting for transfers between devices: 173 us -> 63.5 us  [the longest x2 37.9 us: local(): lax.all_gather(acts[c * half:(c + 1) * half], ROW, axis=0, tiled=True)]
    reduce_scatter x1, waiting for transfers between devices: 177 us -> 237 us  [local(): share = lax.psum_scatter(summed, 'rchip', scatter_dimension=0, tiled=True)]
    ppermute x0 -> x3, waiting for transfers between devices: none -> 54 us  [the longest x2 40.5 us: local(): other = lax.ppermute(part.astype(jnp.bfloat16), 'col', swap_perm(2))]
    add x0 -> x1, other arithmetic: none -> 11.3 us  [local(): summed = keep + lax.ppermute(send, 'core', swap_perm(2))]
    dot_general x3 -> x4, matrix products: 113 us -> 115 us  [the longest x2 70.2 us: local(): lax.dot_general(basis_in, gathered, (((1,), (1,)), ((), ())), preferred_e...]
  transfers between devices with their start and end apart: 4 -> 8, of which waited for: 3 -> 5; matrix products, arithmetic and copies ran while one was open for 9% -> 14% of each run, Pallas kernels for 0% -> 0%
where the time goes in v1:
time: 547 us
  waiting for transfers between devices  356 us (65%)
  matrix products  115 us (21%)
  other arithmetic  45.9 us (8%)
  between operations  15.1 us (3%)
  local copies, waits for them, and re-layouts  12.7 us (2%)
    reduce_scatter x1, waiting for transfers between devices, local(): share = lax.psum_scatter(summed, 'rchip', scatter_dimension=0, tiled=True)  237 us
    dot_general x2, matrix products, local(): lax.dot_general(basis_in, gathered, (((1,), (1,)), ((), ())), preferred_e...  70.2 us
    ppermute x2, waiting for transfers between devices, local(): other = lax.ppermute(part.astype(jnp.bfloat16), 'col', swap_perm(2))  40.5 us
    dot_general x1, matrix products, local(): jnp.einsum('kcsu,csum->skm', a, g, preferred_element_type=jnp.float32)  38.2 us
    all_gather x2, waiting for transfers between devices, local(): lax.all_gather(acts[c * half:(c + 1) * half], ROW, axis=0, tiled=True)  37.9 us
    add x1, other arithmetic, local(): return corr + jnp.sum(seq_grad * seq_grad, axis=0) * scale_factor  29.8 us
    all_gather x1, waiting for transfers between devices, local(): g_all = lax.all_gather(grads, 'col', axis=0, tiled=True)  25.6 us
    ppermute x1, waiting for transfers between devices, local(): summed = keep + lax.ppermute(send, 'core', swap_perm(2))  13.5 us
  transfers between devices with their start and end apart: 8, of which 5 were waited for; matrix products, arithmetic and copies ran while one was open for 14% of the time, Pallas kernels for 0%

profile of v1, /device:TPU:0, one launch (start us, length us, event | category | flops | bytes accessed | tf_op | source)
XLA Modules:
  0.0 546.9 jit_solution(15517978028183526998)
XLA Ops:
  7.4 0.7 all-gather.9.cloned.1.call-update
  8.1 25.6 %all-gather.9.cloned.1.call-done = bf16[1024,512]{1,0:T(8,128)(2,1)} async-done(((bf16[512,512]{1,0:T(8,128)(2,1)}), bf16[1024,512]{1,0:T(8,128)(2,1)}) %all-gather.9.cloned.1.call-update) | async-done | bytes 1048592 | tf_op jit(solution)/shard_map/all_gather | solution.py:38
  33.7 1.3 copy.10
  35.0 6.4 %fusion.4 = f32[1024,4096]{1,0:T(8,128)S(1)} fusion(bf16[1024,512]{1,0:T(8,128)(2,1)S(1)} %bitcast.20, bf16[4096,512]{1,0:T(8,128)(2,1)} %param.8), kind=kOutput, calls=%fused_computation.11 | convolution fusion | flops 4294967296 | bytes 22020096 | tf_op jit(solution)/shard_map/dot_general | solution.py:41
  41.4 4.1 constant_dynamic-slice_fusion
  45.5 4.6 copy-done
  50.1 13.5 %collective-permute-done.2 = f32[512,4096]{1,0:T(8,128)} collective-permute-done((f32[512,4096]{1,0:T(8,128)}, f32[512,4096]{1,0:T(8,128)}, u32[]{:S(2)}, u32[]{:S(2)}) %collective-permute-start.2) | collective-permute-done | bytes 8388640 | tf_op jit(solution)/shard_map/ppermute | solution.py:48
  63.6 11.3 %dynamic-slice_add_fusion = f32[512,4096]{1,0:T(8,128)} fusion(f32[512,4096]{1,0:T(8,128)} %collective-permute-done.2, f32[1024,4096]{1,0:T(8,128)} %copy-done, s32[]{:T(128)S(6)} %select_n.6), kind=kLoop, calls=%fused_computation.3 | loop fusion | flops 2097152 | bytes 25165828 | tf_op jit(solution)/shard_map/add | solution.py:48
  75.0 1.4 copy-done.2
  76.4 1.3 fusion.1
  77.8 0.5 all-gather.5.cloned.1.call-update
  78.6 237.0 %reduce-scatter.2.cloned.1.call-done = f32[64,4096]{1,0:T(8,128)} async-done(((f32[512,4096]{1,0:T(8,128)}), f32[64,4096]{1,0:T(8,128)}) %reduce-scatter.2.cloned.1.call-update) | async-done | bytes 1048592 | tf_op jit(solution)/shard_map/reduce_scatter | solution.py:49
  315.6 2.1 convert_element_type.27
  317.7 35.7 %fusion.2 = (bf16[1792,512]{0,1:T(8,128)(2,1)}, f32[1792,512]{0,1:T(8,128)}) fusion(bf16[1792,14336]{1,0:T(8,128)(2,1)} %param.7, bf16[512,14336]{1,0:T(8,128)(2,1)} %all-gather.7.cloned.1.call-done), kind=kOutput, calls=%fused_computation.9 | convolution fusion | flops 26307592192 | bytes 71565312 | tf_op jit(solution)/shard_map/dot_general | solution.py:29
  353.4 0.8 collective-permute-start.1
  354.2 37.9 %all-gather.5.cloned.1.call-done = bf16[512,14336]{1,0:T(8,128)(2,1)} async-done(((bf16[32,14336]{1,0:T(8,128)(2,1)}), bf16[512,14336]{1,0:T(8,128)(2,1)}) %all-gather.5.cloned.1.call-update) | async-done | bytes 14680080 | tf_op jit(solution)/shard_map/all_gather | solution.py:28
  392.1 34.6 %fusion.3 = (bf16[1792,512]{0,1:T(8,128)(2,1)}, f32[1792,512]{0,1:T(8,128)S(1)}) fusion(bf16[1792,14336]{1,0:T(8,128)(2,1)} %param.7, bf16[512,14336]{1,0:T(8,128)(2,1)} %all-gather.5.cloned.1.call-done), kind=kOutput, calls=%fused_computation.10 | convolution fusion | flops 26307592192 | bytes 71565312 | tf_op jit(solution)/shard_map/dot_general | solution.py:29
  426.6 1.5 collective-permute-start
  428.1 0.4 add_convert_fusion
  428.4 40.5 %collective-permute-done = bf16[1792,512]{0,1:T(8,128)(2,1)S(1)} collective-permute-done((bf16[1792,512]{0,1:T(8,128)(2,1)}, bf16[1792,512]{0,1:T(8,128)(2,1)S(1)}, u32[]{:S(2)}, u32[]{:S(2)}) %collective-permute-start) | collective-permute-done | bytes 1835040 | tf_op jit(solution)/shard_map/ppermute | solution.py:33
  469.0 0.4 add_convert_fusion.1
  469.4 2.0 pad_maximum_fusion
  471.4 38.2 %fusion = f32[1792,4096]{1,0:T(8,128)} fusion(bf16[1792,2,2,256]{0,3,2,1:T(8,128)(2,1)} %bitcast.18, bf16[2,2,256,4096]{3,2,1,0:T(8,128)(2,1)} %bitcast.21), kind=kOutput, calls=%fused_computation.1 | convolution fusion | flops 15054405632 | bytes 41418752 | tf_op jit(solution)/shard_map/kcsu,csum->skm/dot_general | solution.py:55
  509.6 29.8 %multiply_add_fusion = f32[1792,4096]{1,0:T(8,128)} fusion(f32[1792,4096]{1,0:T(8,128)} %param.9, f32[1792,4096]{1,0:T(8,128)} %fusion), kind=kLoop, calls=%fused_computation.2 | loop fusion | flops 14680064 | bytes 88080384 | tf_op jit(solution)/shard_map/add | solution.py:57
  (16 shorter events, 0.4 us)
Async XLA Ops:
  7.4 26.4 %all-gather.9.cloned.1.call-start = ((), (), s32[]{:S(2)}) async-start(), calls=%async_computation.3 | async-start | bytes 1572864 | tf_op jit(solution)/shard_map/all_gather | solution.py:38
  8.1 307.5 %reduce-scatter.2.cloned.1.call-start = ((), (), s32[]{:S(2)}) async-start(), calls=%async_computation.4 | async-start | bytes 9437184 | tf_op jit(solution)/shard_map/reduce_scatter | solution.py:49
  41.4 8.7 %copy-start = (f32[1024,4096]{1,0:T(8,128)}, f32[1024,4096]{1,0:T(8,128)S(1)}, u32[]{:S(2)}) copy-start(f32[1024,4096]{1,0:T(8,128)S(1)} %fusion.4) | copy-start | bytes 50331652
  50.1 13.5 %collective-permute-start.2 = (f32[512,4096]{1,0:T(8,128)}, f32[512,4096]{1,0:T(8,128)}, u32[]{:S(2)}, u32[]{:S(2)}) collective-permute-start(f32[512,4096]{1,0:T(8,128)} %constant_dynamic-slice_fusion), channel_id=1, source_target_pairs={{0,2},{2,0},{1,3},{3,1},{4,6},{6,4},{5,7},{7,5},{8,10},{10,8},{9,1... | collective-permute-start | bytes 25165832 | tf_op jit(solution)/shard_map/ppermute | solution.py:48
  74.9 1.5 copy-start.2
  74.9 242.8 %all-gather.7.cloned.1.call-start = ((), (), s32[]{:S(2)}) async-start(), calls=%async_computation.2 | async-start | bytes 15597568 | tf_op jit(solution)/shard_map/all_gather | solution.py:28
  77.8 314.3 %all-gather.5.cloned.1.call-start = ((), (), s32[]{:S(2)}) async-start(), calls=%async_computation.1 | async-start | bytes 15597568 | tf_op jit(solution)/shard_map/all_gather | solution.py:28
  78.3 393.0 %all-gather.11.cloned.1.call-start = ((), (), s32[]{:S(2)}) async-start(), calls=%async_computation.5 | async-start | bytes 8912896 | tf_op jit(solution)/shard_map/all_gather | solution.py:50
  353.4 74.7 %collective-permute-start.1 = (bf16[1792,512]{0,1:T(8,128)(2,1)}, bf16[1792,512]{0,1:T(8,128)(2,1)S(1)}, u32[]{:S(2)}, u32[]{:S(2)}) collective-permute-start(bf16[1792,512]{0,1:T(8,128)(2,1)} %get-tuple-element.7), channel_id=1, source_target_pairs={{0,1},{1,0},{2,3},{3,2},{4,5},{5,4},{6,7},{7,6},{8,9},{9,8},{10,11... | collective-permute-start | bytes 5505032 | tf_op jit(solution)/shard_map/ppermute | solution.py:33
  392.1 36.0 %copy-start.1 = (f32[1792,512]{0,1:T(8,128)S(1)}, f32[1792,512]{0,1:T(8,128)}, u32[]{:S(2)}) copy-start(f32[1792,512]{0,1:T(8,128)} %get-tuple-element.8) | copy-start | bytes 11010052
  426.6 42.4 %collective-permute-start = (bf16[1792,512]{0,1:T(8,128)(2,1)}, bf16[1792,512]{0,1:T(8,128)(2,1)S(1)}, u32[]{:S(2)}, u32[]{:S(2)}) collective-permute-start(bf16[1792,512]{0,1:T(8,128)(2,1)} %get-tuple-element.9), channel_id=1, source_target_pairs={{0,1},{1,0},{2,3},{3,2},{4,5},{5,4},{6,7},{7,6},{8,9},{9,8},{10,11... | collective-permute-start | bytes 5505032 | tf_op jit(solution)/shard_map/ppermute | solution.py:33
Sparse Core Ops, SparseCore 0:
  9.7 23.9 all-gather.8
  75.0 240.5 reduce-scatter.1
Sparse Core Ops, SparseCore 1:
  77.8 165.9 all-gather.6
  245.9 146.1 all-gather.4
  394.2 72.2 all-gather.10

commit v2 on v1

--- a/solution.py
+++ b/solution.py
@@ -1,3 +1,5 @@
+import functools
+
 import jax
 import jax.numpy as jnp
 import numpy as np
@@ -15,7 +17,51 @@
     return [(i, i ^ 1) for i in range(n)]
 
 
-def local(acts, grads, basis_in, basis_out, corr):
+def chip_ring(devices):
+    n_chip = devices.shape[0] // 2
+    coords = [getattr(devices[2 * i, 0], "coords", None) for i in range(n_chip)]
+    if any(c is None for c in coords):
+        return list(range(n_chip))
+    coords = [tuple(c) for c in coords]
+    vary = [d for d in range(len(coords[0])) if len({c[d] for c in coords}) > 1]
+    if len(vary) == 1:
+        return sorted(range(n_chip), key=lambda i: coords[i][vary[0]])
+    if len(vary) != 2:
+        return list(range(n_chip))
+    a, b = vary
+    if len({c[a] for c in coords}) != 2:
+        a, b = b, a
+    if len({c[a] for c in coords}) != 2:
+        return list(range(n_chip))
+    lo = min(c[a] for c in coords)
+    first = sorted([i for i in range(n_chip) if coords[i][a] == lo], key=lambda i: coords[i][b])
+    second = sorted([i for i in range(n_chip) if coords[i][a] != lo], key=lambda i: -coords[i][b])
+    return first + second
+
+
+def ring_reduce_scatter(x, ring, axis):
+    n = len(ring)
+    blk = x.shape[0] // n
+    ring_arr = jnp.asarray(ring, jnp.int32)
+    pos_arr = jnp.asarray(np.argsort(ring), jnp.int32)
+    p = pos_arr[lax.axis_index(axis)]
+    cols = x.shape[1] // 2
+    right = [(ring[i], ring[(i + 1) % n]) for i in range(n)]
+    left = [(ring[i], ring[(i - 1) % n]) for i in range(n)]
+
+    def block(part, pos):
+        return lax.dynamic_slice_in_dim(part, ring_arr[pos % n] * blk, blk, axis=0)
+
+    xa, xb = x[:, :cols], x[:, cols:]
+    buf_a = block(xa, p - 1 + n)
+    buf_b = block(xb, p + 1)
+    for s in range(1, n):
+        buf_a = lax.ppermute(buf_a, axis, right) + block(xa, p - 1 - s + 2 * n)
+        buf_b = lax.ppermute(buf_b, axis, left) + block(xb, p + 1 + s)
+    return jnp.concatenate([buf_a, buf_b], axis=1)
+
+
+def local(ring, acts, grads, basis_in, basis_out, corr):
     n_chip = lax.axis_size("rchip")
     n_row = n_chip * 2
     n_col = lax.axis_size("col")
@@ -46,7 +92,7 @@
     keep = lax.dynamic_slice_in_dim(g_part, core * pair, pair, axis=0)
     send = lax.dynamic_slice_in_dim(g_part, (1 - core) * pair, pair, axis=0)
     summed = keep + lax.ppermute(send, "core", swap_perm(2))
-    share = lax.psum_scatter(summed, "rchip", scatter_dimension=0, tiled=True)
+    share = ring_reduce_scatter(summed, ring, "rchip")
     grad_rot = lax.all_gather(share.astype(jnp.bfloat16), ("core", "rchip"), axis=0, tiled=True)
 
     seg = n_row * half // SEQS
@@ -61,8 +107,9 @@
     devices = np.asarray(mesh.devices)
     n_row, n_col = devices.shape
     inner = Mesh(devices.reshape(n_row // 2, 2, n_col), ("rchip", "core", "col"))
+    ring = chip_ring(devices)
     return jax.shard_map(
-        local,
+        functools.partial(local, ring),
         mesh=inner,
         in_specs=(
             P(ROW, "col"),

time: 547 us -> 480 us (0.88)
  waiting for transfers between devices: 356 us -> 204 us
  starting transfers between devices: 2.6 us -> 43.7 us
  between operations: 15.1 us -> 31.1 us
  other arithmetic: 45.9 us -> 60 us
  local copies, waits for them, and re-layouts: 12.7 us -> 24.4 us
    reduce_scatter x1 -> x0, waiting for transfers between devices: 237 us -> none  [local(): share = lax.psum_scatter(summed, 'rchip', scatter_dimension=0, tiled=True)]
    ppermute x0 -> x14, waiting for transfers between devices: none -> 141 us  [the longest x7 97.9 us: ring_reduce_scatter(): buf_a = lax.ppermute(buf_a, axis, right) + block(xa, p - 1 - s + 2 * n)]
    ppermute x0 -> x14, starting transfers between devices: none -> 41.6 us  [the longest x7 40.1 us: ring_reduce_scatter(): buf_a = lax.ppermute(buf_a, axis, right) + block(xa, p - 1 - s + 2 * n)]
    all_gather x2, waiting for transfers between devices: 37.9 us -> 0.02 us  [local(): lax.all_gather(acts[c * half:(c + 1) * half], ROW, axis=0, tiled=True)]
    add x0 -> x12, other arithmetic: none -> 13.2 us  [the longest x6 6.64 us: ring_reduce_scatter(): buf_b = lax.ppermute(buf_b, axis, left) + block(xb, p + 1 + s)]
    ppermute x1, waiting for transfers between devices: 13.5 us -> 2.35 us  [local(): summed = keep + lax.ppermute(send, 'core', swap_perm(2))]
    slice x0 -> x1, local copies, waits for them, and re-layouts: none -> 6.33 us  [ring_reduce_scatter(): xa, xb = (x[:, :cols], x[:, cols:])]
  transfers between devices with their start and end apart: 8 -> 21, of which waited for: 5 -> 17; matrix products, arithmetic and copies ran while one was open for 14% -> 26% of each run, Pallas kernels for 0% -> 0%
where the time goes in v2:
time: 480 us; the launch traced here: 479 us
  waiting for transfers between devices  204 us (42%)
  matrix products  116 us (24%)
  other arithmetic  60 us (12%)
  starting transfers between devices  43.7 us (9%)
  between operations  31.1 us (6%)
  local copies, waits for them, and re-layouts  24.4 us (5%)
    ppermute x7, waiting for transfers between devices, ring_reduce_scatter(): buf_a = lax.ppermute(buf_a, axis, right) + block(xa, p - 1 - s + 2 * n)  97.9 us
    dot_general x2, matrix products, local(): lax.dot_general(basis_in, gathered, (((1,), (1,)), ((), ())), preferred_e...  71 us
    ppermute x7, waiting for transfers between devices, ring_reduce_scatter(): buf_b = lax.ppermute(buf_b, axis, left) + block(xb, p + 1 + s)  43.6 us
    ppermute x7, starting transfers between devices, ring_reduce_scatter(): buf_a = lax.ppermute(buf_a, axis, right) + block(xa, p - 1 - s + 2 * n)  40.1 us
    dot_general x1, matrix products, local(): jnp.einsum('kcsu,csum->skm', a, g, preferred_element_type=jnp.float32)  38.2 us
    ppermute x2, waiting for transfers between devices, local(): other = lax.ppermute(part.astype(jnp.bfloat16), 'col', swap_perm(2))  37.2 us
    add x1, other arithmetic, local(): return corr + jnp.sum(seq_grad * seq_grad, axis=0) * scale_factor  29.8 us
    all_gather x1, waiting for transfers between devices, local(): g_all = lax.all_gather(grads, 'col', axis=0, tiled=True)  22 us
  transfers between devices with their start and end apart: 21, of which 17 were waited for; matrix products, arithmetic and copies ran while one was open for 26% of the time, Pallas kernels for 0%

profile of v2, /device:TPU:0, one launch (start us, length us, event | category | flops | bytes accessed | tf_op | source)
XLA Modules:
  0.0 479.2 jit_solution(16825136567103338081)
XLA Ops:
  11.0 22.0 %all-gather.9.cloned.1.call-done = bf16[1024,512]{1,0:T(8,128)(2,1)} async-done(((bf16[512,512]{1,0:T(8,128)(2,1)}), bf16[1024,512]{1,0:T(8,128)(2,1)}) %all-gather.9.cloned.1.call-update) | async-done | bytes 1048592 | tf_op jit(solution)/shard_map/all_gather | solution.py:84
  34.2 6.4 %fusion.6 = f32[1024,4096]{1,0:T(8,128)S(1)} fusion(bf16[1024,512]{1,0:T(8,128)(2,1)S(1)} %bitcast.48, bf16[4096,512]{1,0:T(8,128)(2,1)} %param.10), kind=kOutput, calls=%fused_computation.30 | convolution fusion | flops 4294967296 | bytes 22020096 | tf_op jit(solution)/shard_map/dot_general | solution.py:87
  44.7 4.9 %copy-done = f32[1024,4096]{1,0:T(8,128)} copy-done((f32[1024,4096]{1,0:T(8,128)}, f32[1024,4096]{1,0:T(8,128)S(1)}, u32[]{:S(2)}) %copy-start) | copy-done | bytes 16777240
  63.1 11.2 %dynamic-slice_add_fusion = f32[512,4096]{1,0:T(8,128)} fusion(f32[512,4096]{1,0:T(8,128)} %collective-permute-done.2, f32[1024,4096]{1,0:T(8,128)} %copy-done, s32[]{:T(128)S(6)} %select_n.160), kind=kLoop, calls=%fused_computation.3 | loop fusion | flops 2097152 | bytes 25165828 | tf_op jit(solution)/shard_map/add | solution.py:94
  74.3 6.3 %fusion.1 = (f32[512,2048]{1,0:T(8,128)S(1)}, f32[512,2048]{1,0:T(8,128)}) fusion(f32[512,4096]{1,0:T(8,128)} %dynamic-slice_add_fusion), kind=kLoop, calls=%fused_computation.25 | loop fusion | bytes 16777216 | tf_op jit(solution)/shard_map/slice | solution.py:55
  88.2 20.6 %collective-permute-done.3 = f32[64,2048]{1,0:T(8,128)S(1)} collective-permute-done((f32[64,2048]{1,0:T(8,128)S(1)}, f32[64,2048]{1,0:T(8,128)S(1)}, u32[]{:S(2)}, u32[]{:S(2)}) %collective-permute-start.3) | collective-permute-done | bytes 524320 | tf_op jit(solution)/shard_map/ppermute | solution.py:59
  110.0 10.1 %collective-permute-start.4 = (f32[64,2048]{1,0:T(8,128)S(1)}, f32[64,2048]{1,0:T(8,128)S(1)}, u32[]{:S(2)}, u32[]{:S(2)}) collective-permute-start(f32[64,2048]{1,0:T(8,128)S(1)} %dynamic-slice_add_fusion.12), channel_id=1, source_target_pairs={{0,8},{8,16},{16,24},{24,28},{28,20},{20,12},{12,4},{4,0},{1,9},{9... | collective-permute-start | bytes 1572872 | tf_op jit(solution)/shard_map/ppermute | solution.py:59
  125.8 19.8 %collective-permute-done.4 = f32[64,2048]{1,0:T(8,128)S(1)} collective-permute-done((f32[64,2048]{1,0:T(8,128)S(1)}, f32[64,2048]{1,0:T(8,128)S(1)}, u32[]{:S(2)}, u32[]{:S(2)}) %collective-permute-start.4) | collective-permute-done | bytes 524320 | tf_op jit(solution)/shard_map/ppermute | solution.py:59
  146.7 10.8 %collective-permute-start.5 = (f32[64,2048]{1,0:T(8,128)S(1)}, f32[64,2048]{1,0:T(8,128)S(1)}, u32[]{:S(2)}, u32[]{:S(2)}) collective-permute-start(f32[64,2048]{1,0:T(8,128)S(1)} %dynamic-slice_add_fusion.11), channel_id=1, source_target_pairs={{0,8},{8,16},{16,24},{24,28},{28,20},{20,12},{12,4},{4,0},{1,9},{9... | collective-permute-start | bytes 1572872 | tf_op jit(solution)/shard_map/ppermute | solution.py:59
  164.5 12.4 %collective-permute-done.5 = f32[64,2048]{1,0:T(8,128)S(1)} collective-permute-done((f32[64,2048]{1,0:T(8,128)S(1)}, f32[64,2048]{1,0:T(8,128)S(1)}, u32[]{:S(2)}, u32[]{:S(2)}) %collective-permute-start.5) | collective-permute-done | bytes 524320 | tf_op jit(solution)/shard_map/ppermute | solution.py:59
  183.0 10.2 %collective-permute-done.6 = f32[64,2048]{1,0:T(8,128)S(1)} collective-permute-done((f32[64,2048]{1,0:T(8,128)S(1)}, f32[64,2048]{1,0:T(8,128)S(1)}, u32[]{:S(2)}, u32[]{:S(2)}) %collective-permute-start.6) | collective-permute-done | bytes 524320 | tf_op jit(solution)/shard_map/ppermute | solution.py:59
  196.9 7.4 %collective-permute-done.13 = f32[64,2048]{1,0:T(8,128)S(1)} collective-permute-done((f32[64,2048]{1,0:T(8,128)S(1)}, f32[64,2048]{1,0:T(8,128)S(1)}, u32[]{:S(2)}, u32[]{:S(2)}) %collective-permute-start.13) | collective-permute-done | bytes 524320 | tf_op jit(solution)/shard_map/ppermute | solution.py:60
  206.6 12.4 %collective-permute-done.7 = f32[64,2048]{1,0:T(8,128)S(1)} collective-permute-done((f32[64,2048]{1,0:T(8,128)S(1)}, f32[64,2048]{1,0:T(8,128)S(1)}, u32[]{:S(2)}, u32[]{:S(2)}) %collective-permute-start.7) | collective-permute-done | bytes 524320 | tf_op jit(solution)/shard_map/ppermute | solution.py:59
  220.1 10.4 %collective-permute-start.8 = (f32[64,2048]{1,0:T(8,128)S(1)}, f32[64,2048]{1,0:T(8,128)S(1)}, u32[]{:S(2)}, u32[]{:S(2)}) collective-permute-start(f32[64,2048]{1,0:T(8,128)S(1)} %dynamic-slice_add_fusion.8), channel_id=1, source_target_pairs={{0,8},{8,16},{16,24},{24,28},{28,20},{20,12},{12,4},{4,0},{1,9},{9... | collective-permute-start | bytes 1572872 | tf_op jit(solution)/shard_map/ppermute | solution.py:59
  230.6 5.1 %collective-permute-done.14 = f32[64,2048]{1,0:T(8,128)S(1)} collective-permute-done((f32[64,2048]{1,0:T(8,128)S(1)}, f32[64,2048]{1,0:T(8,128)S(1)}, u32[]{:S(2)}, u32[]{:S(2)}) %collective-permute-start.14) | collective-permute-done | bytes 524320 | tf_op jit(solution)/shard_map/ppermute | solution.py:60
  237.5 6.9 %collective-permute-done.8 = f32[64,2048]{1,0:T(8,128)S(1)} collective-permute-done((f32[64,2048]{1,0:T(8,128)S(1)}, f32[64,2048]{1,0:T(8,128)S(1)}, u32[]{:S(2)}, u32[]{:S(2)}) %collective-permute-start.8) | collective-permute-done | bytes 524320 | tf_op jit(solution)/shard_map/ppermute | solution.py:59
  248.1 5.2 %collective-permute-done.15 = f32[64,2048]{1,0:T(8,128)S(1)} collective-permute-done((f32[64,2048]{1,0:T(8,128)S(1)}, f32[64,2048]{1,0:T(8,128)S(1)}, u32[]{:S(2)}, u32[]{:S(2)}) %collective-permute-start.15) | collective-permute-done | bytes 524320 | tf_op jit(solution)/shard_map/ppermute | solution.py:60
  255.3 15.5 %collective-permute-done.9 = f32[64,2048]{1,0:T(8,128)S(1)} collective-permute-done((f32[64,2048]{1,0:T(8,128)S(1)}, f32[64,2048]{1,0:T(8,128)S(1)}, u32[]{:S(2)}, u32[]{:S(2)}) %collective-permute-start.9) | collective-permute-done | bytes 524320 | tf_op jit(solution)/shard_map/ppermute | solution.py:59
  271.9 17.8 %collective-permute-done.16 = f32[64,2048]{1,0:T(8,128)S(1)} collective-permute-done((f32[64,2048]{1,0:T(8,128)S(1)}, f32[64,2048]{1,0:T(8,128)S(1)}, u32[]{:S(2)}, u32[]{:S(2)}) %collective-permute-start.16) | collective-permute-done | bytes 524320 | tf_op jit(solution)/shard_map/ppermute | solution.py:60
  291.8 36.0 %fusion.4 = (bf16[1792,512]{0,1:T(8,128)(2,1)}, f32[1792,512]{0,1:T(8,128)}) fusion(bf16[1792,14336]{1,0:T(8,128)(2,1)} %param.9, bf16[512,14336]{1,0:T(8,128)(2,1)} %all-gather.7.cloned.1.call-done), kind=kOutput, calls=%fused_computation.28 | convolution fusion | flops 26307592192 | bytes 71565312 | tf_op jit(solution)/shard_map/dot_general | solution.py:75
  327.8 35.0 %fusion.5 = (bf16[1792,512]{0,1:T(8,128)(2,1)}, f32[1792,512]{0,1:T(8,128)S(1)}) fusion(bf16[1792,14336]{1,0:T(8,128)(2,1)} %param.9, bf16[512,14336]{1,0:T(8,128)(2,1)} %all-gather.5.cloned.1.call-done), kind=kOutput, calls=%fused_computation.29 | convolution fusion | flops 26307592192 | bytes 71565312 | tf_op jit(solution)/shard_map/dot_general | solution.py:75
  368.1 34.2 %collective-permute-done = bf16[1792,512]{0,1:T(8,128)(2,1)S(1)} collective-permute-done((bf16[1792,512]{0,1:T(8,128)(2,1)}, bf16[1792,512]{0,1:T(8,128)(2,1)S(1)}, u32[]{:S(2)}, u32[]{:S(2)}) %collective-permute-start) | collective-permute-done | bytes 1835040 | tf_op jit(solution)/shard_map/ppermute | solution.py:79
  404.7 38.2 %fusion = f32[1792,4096]{1,0:T(8,128)} fusion(bf16[1792,2,2,256]{0,3,2,1:T(8,128)(2,1)} %bitcast.46, bf16[2,2,256,4096]{3,2,1,0:T(8,128)(2,1)} %bitcast.49), kind=kOutput, calls=%fused_computation.1 | convolution fusion | flops 15054405632 | bytes 41418752 | tf_op jit(solution)/shard_map/kcsu,csum->skm/dot_general | solution.py:101
  442.9 29.8 %multiply_add_fusion = f32[1792,4096]{1,0:T(8,128)} fusion(f32[1792,4096]{1,0:T(8,128)} %param.11, f32[1792,4096]{1,0:T(8,128)} %fusion), kind=kLoop, calls=%fused_computation.2 | loop fusion | flops 14680064 | bytes 88080384 | tf_op jit(solution)/shard_map/add | solution.py:103
  (64 shorter events, 59.4 us)
Async XLA Ops:
  6.5 26.4 %all-gather.9.cloned.1.call-start = ((), (), s32[]{:S(2)}) async-start(), calls=%async_computation.2 | async-start | bytes 1572864 | tf_op jit(solution)/shard_map/all_gather | solution.py:84
  7.3 284.5 %all-gather.7.cloned.1.call-start = ((), (), s32[]{:S(2)}) async-start(), calls=%async_computation.1 | async-start | bytes 15597568 | tf_op jit(solution)/shard_map/all_gather | solution.py:74
  10.2 317.6 %all-gather.5.cloned.1.call-start = ((), (), s32[]{:S(2)}) async-start(), calls=%async_computation | async-start | bytes 15597568 | tf_op jit(solution)/shard_map/all_gather | solution.py:74
  10.9 393.8 %all-gather.11.cloned.1.call-start = ((), (), s32[]{:S(2)}) async-start(), calls=%async_computation.3 | async-start | bytes 8912896 | tf_op jit(solution)/shard_map/all_gather | solution.py:96
  40.6 9.1 %copy-start = (f32[1024,4096]{1,0:T(8,128)}, f32[1024,4096]{1,0:T(8,128)S(1)}, u32[]{:S(2)}) copy-start(f32[1024,4096]{1,0:T(8,128)S(1)} %fusion.6) | copy-start | bytes 50331652
  40.6 18.8 %copy-start.3 = (s32[8]{0:T(128)S(1)}, s32[8]{0:T(128)}, u32[]{:S(2)}) copy-start(s32[8]{0:T(128)} %constant.179.clone) | copy-start | bytes 100
  49.6 13.5 %collective-permute-start.2 = (f32[512,4096]{1,0:T(8,128)}, f32[512,4096]{1,0:T(8,128)}, u32[]{:S(2)}, u32[]{:S(2)}) collective-permute-start(f32[512,4096]{1,0:T(8,128)} %constant_dynamic-slice_fusion.2), channel_id=1, source_target_pairs={{0,2},{2,0},{1,3},{3,1},{4,6},{6,4},{5,7},{7,5},{8,10},{10,8},{9,1... | collective-permute-start | bytes 25165832 | tf_op jit(solution)/shard_map/ppermute | solution.py:94
  83.1 25.7 %collective-permute-start.3 = (f32[64,2048]{1,0:T(8,128)S(1)}, f32[64,2048]{1,0:T(8,128)S(1)}, u32[]{:S(2)}, u32[]{:S(2)}) collective-permute-start(f32[64,2048]{1,0:T(8,128)S(1)} %constant_dynamic-slice_fusion.1), channel_id=1, source_target_pairs={{0,8},{8,16},{16,24},{24,28},{28,20},{20,12},{12,4},{4,0},{1,9},{9... | collective-permute-start | bytes 1572872 | tf_op jit(solution)/shard_map/ppermute | solution.py:59
  86.0 37.4 %collective-permute-start.10 = (f32[64,2048]{1,0:T(8,128)S(1)}, f32[64,2048]{1,0:T(8,128)S(1)}, u32[]{:S(2)}, u32[]{:S(2)}) collective-permute-start(f32[64,2048]{1,0:T(8,128)S(1)} %constant_dynamic-slice_fusion), channel_id=1, source_target_pairs={{0,4},{8,0},{16,8},{24,16},{28,24},{20,28},{12,20},{4,12},{1,5},{9... | collective-permute-start | bytes 1572872 | tf_op jit(solution)/shard_map/ppermute | solution.py:60
  110.0 35.6 %collective-permute-start.4 = (f32[64,2048]{1,0:T(8,128)S(1)}, f32[64,2048]{1,0:T(8,128)S(1)}, u32[]{:S(2)}, u32[]{:S(2)}) collective-permute-start(f32[64,2048]{1,0:T(8,128)S(1)} %dynamic-slice_add_fusion.12), channel_id=1, source_target_pairs={{0,8},{8,16},{16,24},{24,28},{28,20},{20,12},{12,4},{4,0},{1,9},{9... | collective-permute-start | bytes 1572872 | tf_op jit(solution)/shard_map/ppermute | solution.py:59
  124.6 37.5 %collective-permute-start.11 = (f32[64,2048]{1,0:T(8,128)S(1)}, f32[64,2048]{1,0:T(8,128)S(1)}, u32[]{:S(2)}, u32[]{:S(2)}) collective-permute-start(f32[64,2048]{1,0:T(8,128)S(1)} %dynamic-slice_add_fusion.6), channel_id=1, source_target_pairs={{0,4},{8,0},{16,8},{24,16},{28,24},{20,28},{12,20},{4,12},{1,5},{9... | collective-permute-start | bytes 1572872 | tf_op jit(solution)/shard_map/ppermute | solution.py:60
  146.7 30.3 %collective-permute-start.5 = (f32[64,2048]{1,0:T(8,128)S(1)}, f32[64,2048]{1,0:T(8,128)S(1)}, u32[]{:S(2)}, u32[]{:S(2)}) collective-permute-start(f32[64,2048]{1,0:T(8,128)S(1)} %dynamic-slice_add_fusion.11), channel_id=1, source_target_pairs={{0,8},{8,16},{16,24},{24,28},{28,20},{20,12},{12,4},{4,0},{1,9},{9... | collective-permute-start | bytes 1572872 | tf_op jit(solution)/shard_map/ppermute | solution.py:59
  163.2 17.4 %collective-permute-start.12 = (f32[64,2048]{1,0:T(8,128)S(1)}, f32[64,2048]{1,0:T(8,128)S(1)}, u32[]{:S(2)}, u32[]{:S(2)}) collective-permute-start(f32[64,2048]{1,0:T(8,128)S(1)} %dynamic-slice_add_fusion.5), channel_id=1, source_target_pairs={{0,4},{8,0},{16,8},{24,16},{28,24},{20,28},{12,20},{4,12},{1,5},{9... | collective-permute-start | bytes 1572872 | tf_op jit(solution)/shard_map/ppermute | solution.py:60
  178.1 15.2 %collective-permute-start.6 = (f32[64,2048]{1,0:T(8,128)S(1)}, f32[64,2048]{1,0:T(8,128)S(1)}, u32[]{:S(2)}, u32[]{:S(2)}) collective-permute-start(f32[64,2048]{1,0:T(8,128)S(1)} %dynamic-slice_add_fusion.10), channel_id=1, source_target_pairs={{0,8},{8,16},{16,24},{24,28},{28,20},{20,12},{12,4},{4,0},{1,9},{9... | collective-permute-start | bytes 1572872 | tf_op jit(solution)/shard_map/ppermute | solution.py:59
  181.7 22.6 %collective-permute-start.13 = (f32[64,2048]{1,0:T(8,128)S(1)}, f32[64,2048]{1,0:T(8,128)S(1)}, u32[]{:S(2)}, u32[]{:S(2)}) collective-permute-start(f32[64,2048]{1,0:T(8,128)S(1)} %dynamic-slice_add_fusion.4), channel_id=1, source_target_pairs={{0,4},{8,0},{16,8},{24,16},{28,24},{20,28},{12,20},{4,12},{1,5},{9... | collective-permute-start | bytes 1572872 | tf_op jit(solution)/shard_map/ppermute | solution.py:60
  194.4 24.6 %collective-permute-start.7 = (f32[64,2048]{1,0:T(8,128)S(1)}, f32[64,2048]{1,0:T(8,128)S(1)}, u32[]{:S(2)}, u32[]{:S(2)}) collective-permute-start(f32[64,2048]{1,0:T(8,128)S(1)} %dynamic-slice_add_fusion.9), channel_id=1, source_target_pairs={{0,8},{8,16},{16,24},{24,28},{28,20},{20,12},{12,4},{4,0},{1,9},{9... | collective-permute-start | bytes 1572872 | tf_op jit(solution)/shard_map/ppermute | solution.py:59
  205.4 30.3 %collective-permute-start.14 = (f32[64,2048]{1,0:T(8,128)S(1)}, f32[64,2048]{1,0:T(8,128)S(1)}, u32[]{:S(2)}, u32[]{:S(2)}) collective-permute-start(f32[64,2048]{1,0:T(8,128)S(1)} %dynamic-slice_add_fusion.3), channel_id=1, source_target_pairs={{0,4},{8,0},{16,8},{24,16},{28,24},{20,28},{12,20},{4,12},{1,5},{9... | collective-permute-start | bytes 1572872 | tf_op jit(solution)/shard_map/ppermute | solution.py:60
  220.1 24.4 %collective-permute-start.8 = (f32[64,2048]{1,0:T(8,128)S(1)}, f32[64,2048]{1,0:T(8,128)S(1)}, u32[]{:S(2)}, u32[]{:S(2)}) collective-permute-start(f32[64,2048]{1,0:T(8,128)S(1)} %dynamic-slice_add_fusion.8), channel_id=1, source_target_pairs={{0,8},{8,16},{16,24},{24,28},{28,20},{20,12},{12,4},{4,0},{1,9},{9... | collective-permute-start | bytes 1572872 | tf_op jit(solution)/shard_map/ppermute | solution.py:59
  236.8 16.5 %collective-permute-start.15 = (f32[64,2048]{1,0:T(8,128)S(1)}, f32[64,2048]{1,0:T(8,128)S(1)}, u32[]{:S(2)}, u32[]{:S(2)}) collective-permute-start(f32[64,2048]{1,0:T(8,128)S(1)} %dynamic-slice_add_fusion.2), channel_id=1, source_target_pairs={{0,4},{8,0},{16,8},{24,16},{28,24},{20,28},{12,20},{4,12},{1,5},{9... | collective-permute-start | bytes 1572872 | tf_op jit(solution)/shard_map/ppermute | solution.py:60
  245.6 25.2 %collective-permute-start.9 = (f32[64,2048]{1,0:T(8,128)S(1)}, f32[64,2048]{1,0:T(8,128)S(1)}, u32[]{:S(2)}, u32[]{:S(2)}) collective-permute-start(f32[64,2048]{1,0:T(8,128)S(1)} %dynamic-slice_add_fusion.7), channel_id=1, source_target_pairs={{0,8},{8,16},{16,24},{24,28},{28,20},{20,12},{12,4},{4,0},{1,9},{9... | collective-permute-start | bytes 1572872 | tf_op jit(solution)/shard_map/ppermute | solution.py:59
  254.4 35.3 %collective-permute-start.16 = (f32[64,2048]{1,0:T(8,128)S(1)}, f32[64,2048]{1,0:T(8,128)S(1)}, u32[]{:S(2)}, u32[]{:S(2)}) collective-permute-start(f32[64,2048]{1,0:T(8,128)S(1)} %dynamic-slice_add_fusion.1), channel_id=1, source_target_pairs={{0,4},{8,0},{16,8},{24,16},{28,24},{20,28},{12,20},{4,12},{1,5},{9... | collective-permute-start | bytes 1572872 | tf_op jit(solution)/shard_map/ppermute | solution.py:60
  327.8 40.0 %collective-permute-start.1 = (bf16[1792,512]{0,1:T(8,128)(2,1)}, bf16[1792,512]{0,1:T(8,128)(2,1)S(1)}, u32[]{:S(2)}, u32[]{:S(2)}) collective-permute-start(bf16[1792,512]{0,1:T(8,128)(2,1)} %get-tuple-element.23), channel_id=1, source_target_pairs={{0,1},{1,0},{2,3},{3,2},{4,5},{5,4},{6,7},{7,6},{8,9},{9,8},{10,11... | collective-permute-start | bytes 5505032 | tf_op jit(solution)/shard_map/ppermute | solution.py:79
  327.8 40.0 %copy-start.2 = (f32[1792,512]{0,1:T(8,128)S(1)}, f32[1792,512]{0,1:T(8,128)}, u32[]{:S(2)}) copy-start(f32[1792,512]{0,1:T(8,128)} %get-tuple-element.24) | copy-start | bytes 11010052
  362.7 39.6 %collective-permute-start = (bf16[1792,512]{0,1:T(8,128)(2,1)}, bf16[1792,512]{0,1:T(8,128)(2,1)S(1)}, u32[]{:S(2)}, u32[]{:S(2)}) collective-permute-start(bf16[1792,512]{0,1:T(8,128)(2,1)} %get-tuple-element.25), channel_id=1, source_target_pairs={{0,1},{1,0},{2,3},{3,2},{4,5},{5,4},{6,7},{7,6},{8,9},{9,8},{10,11... | collective-permute-start | bytes 5505032 | tf_op jit(solution)/shard_map/ppermute | solution.py:79
  (2 other events, 11.5 us)
Sparse Core Ops, SparseCore 0:
  8.9 23.9 all-gather.8
  35.2 140.4 all-gather.6
  178.0 141.1 all-gather.4
  321.3 74.1 all-gather.10

commit v3 on v2

--- a/solution.py
+++ b/solution.py
@@ -4,6 +4,8 @@
 import jax.numpy as jnp
 import numpy as np
 from jax import lax
+from jax.experimental import pallas as pl
+from jax.experimental.pallas import tpu as pltpu
 from jax.sharding import Mesh
 from jax.sharding import PartitionSpec as P
 
@@ -61,6 +63,39 @@
     return jnp.concatenate([buf_a, buf_b], axis=1)
 
 
+def correction_kernel(seg, at_ref, g_ref, corr_ref, out_ref):
+    total = None
+    for s in range(SEQS):
+        cols = slice(s * seg, (s + 1) * seg)
+        sg = jnp.dot(at_ref[:, cols], g_ref[cols, :], preferred_element_type=jnp.float32)
+        total = sg * sg if total is None else total + sg * sg
+    out_ref[...] = corr_ref[...] + total * (1.0 / (SEQS * SEQ_LEN))
+
+
+def correction(at, g, corr, tm=256):
+    k, t = at.shape
+    m = g.shape[1]
+    tm = min(tm, m)
+    seg = t // SEQS
+    return pl.pallas_call(
+        functools.partial(correction_kernel, seg),
+        out_shape=jax.ShapeDtypeStruct((k, m), jnp.float32),
+        grid=(m // tm,),
+        in_specs=[
+            pl.BlockSpec((k, t), lambda j: (0, 0)),
+            pl.BlockSpec((t, tm), lambda j: (0, j)),
+            pl.BlockSpec((k, tm), lambda j: (0, j)),
+        ],
+        out_specs=pl.BlockSpec((k, tm), lambda j: (0, j)),
+        compiler_params=pltpu.CompilerParams(vmem_limit_bytes=48 * 1024 * 1024),
+        cost_estimate=pl.CostEstimate(
+            flops=2 * k * t * m + 3 * k * m,
+            transcendentals=0,
+            bytes_accessed=2 * k * t + 2 * t * m + 8 * k * m,
+        ),
+    )(at, g, corr)
+
+
 def local(ring, acts, grads, basis_in, basis_out, corr):
     n_chip = lax.axis_size("rchip")
     n_row = n_chip * 2
@@ -81,8 +116,14 @@
         else:
             act_t.append(lax.psum(part, "col").astype(jnp.bfloat16))
 
-    g_all = lax.all_gather(grads, "col", axis=0, tiled=True)
-    g_all = g_all.reshape(n_row, CHUNKS, half, g_all.shape[1]).transpose(1, 0, 2, 3)
+    if n_col == 2:
+        other = lax.ppermute(grads, "col", swap_perm(2))
+        first = lax.axis_index("col") == 0
+        g_all = jnp.concatenate([jnp.where(first, grads, other), jnp.where(first, other, grads)])
+    else:
+        g_all = lax.all_gather(grads, "col", axis=0, tiled=True)
+    per_seq = n_row // SEQS
+    g_all = g_all.reshape(SEQS, per_seq, CHUNKS, half, g_all.shape[1]).transpose(0, 2, 1, 3, 4)
     g_all = g_all.reshape(tokens, grads.shape[1])
     g_part = lax.dot_general(
         g_all, basis_out, (((1,), (1,)), ((), ())), preferred_element_type=jnp.float32
@@ -95,12 +136,11 @@
     share = ring_reduce_scatter(summed, ring, "rchip")
     grad_rot = lax.all_gather(share.astype(jnp.bfloat16), ("core", "rchip"), axis=0, tiled=True)
 
-    seg = n_row * half // SEQS
-    a = jnp.concatenate(act_t, axis=1).reshape(basis_in.shape[0], CHUNKS, SEQS, seg)
-    g = grad_rot.reshape(CHUNKS, SEQS, seg, grad_rot.shape[1])
-    seq_grad = jnp.einsum("kcsu,csum->skm", a, g, preferred_element_type=jnp.float32)
-    scale_factor = 1.0 / (SEQS * SEQ_LEN)
-    return corr + jnp.sum(seq_grad * seq_grad, axis=0) * scale_factor
+    seg = per_seq * half
+    at = jnp.concatenate(
+        [act_t[c][:, s * seg:(s + 1) * seg] for s in range(SEQS) for c in range(CHUNKS)], axis=1
+    )
+    return correction(at, grad_rot, corr)
 
 
 def solution(mesh):

time: 480 us -> 437 us (0.910)
  matrix products: 116 us -> 75.5 us
  Pallas kernels: 0 us -> 33.7 us
  other arithmetic: 60 us -> 33.4 us
  waiting for transfers between devices: 204 us -> 190 us
    dot_general x1 -> x0, matrix products: 38.2 us -> none  [local(): jnp.einsum('kcsu,csum->skm', a, g, preferred_element_type=jnp.float32)]
    pallas_call x0 -> x1, Pallas kernels: none -> 33.7 us  [correction(): pl.pallas_call(functools.partial(correction_kernel, seg), out_shape=jax.S...]
    add x1 -> x0, other arithmetic: 29.8 us -> none  [local(): return corr + jnp.sum(seq_grad * seq_grad, axis=0) * scale_factor]
    all_gather x1 -> x0, waiting for transfers between devices: 22 us -> none  [local(): g_all = lax.all_gather(grads, 'col', axis=0, tiled=True)]
    ppermute x0 -> x1, waiting for transfers between devices: none -> 11.9 us  [local(): other = lax.ppermute(grads, 'col', swap_perm(2))]
    ppermute x2, waiting for transfers between devices: 37.2 us -> 28.8 us  [local(): other = lax.ppermute(part.astype(jnp.bfloat16), 'col', swap_perm(2))]
    ppermute x7, starting transfers between devices: 40.1 us -> 32.3 us  [ring_reduce_scatter(): buf_a = lax.ppermute(buf_a, axis, right) + block(xa, p - 1 - s + 2 * n)]
    ppermute x7, starting transfers between devices: 1.51 us -> 7.98 us  [ring_reduce_scatter(): buf_b = lax.ppermute(buf_b, axis, left) + block(xb, p + 1 + s)]
  transfers between devices with their start and end apart: 21 -> 21, of which waited for: 17 -> 15; matrix products, arithmetic and copies ran while one was open for 26% -> 28% of each run, Pallas kernels for 0% -> 0%
where the time goes in v3:
time: 437 us; the launch traced here: 435 us
  waiting for transfers between devices  190 us (43%)
  matrix products  75.5 us (17%)
  starting transfers between devices  45.4 us (10%)
  Pallas kernels  33.7 us (8%)
  other arithmetic  33.4 us (8%)
  between operations  30.2 us (7%)
  local copies, waits for them, and re-layouts  26.7 us (6%)
    ppermute x7, waiting for transfers between devices, ring_reduce_scatter(): buf_a = lax.ppermute(buf_a, axis, right) + block(xa, p - 1 - s + 2 * n)  99 us
    dot_general x2, matrix products, local(): lax.dot_general(basis_in, gathered, (((1,), (1,)), ((), ())), preferred_e...  71 us
    ppermute x7, waiting for transfers between devices, ring_reduce_scatter(): buf_b = lax.ppermute(buf_b, axis, left) + block(xb, p + 1 + s)  46.7 us
    pallas_call x1, Pallas kernels, correction(): pl.pallas_call(functools.partial(correction_kernel, seg), out_shape=jax.S...  33.7 us
    ppermute x7, starting transfers between devices, ring_reduce_scatter(): buf_a = lax.ppermute(buf_a, axis, right) + block(xa, p - 1 - s + 2 * n)  32.3 us
    ppermute x2, waiting for transfers between devices, local(): other = lax.ppermute(part.astype(jnp.bfloat16), 'col', swap_perm(2))  28.8 us
    add x1, other arithmetic, local(): summed = keep + lax.ppermute(send, 'core', swap_perm(2))  11.9 us
    ppermute x1, waiting for transfers between devices, local(): other = lax.ppermute(grads, 'col', swap_perm(2))  11.9 us
  transfers between devices with their start and end apart: 21, of which 15 were waited for; matrix products, arithmetic and copies ran while one was open for 28% of the time, Pallas kernels for 0%

profile of v3, /device:TPU:0, one launch (start us, length us, event | category | flops | bytes accessed | tf_op | source)
XLA Modules:
  0.0 435.4 jit_solution(318173295929952624)
XLA Ops:
  13.3 11.9 %collective-permute-done.2 = bf16[512,512]{1,0:T(8,128)(2,1)S(1)} collective-permute-done((bf16[512,512]{1,0:T(8,128)(2,1)S(1)}, bf16[512,512]{1,0:T(8,128)(2,1)S(1)}, u32[]{:S(2)}, u32[]{:S(2)}) %collective-permute-start.2) | collective-permute-done | bytes 524320 | tf_op jit(solution)/shard_map/ppermute | solution.py:120
  27.5 4.6 %fusion.7 = f32[1024,4096]{1,0:T(8,128)S(1)} fusion(bf16[1024,512]{1,0:T(8,128)(2,1)S(1)} %bitcast.39, bf16[4096,512]{1,0:T(8,128)(2,1)S(1)} %copy-done.6), kind=kOutput, calls=%fused_computation.32 | convolution fusion | flops 4294967296 | bytes 22020096 | tf_op jit(solution)/shard_map/dot_general | solution.py:128
  36.2 4.5 %copy-done.1 = f32[1024,4096]{1,0:T(8,128)} copy-done((f32[1024,4096]{1,0:T(8,128)}, f32[1024,4096]{1,0:T(8,128)S(1)}, u32[]{:S(2)}) %copy-start.1) | copy-done | bytes 16777240
  54.2 11.9 %dynamic-slice_add_fusion = f32[512,4096]{1,0:T(8,128)} fusion(f32[512,4096]{1,0:T(8,128)} %collective-permute-done.3, f32[1024,4096]{1,0:T(8,128)} %copy-done.1, s32[]{:T(128)S(6)} %select_n.175), kind=kLoop, calls=%fused_computation | loop fusion | flops 2097152 | bytes 25165828 | tf_op jit(solution)/shard_map/add | solution.py:135
  66.2 6.4 %fusion = (f32[512,2048]{1,0:T(8,128)S(1)}, f32[512,2048]{1,0:T(8,128)}) fusion(f32[512,4096]{1,0:T(8,128)} %dynamic-slice_add_fusion), kind=kLoop, calls=%fused_computation.25 | loop fusion | bytes 16777216 | tf_op jit(solution)/shard_map/slice | solution.py:57
  79.7 20.7 %collective-permute-done.4 = f32[64,2048]{1,0:T(8,128)S(1)} collective-permute-done((f32[64,2048]{1,0:T(8,128)S(1)}, f32[64,2048]{1,0:T(8,128)S(1)}, u32[]{:S(2)}, u32[]{:S(2)}) %collective-permute-start.4) | collective-permute-done | bytes 524320 | tf_op jit(solution)/shard_map/ppermute | solution.py:61
  101.5 10.9 %collective-permute-start.5 = (f32[64,2048]{1,0:T(8,128)S(1)}, f32[64,2048]{1,0:T(8,128)S(1)}, u32[]{:S(2)}, u32[]{:S(2)}) collective-permute-start(f32[64,2048]{1,0:T(8,128)S(1)} %dynamic-slice_add_fusion.12), channel_id=1, source_target_pairs={{0,8},{8,16},{16,24},{24,28},{28,20},{20,12},{12,4},{4,0},{1,9},{9... | collective-permute-start | bytes 1572872 | tf_op jit(solution)/shard_map/ppermute | solution.py:61
  112.4 5.1 %collective-permute-done.11 = f32[64,2048]{1,0:T(8,128)S(1)} collective-permute-done((f32[64,2048]{1,0:T(8,128)S(1)}, f32[64,2048]{1,0:T(8,128)S(1)}, u32[]{:S(2)}, u32[]{:S(2)}) %collective-permute-start.11) | collective-permute-done | bytes 524320 | tf_op jit(solution)/shard_map/ppermute | solution.py:62
  119.9 15.0 %collective-permute-done.5 = f32[64,2048]{1,0:T(8,128)S(1)} collective-permute-done((f32[64,2048]{1,0:T(8,128)S(1)}, f32[64,2048]{1,0:T(8,128)S(1)}, u32[]{:S(2)}, u32[]{:S(2)}) %collective-permute-start.5) | collective-permute-done | bytes 524320 | tf_op jit(solution)/shard_map/ppermute | solution.py:61
  136.0 5.1 %collective-permute-start.6 = (f32[64,2048]{1,0:T(8,128)S(1)}, f32[64,2048]{1,0:T(8,128)S(1)}, u32[]{:S(2)}, u32[]{:S(2)}) collective-permute-start(f32[64,2048]{1,0:T(8,128)S(1)} %dynamic-slice_add_fusion.11), channel_id=1, source_target_pairs={{0,8},{8,16},{16,24},{24,28},{28,20},{20,12},{12,4},{4,0},{1,9},{9... | collective-permute-start | bytes 1572872 | tf_op jit(solution)/shard_map/ppermute | solution.py:61
  147.6 9.5 %collective-permute-done.6 = f32[64,2048]{1,0:T(8,128)S(1)} collective-permute-done((f32[64,2048]{1,0:T(8,128)S(1)}, f32[64,2048]{1,0:T(8,128)S(1)}, u32[]{:S(2)}, u32[]{:S(2)}) %collective-permute-start.6) | collective-permute-done | bytes 524320 | tf_op jit(solution)/shard_map/ppermute | solution.py:61
  162.8 18.5 %collective-permute-done.7 = f32[64,2048]{1,0:T(8,128)S(1)} collective-permute-done((f32[64,2048]{1,0:T(8,128)S(1)}, f32[64,2048]{1,0:T(8,128)S(1)}, u32[]{:S(2)}, u32[]{:S(2)}) %collective-permute-start.7) | collective-permute-done | bytes 524320 | tf_op jit(solution)/shard_map/ppermute | solution.py:61
  182.4 7.3 %collective-permute-start.8 = (f32[64,2048]{1,0:T(8,128)S(1)}, f32[64,2048]{1,0:T(8,128)S(1)}, u32[]{:S(2)}, u32[]{:S(2)}) collective-permute-start(f32[64,2048]{1,0:T(8,128)S(1)} %dynamic-slice_add_fusion.9), channel_id=1, source_target_pairs={{0,8},{8,16},{16,24},{24,28},{28,20},{20,12},{12,4},{4,0},{1,9},{9... | collective-permute-start | bytes 1572872 | tf_op jit(solution)/shard_map/ppermute | solution.py:61
  189.8 6.7 %collective-permute-done.14 = f32[64,2048]{1,0:T(8,128)S(1)} collective-permute-done((f32[64,2048]{1,0:T(8,128)S(1)}, f32[64,2048]{1,0:T(8,128)S(1)}, u32[]{:S(2)}, u32[]{:S(2)}) %collective-permute-start.14) | collective-permute-done | bytes 524320 | tf_op jit(solution)/shard_map/ppermute | solution.py:62
  201.3 10.2 %collective-permute-done.8 = f32[64,2048]{1,0:T(8,128)S(1)} collective-permute-done((f32[64,2048]{1,0:T(8,128)S(1)}, f32[64,2048]{1,0:T(8,128)S(1)}, u32[]{:S(2)}, u32[]{:S(2)}) %collective-permute-start.8) | collective-permute-done | bytes 524320 | tf_op jit(solution)/shard_map/ppermute | solution.py:61
  217.0 15.4 %collective-permute-done.9 = f32[64,2048]{1,0:T(8,128)S(1)} collective-permute-done((f32[64,2048]{1,0:T(8,128)S(1)}, f32[64,2048]{1,0:T(8,128)S(1)}, u32[]{:S(2)}, u32[]{:S(2)}) %collective-permute-start.9) | collective-permute-done | bytes 524320 | tf_op jit(solution)/shard_map/ppermute | solution.py:61
  233.4 4.6 %collective-permute-start.10 = (f32[64,2048]{1,0:T(8,128)S(1)}, f32[64,2048]{1,0:T(8,128)S(1)}, u32[]{:S(2)}, u32[]{:S(2)}) collective-permute-start(f32[64,2048]{1,0:T(8,128)S(1)} %dynamic-slice_add_fusion.7), channel_id=1, source_target_pairs={{0,8},{8,16},{16,24},{24,28},{28,20},{20,12},{12,4},{4,0},{1,9},{9... | collective-permute-start | bytes 1572872 | tf_op jit(solution)/shard_map/ppermute | solution.py:61
  238.0 11.2 %collective-permute-done.16 = f32[64,2048]{1,0:T(8,128)S(1)} collective-permute-done((f32[64,2048]{1,0:T(8,128)S(1)}, f32[64,2048]{1,0:T(8,128)S(1)}, u32[]{:S(2)}, u32[]{:S(2)}) %collective-permute-start.16) | collective-permute-done | bytes 524320 | tf_op jit(solution)/shard_map/ppermute | solution.py:62
  251.2 9.7 %collective-permute-done.10 = f32[64,2048]{1,0:T(8,128)S(1)} collective-permute-done((f32[64,2048]{1,0:T(8,128)S(1)}, f32[64,2048]{1,0:T(8,128)S(1)}, u32[]{:S(2)}, u32[]{:S(2)}) %collective-permute-start.10) | collective-permute-done | bytes 524320 | tf_op jit(solution)/shard_map/ppermute | solution.py:61
  261.9 22.2 %collective-permute-done.17 = f32[64,2048]{1,0:T(8,128)S(1)} collective-permute-done((f32[64,2048]{1,0:T(8,128)S(1)}, f32[64,2048]{1,0:T(8,128)S(1)}, u32[]{:S(2)}, u32[]{:S(2)}) %collective-permute-start.17) | collective-permute-done | bytes 524320 | tf_op jit(solution)/shard_map/ppermute | solution.py:62
  286.2 36.1 %fusion.5 = (bf16[1792,512]{1,0:T(8,128)(2,1)}, f32[1792,512]{1,0:T(8,128)}) fusion(bf16[1792,14336]{1,0:T(8,128)(2,1)} %param.9, bf16[512,14336]{1,0:T(8,128)(2,1)} %all-gather.6.cloned.1.call-done), kind=kOutput, calls=%fused_computation.30 | convolution fusion | flops 26307592192 | bytes 71565312 | tf_op jit(solution)/shard_map/dot_general | solution.py:110
  323.5 34.9 %fusion.6 = (bf16[1792,512]{1,0:T(8,128)(2,1)}, f32[1792,512]{1,0:T(8,128)S(1)}) fusion(bf16[1792,14336]{1,0:T(8,128)(2,1)} %param.9, bf16[512,14336]{1,0:T(8,128)(2,1)} %all-gather.4.cloned.1.call-done), kind=kOutput, calls=%fused_computation.31 | convolution fusion | flops 26307592192 | bytes 71565312 | tf_op jit(solution)/shard_map/dot_general | solution.py:110
  361.5 28.8 %collective-permute-done = bf16[1792,512]{1,0:T(8,128)(2,1)S(1)} collective-permute-done((bf16[1792,512]{1,0:T(8,128)(2,1)}, bf16[1792,512]{1,0:T(8,128)(2,1)S(1)}, u32[]{:S(2)}, u32[]{:S(2)}) %collective-permute-start) | collective-permute-done | bytes 1835040 | tf_op jit(solution)/shard_map/ppermute | solution.py:114
  395.2 33.7 %shard_map.73 = f32[1792,4096]{1,0:T(8,128)} custom-call(bf16[1792,1024]{1,0:T(8,128)(2,1)S(1)} %copy-done, bf16[1024,4096]{1,0:T(8,128)(2,1)} %all-gather.8.cloned.1.call-done.g_ref, f32[1792,4096]{1,0:T(8,128)} %corr_ref.1), custom_call_target="tpu_custom_call" | custom-call | flops 15054405632 | bytes 70778880 | tf_op jit(solution)/shard_map/pallas_call | solution.py:80
  (72 shorter events, 60.2 us)
Async XLA Ops:
  6.5 279.7 %all-gather.6.cloned.1.call-start = ((), (), s32[]{:S(2)}) async-start(), calls=%async_computation.1 | async-start | bytes 15597568 | tf_op jit(solution)/shard_map/all_gather | solution.py:109
  9.4 314.1 %all-gather.4.cloned.1.call-start = ((), (), s32[]{:S(2)}) async-start(), calls=%async_computation | async-start | bytes 15597568 | tf_op jit(solution)/shard_map/all_gather | solution.py:109
  10.2 382.9 %all-gather.8.cloned.1.call-start = ((), (), s32[]{:S(2)}) async-start(), calls=%async_computation.2 | async-start | bytes 8912896 | tf_op jit(solution)/shard_map/all_gather | solution.py:137
  10.3 15.0 %collective-permute-start.2 = (bf16[512,512]{1,0:T(8,128)(2,1)S(1)}, bf16[512,512]{1,0:T(8,128)(2,1)S(1)}, u32[]{:S(2)}, u32[]{:S(2)}) collective-permute-start(bf16[512,512]{1,0:T(8,128)(2,1)S(1)} %copy-done.4), channel_id=1, source_target_pairs={{0,1},{1,0},{2,3},{3,2},{4,5},{5,4},{6,7},{7,6},{8,9},{9,8},{10,11... | collective-permute-start | bytes 1572872 | tf_op jit(solution)/shard_map/ppermute | solution.py:120
  32.1 8.7 %copy-start.1 = (f32[1024,4096]{1,0:T(8,128)}, f32[1024,4096]{1,0:T(8,128)S(1)}, u32[]{:S(2)}) copy-start(f32[1024,4096]{1,0:T(8,128)S(1)} %fusion.7) | copy-start | bytes 50331652
  32.1 17.5 %copy-start.5 = (s32[8]{0:T(128)S(1)}, s32[8]{0:T(128)}, u32[]{:S(2)}) copy-start(s32[8]{0:T(128)} %constant.177.clone) | copy-start | bytes 100
  40.7 13.5 %collective-permute-start.3 = (f32[512,4096]{1,0:T(8,128)}, f32[512,4096]{1,0:T(8,128)}, u32[]{:S(2)}, u32[]{:S(2)}) collective-permute-start(f32[512,4096]{1,0:T(8,128)} %constant_dynamic-slice_fusion.2), channel_id=1, source_target_pairs={{0,2},{2,0},{1,3},{3,1},{4,6},{6,4},{5,7},{7,5},{8,10},{10,8},{9,1... | collective-permute-start | bytes 25165832 | tf_op jit(solution)/shard_map/ppermute | solution.py:135
  74.6 25.8 %collective-permute-start.4 = (f32[64,2048]{1,0:T(8,128)S(1)}, f32[64,2048]{1,0:T(8,128)S(1)}, u32[]{:S(2)}, u32[]{:S(2)}) collective-permute-start(f32[64,2048]{1,0:T(8,128)S(1)} %constant_dynamic-slice_fusion.1), channel_id=1, source_target_pairs={{0,8},{8,16},{16,24},{24,28},{28,20},{20,12},{12,4},{4,0},{1,9},{9... | collective-permute-start | bytes 1572872 | tf_op jit(solution)/shard_map/ppermute | solution.py:61
  78.2 39.3 %collective-permute-start.11 = (f32[64,2048]{1,0:T(8,128)S(1)}, f32[64,2048]{1,0:T(8,128)S(1)}, u32[]{:S(2)}, u32[]{:S(2)}) collective-permute-start(f32[64,2048]{1,0:T(8,128)S(1)} %constant_dynamic-slice_fusion), channel_id=1, source_target_pairs={{0,4},{8,0},{16,8},{24,16},{28,24},{20,28},{12,20},{4,12},{1,5},{9... | collective-permute-start | bytes 1572872 | tf_op jit(solution)/shard_map/ppermute | solution.py:62
  101.5 33.4 %collective-permute-start.5 = (f32[64,2048]{1,0:T(8,128)S(1)}, f32[64,2048]{1,0:T(8,128)S(1)}, u32[]{:S(2)}, u32[]{:S(2)}) collective-permute-start(f32[64,2048]{1,0:T(8,128)S(1)} %dynamic-slice_add_fusion.12), channel_id=1, source_target_pairs={{0,8},{8,16},{16,24},{24,28},{28,20},{20,12},{12,4},{4,0},{1,9},{9... | collective-permute-start | bytes 1572872 | tf_op jit(solution)/shard_map/ppermute | solution.py:61
  118.6 23.9 %collective-permute-start.12 = (f32[64,2048]{1,0:T(8,128)S(1)}, f32[64,2048]{1,0:T(8,128)S(1)}, u32[]{:S(2)}, u32[]{:S(2)}) collective-permute-start(f32[64,2048]{1,0:T(8,128)S(1)} %dynamic-slice_add_fusion.6), channel_id=1, source_target_pairs={{0,4},{8,0},{16,8},{24,16},{28,24},{20,28},{12,20},{4,12},{1,5},{9... | collective-permute-start | bytes 1572872 | tf_op jit(solution)/shard_map/ppermute | solution.py:62
  136.0 21.1 %collective-permute-start.6 = (f32[64,2048]{1,0:T(8,128)S(1)}, f32[64,2048]{1,0:T(8,128)S(1)}, u32[]{:S(2)}, u32[]{:S(2)}) collective-permute-start(f32[64,2048]{1,0:T(8,128)S(1)} %dynamic-slice_add_fusion.11), channel_id=1, source_target_pairs={{0,8},{8,16},{16,24},{24,28},{28,20},{20,12},{12,4},{4,0},{1,9},{9... | collective-permute-start | bytes 1572872 | tf_op jit(solution)/shard_map/ppermute | solution.py:61
  143.6 14.8 %collective-permute-start.13 = (f32[64,2048]{1,0:T(8,128)S(1)}, f32[64,2048]{1,0:T(8,128)S(1)}, u32[]{:S(2)}, u32[]{:S(2)}) collective-permute-start(f32[64,2048]{1,0:T(8,128)S(1)} %dynamic-slice_add_fusion.5), channel_id=1, source_target_pairs={{0,4},{8,0},{16,8},{24,16},{28,24},{20,28},{12,20},{4,12},{1,5},{9... | collective-permute-start | bytes 1572872 | tf_op jit(solution)/shard_map/ppermute | solution.py:62
  158.3 23.0 %collective-permute-start.7 = (f32[64,2048]{1,0:T(8,128)S(1)}, f32[64,2048]{1,0:T(8,128)S(1)}, u32[]{:S(2)}, u32[]{:S(2)}) collective-permute-start(f32[64,2048]{1,0:T(8,128)S(1)} %dynamic-slice_add_fusion.10), channel_id=1, source_target_pairs={{0,8},{8,16},{16,24},{24,28},{28,20},{20,12},{12,4},{4,0},{1,9},{9... | collective-permute-start | bytes 1572872 | tf_op jit(solution)/shard_map/ppermute | solution.py:61
  159.6 36.9 %collective-permute-start.14 = (f32[64,2048]{1,0:T(8,128)S(1)}, f32[64,2048]{1,0:T(8,128)S(1)}, u32[]{:S(2)}, u32[]{:S(2)}) collective-permute-start(f32[64,2048]{1,0:T(8,128)S(1)} %dynamic-slice_add_fusion.4), channel_id=1, source_target_pairs={{0,4},{8,0},{16,8},{24,16},{28,24},{20,28},{12,20},{4,12},{1,5},{9... | collective-permute-start | bytes 1572872 | tf_op jit(solution)/shard_map/ppermute | solution.py:62
  182.4 29.0 %collective-permute-start.8 = (f32[64,2048]{1,0:T(8,128)S(1)}, f32[64,2048]{1,0:T(8,128)S(1)}, u32[]{:S(2)}, u32[]{:S(2)}) collective-permute-start(f32[64,2048]{1,0:T(8,128)S(1)} %dynamic-slice_add_fusion.9), channel_id=1, source_target_pairs={{0,8},{8,16},{16,24},{24,28},{28,20},{20,12},{12,4},{4,0},{1,9},{9... | collective-permute-start | bytes 1572872 | tf_op jit(solution)/shard_map/ppermute | solution.py:61
  197.6 17.5 %collective-permute-start.15 = (f32[64,2048]{1,0:T(8,128)S(1)}, f32[64,2048]{1,0:T(8,128)S(1)}, u32[]{:S(2)}, u32[]{:S(2)}) collective-permute-start(f32[64,2048]{1,0:T(8,128)S(1)} %dynamic-slice_add_fusion.3), channel_id=1, source_target_pairs={{0,4},{8,0},{16,8},{24,16},{28,24},{20,28},{12,20},{4,12},{1,5},{9... | collective-permute-start | bytes 1572872 | tf_op jit(solution)/shard_map/ppermute | solution.py:62
  212.6 19.7 %collective-permute-start.9 = (f32[64,2048]{1,0:T(8,128)S(1)}, f32[64,2048]{1,0:T(8,128)S(1)}, u32[]{:S(2)}, u32[]{:S(2)}) collective-permute-start(f32[64,2048]{1,0:T(8,128)S(1)} %dynamic-slice_add_fusion.8), channel_id=1, source_target_pairs={{0,8},{8,16},{16,24},{24,28},{28,20},{20,12},{12,4},{4,0},{1,9},{9... | collective-permute-start | bytes 1572872 | tf_op jit(solution)/shard_map/ppermute | solution.py:61
  216.2 33.0 %collective-permute-start.16 = (f32[64,2048]{1,0:T(8,128)S(1)}, f32[64,2048]{1,0:T(8,128)S(1)}, u32[]{:S(2)}, u32[]{:S(2)}) collective-permute-start(f32[64,2048]{1,0:T(8,128)S(1)} %dynamic-slice_add_fusion.2), channel_id=1, source_target_pairs={{0,4},{8,0},{16,8},{24,16},{28,24},{20,28},{12,20},{4,12},{1,5},{9... | collective-permute-start | bytes 1572872 | tf_op jit(solution)/shard_map/ppermute | solution.py:62
  233.4 27.4 %collective-permute-start.10 = (f32[64,2048]{1,0:T(8,128)S(1)}, f32[64,2048]{1,0:T(8,128)S(1)}, u32[]{:S(2)}, u32[]{:S(2)}) collective-permute-start(f32[64,2048]{1,0:T(8,128)S(1)} %dynamic-slice_add_fusion.7), channel_id=1, source_target_pairs={{0,8},{8,16},{16,24},{24,28},{28,20},{20,12},{12,4},{4,0},{1,9},{9... | collective-permute-start | bytes 1572872 | tf_op jit(solution)/shard_map/ppermute | solution.py:61
  250.4 33.8 %collective-permute-start.17 = (f32[64,2048]{1,0:T(8,128)S(1)}, f32[64,2048]{1,0:T(8,128)S(1)}, u32[]{:S(2)}, u32[]{:S(2)}) collective-permute-start(f32[64,2048]{1,0:T(8,128)S(1)} %dynamic-slice_add_fusion.1), channel_id=1, source_target_pairs={{0,4},{8,0},{16,8},{24,16},{28,24},{20,28},{12,20},{4,12},{1,5},{9... | collective-permute-start | bytes 1572872 | tf_op jit(solution)/shard_map/ppermute | solution.py:62
  322.3 36.9 %collective-permute-start.1 = (bf16[1792,512]{1,0:T(8,128)(2,1)}, bf16[1792,512]{1,0:T(8,128)(2,1)}, u32[]{:S(2)}, u32[]{:S(2)}) collective-permute-start(bf16[1792,512]{1,0:T(8,128)(2,1)} %get-tuple-element.29), channel_id=1, source_target_pairs={{0,1},{1,0},{2,3},{3,2},{4,5},{5,4},{6,7},{7,6},{8,9},{9,8},{10,11... | collective-permute-start | bytes 5505032 | tf_op jit(solution)/shard_map/ppermute | solution.py:114
  323.5 35.7 %copy-start.3 = (f32[1792,512]{1,0:T(8,128)S(1)}, f32[1792,512]{1,0:T(8,128)}, u32[]{:S(2)}) copy-start(f32[1792,512]{1,0:T(8,128)} %get-tuple-element.30) | copy-start | bytes 11010052
  358.4 31.8 %collective-permute-start = (bf16[1792,512]{1,0:T(8,128)(2,1)}, bf16[1792,512]{1,0:T(8,128)(2,1)S(1)}, u32[]{:S(2)}, u32[]{:S(2)}) collective-permute-start(bf16[1792,512]{1,0:T(8,128)(2,1)} %get-tuple-element.31), channel_id=1, source_target_pairs={{0,1},{1,0},{2,3},{3,2},{4,5},{5,4},{6,7},{7,6},{8,9},{9,8},{10,11... | collective-permute-start | bytes 5505032 | tf_op jit(solution)/shard_map/ppermute | solution.py:114
  (5 other events, 18.6 us)
Sparse Core Ops, SparseCore 0:
  9.6 135.4 all-gather.5
  147.4 153.2 all-gather.3
  302.8 74.0 all-gather.7

commit v4 on v2

--- a/solution.py
+++ b/solution.py
@@ -4,6 +4,8 @@
 import jax.numpy as jnp
 import numpy as np
 from jax import lax
+from jax.experimental import pallas as pl
+from jax.experimental.pallas import tpu as pltpu
 from jax.sharding import Mesh
 from jax.sharding import PartitionSpec as P
 
@@ -61,46 +63,99 @@
     return jnp.concatenate([buf_a, buf_b], axis=1)
 
 
+def correction_kernel(a0_ref, a1_ref, g0_ref, g1_ref, corr_ref, out_ref):
+    s0 = jnp.dot(a0_ref[...], g0_ref[...], preferred_element_type=jnp.float32)
+    s1 = jnp.dot(a1_ref[...], g1_ref[...], preferred_element_type=jnp.float32)
+    out_ref[...] = corr_ref[...] + (s0 * s0 + s1 * s1) * (1.0 / (SEQS * SEQ_LEN))
+
+
+def correction(a0, a1, g0, g1, corr, tm=256):
+    k, t = a0.shape
+    m = g0.shape[1]
+    tm = min(tm, m)
+    a_spec = pl.BlockSpec((k, t), lambda j: (0, 0))
+    g_spec = pl.BlockSpec((t, tm), lambda j: (0, j))
+    c_spec = pl.BlockSpec((k, tm), lambda j: (0, j))
+    return pl.pallas_call(
+        correction_kernel,
+        out_shape=jax.ShapeDtypeStruct((k, m), jnp.float32),
+        grid=(m // tm,),
+        in_specs=[a_spec, a_spec, g_spec, g_spec, c_spec],
+        out_specs=c_spec,
+        compiler_params=pltpu.CompilerParams(vmem_limit_bytes=48 * 1024 * 1024),
+        cost_estimate=pl.CostEstimate(
+            flops=4 * k * t * m + 4 * k * m,
+            transcendentals=0,
+            bytes_accessed=4 * k * t + 4 * t * m + 8 * k * m,
+        ),
+    )(a0, a1, g0, g1, corr)
+
+
+def in_core_order(core, own, other, axis):
+    first = core == 0
+    return jnp.where(
+        first,
+        jnp.concatenate([own, other], axis=axis),
+        jnp.concatenate([other, own], axis=axis),
+    )
+
+
 def local(ring, acts, grads, basis_in, basis_out, corr):
+    assert SEQS == 2
     n_chip = lax.axis_size("rchip")
     n_row = n_chip * 2
     n_col = lax.axis_size("col")
     tok_dev = acts.shape[0]
     half = tok_dev // CHUNKS
     tokens = tok_dev * n_row
+    k_rows = basis_in.shape[0]
+    core = lax.axis_index("core")
+    chip_seq = n_chip // SEQS
+    seg = chip_seq * half
 
     act_t = []
     for c in range(CHUNKS):
-        gathered = lax.all_gather(acts[c * half:(c + 1) * half], ROW, axis=0, tiled=True)
-        part = lax.dot_general(
-            basis_in, gathered, (((1,), (1,)), ((), ())), preferred_element_type=jnp.float32
-        )
+        own = lax.all_gather(acts[c * half:(c + 1) * half], "rchip", axis=0, tiled=True)
+        other = lax.ppermute(own, "core", swap_perm(2))
+        dims = (((1,), (1,)), ((), ()))
+        p_own = lax.dot_general(basis_in, own, dims, preferred_element_type=jnp.float32)
+        p_other = lax.dot_general(basis_in, other, dims, preferred_element_type=jnp.float32)
+        part = in_core_order(core, p_own, p_other, 1)
         if n_col == 2:
-            other = lax.ppermute(part.astype(jnp.bfloat16), "col", swap_perm(2))
-            act_t.append((part + other.astype(jnp.float32)).astype(jnp.bfloat16))
+            swapped = lax.ppermute(part.astype(jnp.bfloat16), "col", swap_perm(2))
+            act_t.append((part + swapped.astype(jnp.float32)).astype(jnp.bfloat16))
         else:
             act_t.append(lax.psum(part, "col").astype(jnp.bfloat16))
+    a_seq = [
+        jnp.concatenate(
+            [x.reshape(k_rows, 2, SEQS, seg)[:, :, s, :].reshape(k_rows, 2 * seg) for x in act_t],
+            axis=1,
+        )
+        for s in range(SEQS)
+    ]
 
-    g_all = lax.all_gather(grads, "col", axis=0, tiled=True)
-    g_all = g_all.reshape(n_row, CHUNKS, half, g_all.shape[1]).transpose(1, 0, 2, 3)
-    g_all = g_all.reshape(tokens, grads.shape[1])
+    if n_col == 2:
+        peer = lax.ppermute(grads, "col", swap_perm(2))
+        first = lax.axis_index("col") == 0
+        g_all = jnp.concatenate([jnp.where(first, grads, peer), jnp.where(first, peer, grads)])
+    else:
+        g_all = lax.all_gather(grads, "col", axis=0, tiled=True)
+    o_cols = grads.shape[1]
+    g_all = g_all.reshape(SEQS, chip_seq, 2, CHUNKS, half, o_cols).transpose(0, 3, 2, 1, 4, 5)
+    g_all = g_all.reshape(tokens, o_cols)
     g_part = lax.dot_general(
         g_all, basis_out, (((1,), (1,)), ((), ())), preferred_element_type=jnp.float32
     )
-    core = lax.axis_index("core")
     pair = tokens // 2
     keep = lax.dynamic_slice_in_dim(g_part, core * pair, pair, axis=0)
     send = lax.dynamic_slice_in_dim(g_part, (1 - core) * pair, pair, axis=0)
     summed = keep + lax.ppermute(send, "core", swap_perm(2))
     share = ring_reduce_scatter(summed, ring, "rchip")
-    grad_rot = lax.all_gather(share.astype(jnp.bfloat16), ("core", "rchip"), axis=0, tiled=True)
-
-    seg = n_row * half // SEQS
-    a = jnp.concatenate(act_t, axis=1).reshape(basis_in.shape[0], CHUNKS, SEQS, seg)
-    g = grad_rot.reshape(CHUNKS, SEQS, seg, grad_rot.shape[1])
-    seq_grad = jnp.einsum("kcsu,csum->skm", a, g, preferred_element_type=jnp.float32)
-    scale_factor = 1.0 / (SEQS * SEQ_LEN)
-    return corr + jnp.sum(seq_grad * seq_grad, axis=0) * scale_factor
+    g_own = lax.all_gather(share.astype(jnp.bfloat16), "rchip", axis=0, tiled=True)
+    g_other = lax.ppermute(g_own, "core", swap_perm(2))
+    a_own = jnp.where(core == 0, a_seq[0], a_seq[1])
+    a_other = jnp.where(core == 0, a_seq[1], a_seq[0])
+    return correction(a_own, a_other, g_own, g_other, corr)
 
 
 def solution(mesh):

time: 480 us -> 528 us (1.10); the launches traced: 479 us -> 519 us
  local copies, waits for them, and re-layouts: 24.4 us -> 61.9 us
  Pallas kernels: 0 us -> 33.8 us
  waiting for transfers between devices: 204 us -> 184 us
  starting transfers between devices: 43.7 us -> 58.6 us
  matrix products: 116 us -> 102 us
  other arithmetic: 60 us -> 47.6 us
    pallas_call x0 -> x1, Pallas kernels: none -> 33.8 us  [correction(): pl.pallas_call(correction_kernel, out_shape=jax.ShapeDtypeStruct((k, m),...]
    add x1 -> x0, other arithmetic: 29.8 us -> none  [local(): return corr + jnp.sum(seq_grad * seq_grad, axis=0) * scale_factor]
    all_gather x4 -> x3, waiting for transfers between devices: 22 us -> 3.18 us  [the longest x2 3.18 us: local(): lax.all_gather(acts[c * half:(c + 1) * half], 'rchip', axis=0, tiled=True)]
    convert_element_type x2 -> x4, other arithmetic: 0.72 us -> 19.2 us  [the longest x2 10.5 us: local(): act_t.append((part + swapped.astype(jnp.float32)).astype(jnp.bfloat16))]
    slice x0 -> x2, local copies, waits for them, and re-layouts: none -> 15.4 us  [local(): x.reshape(k_rows, 2, SEQS, seg)[:, :, s, :].reshape(k_rows, 2 * seg)]
    ppermute x7, waiting for transfers between devices: 43.6 us -> 29.2 us  [ring_reduce_scatter(): buf_b = lax.ppermute(buf_b, axis, left) + block(xb, p + 1 + s)]
    dot_general x3 -> x4, matrix products: 109 us -> 97.6 us  [the longest x2 49.7 us: local(): lax.dot_general(basis_in, other, dims, preferred_element_type=jnp.float32)]
    unnamed x10 -> x25, local copies, waits for them, and re-layouts: 7.36 us -> 18.7 us
  transfers between devices with their start and end apart: 21 -> 24, of which waited for: 17 -> 17; matrix products, arithmetic and copies ran while one was open for 26% -> 38% of each run, Pallas kernels for 0% -> 0%
where the time goes in v4:
time: 528 us; the launch traced here: 519 us
  waiting for transfers between devices  184 us (35%)
  matrix products  102 us (19%)
  local copies, waits for them, and re-layouts  61.9 us (12%)
  starting transfers between devices  58.6 us (11%)
  other arithmetic  47.6 us (9%)
  Pallas kernels  33.8 us (6%)
  between operations  30.9 us (6%)
    ppermute x7, waiting for transfers between devices, ring_reduce_scatter(): buf_a = lax.ppermute(buf_a, axis, right) + block(xa, p - 1 - s + 2 * n)  109 us
    dot_general x2, matrix products, local(): lax.dot_general(basis_in, other, dims, preferred_element_type=jnp.float32)  49.7 us
    dot_general x2, matrix products, local(): lax.dot_general(basis_in, own, dims, preferred_element_type=jnp.float32)  48 us
    ppermute x7, starting transfers between devices, ring_reduce_scatter(): buf_a = lax.ppermute(buf_a, axis, right) + block(xa, p - 1 - s + 2 * n)  43.9 us
    pallas_call x1, Pallas kernels, correction(): pl.pallas_call(correction_kernel, out_shape=jax.ShapeDtypeStruct((k, m),...  33.8 us
    ppermute x7, waiting for transfers between devices, ring_reduce_scatter(): buf_b = lax.ppermute(buf_b, axis, left) + block(xb, p + 1 + s)  29.2 us
    ppermute x2, waiting for transfers between devices, local(): swapped = lax.ppermute(part.astype(jnp.bfloat16), 'col', swap_perm(2))  27.2 us
    unnamed x25, local copies, waits for them, and re-layouts  18.7 us
  transfers between devices with their start and end apart: 24, of which 17 were waited for; matrix products, arithmetic and copies ran while one was open for 38% of the time, Pallas kernels for 0%

profile of v4, /device:TPU:0, one launch (start us, length us, event | category | flops | bytes accessed | tf_op | source)
XLA Modules:
  0.0 518.9 jit_solution(1195867511399130285)
XLA Ops:
  12.5 11.9 %collective-permute-done.4 = bf16[512,512]{1,0:T(8,128)(2,1)S(1)} collective-permute-done((bf16[512,512]{1,0:T(8,128)(2,1)S(1)}, bf16[512,512]{1,0:T(8,128)(2,1)S(1)}, u32[]{:S(2)}, u32[]{:S(2)}) %collective-permute-start.4) | collective-permute-done | bytes 524320 | tf_op jit(solution)/shard_map/ppermute | solution.py:138
  53.5 11.2 %dynamic-slice_add_fusion = f32[512,4096]{1,0:T(8,128)} fusion(f32[512,4096]{1,0:T(8,128)} %collective-permute-done.5, f32[1024,4096]{1,0:T(8,128)} %copy-done, s32[]{:T(128)S(6)} %select_n.202), kind=kLoop, calls=%fused_computation | loop fusion | flops 2097152 | bytes 25165828 | tf_op jit(solution)/shard_map/add | solution.py:152
  64.7 6.4 %fusion.2 = (f32[512,2048]{1,0:T(8,128)S(1)}, f32[512,2048]{1,0:T(8,128)}) fusion(f32[512,4096]{1,0:T(8,128)} %dynamic-slice_add_fusion), kind=kLoop, calls=%fused_computation.35 | loop fusion | bytes 16777216 | tf_op jit(solution)/shard_map/slice | solution.py:57
  78.3 20.6 %collective-permute-done.6 = f32[64,2048]{1,0:T(8,128)S(1)} collective-permute-done((f32[64,2048]{1,0:T(8,128)S(1)}, f32[64,2048]{1,0:T(8,128)S(1)}, u32[]{:S(2)}, u32[]{:S(2)}) %collective-permute-start.6) | collective-permute-done | bytes 524320 | tf_op jit(solution)/shard_map/ppermute | solution.py:61
  100.0 11.4 %collective-permute-start.7 = (f32[64,2048]{1,0:T(8,128)S(1)}, f32[64,2048]{1,0:T(8,128)S(1)}, u32[]{:S(2)}, u32[]{:S(2)}) collective-permute-start(f32[64,2048]{1,0:T(8,128)S(1)} %dynamic-slice_add_fusion.12), channel_id=1, source_target_pairs={{0,8},{8,16},{16,24},{24,28},{28,20},{20,12},{12,4},{4,0},{1,9},{9... | collective-permute-start | bytes 1572872 | tf_op jit(solution)/shard_map/ppermute | solution.py:61
  119.2 14.7 %collective-permute-done.7 = f32[64,2048]{1,0:T(8,128)S(1)} collective-permute-done((f32[64,2048]{1,0:T(8,128)S(1)}, f32[64,2048]{1,0:T(8,128)S(1)}, u32[]{:S(2)}, u32[]{:S(2)}) %collective-permute-start.7) | collective-permute-done | bytes 524320 | tf_op jit(solution)/shard_map/ppermute | solution.py:61
  135.0 8.0 %collective-permute-start.8 = (f32[64,2048]{1,0:T(8,128)S(1)}, f32[64,2048]{1,0:T(8,128)S(1)}, u32[]{:S(2)}, u32[]{:S(2)}) collective-permute-start(f32[64,2048]{1,0:T(8,128)S(1)} %dynamic-slice_add_fusion.11), channel_id=1, source_target_pairs={{0,8},{8,16},{16,24},{24,28},{28,20},{20,12},{12,4},{4,0},{1,9},{9... | collective-permute-start | bytes 1572872 | tf_op jit(solution)/shard_map/ppermute | solution.py:61
  147.6 9.6 %collective-permute-done.8 = f32[64,2048]{1,0:T(8,128)S(1)} collective-permute-done((f32[64,2048]{1,0:T(8,128)S(1)}, f32[64,2048]{1,0:T(8,128)S(1)}, u32[]{:S(2)}, u32[]{:S(2)}) %collective-permute-start.8) | collective-permute-done | bytes 524320 | tf_op jit(solution)/shard_map/ppermute | solution.py:61
  165.6 15.9 %collective-permute-done.9 = f32[64,2048]{1,0:T(8,128)S(1)} collective-permute-done((f32[64,2048]{1,0:T(8,128)S(1)}, f32[64,2048]{1,0:T(8,128)S(1)}, u32[]{:S(2)}, u32[]{:S(2)}) %collective-permute-start.9) | collective-permute-done | bytes 524320 | tf_op jit(solution)/shard_map/ppermute | solution.py:61
  182.6 11.4 %collective-permute-start.10 = (f32[64,2048]{1,0:T(8,128)S(1)}, f32[64,2048]{1,0:T(8,128)S(1)}, u32[]{:S(2)}, u32[]{:S(2)}) collective-permute-start(f32[64,2048]{1,0:T(8,128)S(1)} %dynamic-slice_add_fusion.9), channel_id=1, source_target_pairs={{0,8},{8,16},{16,24},{24,28},{28,20},{20,12},{12,4},{4,0},{1,9},{9... | collective-permute-start | bytes 1572872 | tf_op jit(solution)/shard_map/ppermute | solution.py:61
  200.7 8.4 %collective-permute-done.10 = f32[64,2048]{1,0:T(8,128)S(1)} collective-permute-done((f32[64,2048]{1,0:T(8,128)S(1)}, f32[64,2048]{1,0:T(8,128)S(1)}, u32[]{:S(2)}, u32[]{:S(2)}) %collective-permute-start.10) | collective-permute-done | bytes 524320 | tf_op jit(solution)/shard_map/ppermute | solution.py:61
  215.4 20.9 %collective-permute-done.11 = f32[64,2048]{1,0:T(8,128)S(1)} collective-permute-done((f32[64,2048]{1,0:T(8,128)S(1)}, f32[64,2048]{1,0:T(8,128)S(1)}, u32[]{:S(2)}, u32[]{:S(2)}) %collective-permute-start.11) | collective-permute-done | bytes 524320 | tf_op jit(solution)/shard_map/ppermute | solution.py:61
  237.4 9.9 %collective-permute-start.12 = (f32[64,2048]{1,0:T(8,128)S(1)}, f32[64,2048]{1,0:T(8,128)S(1)}, u32[]{:S(2)}, u32[]{:S(2)}) collective-permute-start(f32[64,2048]{1,0:T(8,128)S(1)} %dynamic-slice_add_fusion.7), channel_id=1, source_target_pairs={{0,8},{8,16},{16,24},{24,28},{28,20},{20,12},{12,4},{4,0},{1,9},{9... | collective-permute-start | bytes 1572872 | tf_op jit(solution)/shard_map/ppermute | solution.py:61
  253.8 18.9 %collective-permute-done.12 = f32[64,2048]{1,0:T(8,128)S(1)} collective-permute-done((f32[64,2048]{1,0:T(8,128)S(1)}, f32[64,2048]{1,0:T(8,128)S(1)}, u32[]{:S(2)}, u32[]{:S(2)}) %collective-permute-start.12) | collective-permute-done | bytes 524320 | tf_op jit(solution)/shard_map/ppermute | solution.py:61
  273.9 14.7 %collective-permute-done.19 = f32[64,2048]{1,0:T(8,128)S(1)} collective-permute-done((f32[64,2048]{1,0:T(8,128)S(1)}, f32[64,2048]{1,0:T(8,128)S(1)}, u32[]{:S(2)}, u32[]{:S(2)}) %collective-permute-start.19) | collective-permute-done | bytes 524320 | tf_op jit(solution)/shard_map/ppermute | solution.py:62
  293.8 24.4 %fusion.7 = f32[1792,256]{1,0:T(8,128)} fusion(bf16[1792,14336]{1,0:T(8,128)(2,1)} %param.9, bf16[256,14336]{1,0:T(8,128)(2,1)} %all-gather.4.cloned.1.call-done), kind=kOutput, calls=%fused_computation.40 | convolution fusion | flops 13153337344 | bytes 60555264 | tf_op jit(solution)/shard_map/dot_general | solution.py:121
  318.1 23.6 %fusion.9 = f32[1792,256]{1,0:T(8,128)S(1)} fusion(bf16[1792,14336]{1,0:T(8,128)(2,1)} %param.9, bf16[256,14336]{1,0:T(8,128)(2,1)} %all-gather.6.cloned.1.call-done), kind=kOutput, calls=%fused_computation.42 | convolution fusion | flops 13153337344 | bytes 60555264 | tf_op jit(solution)/shard_map/dot_general | solution.py:121
  341.8 25.3 %fusion.8 = f32[1792,256]{1,0:T(8,128)} fusion(bf16[1792,14336]{1,0:T(8,128)(2,1)} %param.9, bf16[256,14336]{1,0:T(8,128)(2,1)} %collective-permute-done), kind=kOutput, calls=%fused_computation.41 | convolution fusion | flops 13153337344 | bytes 60555264 | tf_op jit(solution)/shard_map/dot_general | solution.py:122
  373.4 24.4 %fusion.10 = f32[1792,256]{1,0:T(8,128)} fusion(bf16[1792,14336]{1,0:T(8,128)(2,1)} %param.9, bf16[256,14336]{1,0:T(8,128)(2,1)} %collective-permute-done.2), kind=kOutput, calls=%fused_computation.43 | convolution fusion | flops 13153337344 | bytes 60555264 | tf_op jit(solution)/shard_map/dot_general | solution.py:122
  402.1 13.0 %collective-permute-done.1 = bf16[1792,512]{1,0:T(8,128)(2,1)} collective-permute-done((bf16[1792,512]{1,0:T(8,128)(2,1)}, bf16[1792,512]{1,0:T(8,128)(2,1)}, u32[]{:S(2)}, u32[]{:S(2)}) %collective-permute-start.1) | collective-permute-done | bytes 1835040 | tf_op jit(solution)/shard_map/ppermute | solution.py:125
  425.4 7.2 %fusion.3 = (bf16[1792,2,1,128]{3,2,1,0:T(2,128)(2,1)}, bf16[1792,2,128]{2,1,0:T(2,128)(2,1)S(1)}) fusion(bf16[1792,2,2,128]{3,2,1,0:T(2,128)(2,1)S(1)} %reshape.70), kind=kLoop, calls=%fused_computation.36 | loop fusion | bytes 3670016 | tf_op jit(solution)/shard_map/slice | solution.py:131
  439.9 14.1 %collective-permute-done.3 = bf16[1792,512]{1,0:T(8,128)(2,1)} collective-permute-done((bf16[1792,512]{1,0:T(8,128)(2,1)}, bf16[1792,512]{1,0:T(8,128)(2,1)}, u32[]{:S(2)}, u32[]{:S(2)}) %collective-permute-start.3) | collective-permute-done | bytes 1835040 | tf_op jit(solution)/shard_map/ppermute | solution.py:125
  462.6 8.2 %fusion.4 = (bf16[1792,2,1,128]{3,2,1,0:T(2,128)(2,1)}, bf16[1792,2,128]{2,1,0:T(2,128)(2,1)}) fusion(bf16[1792,2,2,128]{3,2,1,0:T(2,128)(2,1)S(1)} %reshape.71), kind=kLoop, calls=%fused_computation.37 | loop fusion | bytes 3670016 | tf_op jit(solution)/shard_map/slice | solution.py:131
  478.2 33.8 %shard_map.73 = f32[1792,4096]{1,0:T(8,128)} custom-call(bf16[1792,512]{1,0:T(8,128)(2,1)S(1)} %get-tuple-element.8.a0_ref, bf16[1792,512]{1,0:T(8,128)(2,1)S(1)} %get-tuple-element.7.a1_ref, bf16[512,4096]{1,0:T(8,128)(2,1)} %all-gather.8.cloned.1.call-done.g0_ref, bf16[512,4096]{1,0:T(8,128)(2,1)} %collective-permute-done.20.g1_ref, f32[1792,4096]{1,0:T(8,128)} %corr_ref.1), custom_call_target="tpu_custom_call" | custom-call | flops 15061745664 | bytes 70778880 | tf_op jit(solution)/shard_map/pallas_call | solution.py:79
  (96 shorter events, 120.3 us)
Async XLA Ops:
  6.5 284.0 %all-gather.4.cloned.1.call-start = ((), (), s32[]{:S(2)}) async-start(), calls=%async_computation | async-start | bytes 8257536 | tf_op jit(solution)/shard_map/all_gather | solution.py:118
  9.4 284.3 %all-gather.6.cloned.1.call-start = ((), (), s32[]{:S(2)}) async-start(), calls=%async_computation.1 | async-start | bytes 8257536 | tf_op jit(solution)/shard_map/all_gather | solution.py:118
  9.5 15.0 %collective-permute-start.4 = (bf16[512,512]{1,0:T(8,128)(2,1)S(1)}, bf16[512,512]{1,0:T(8,128)(2,1)S(1)}, u32[]{:S(2)}, u32[]{:S(2)}) collective-permute-start(bf16[512,512]{1,0:T(8,128)(2,1)S(1)} %copy-done.7), channel_id=1, source_target_pairs={{0,1},{1,0},{2,3},{3,2},{4,5},{5,4},{6,7},{7,6},{8,9},{9,8},{10,11... | collective-permute-start | bytes 1572872 | tf_op jit(solution)/shard_map/ppermute | solution.py:138
  40.0 13.5 %collective-permute-start.5 = (f32[512,4096]{1,0:T(8,128)}, f32[512,4096]{1,0:T(8,128)}, u32[]{:S(2)}, u32[]{:S(2)}) collective-permute-start(f32[512,4096]{1,0:T(8,128)} %constant_dynamic-slice_fusion.2), channel_id=1, source_target_pairs={{0,2},{2,0},{1,3},{3,1},{4,6},{6,4},{5,7},{7,5},{8,10},{10,8},{9,1... | collective-permute-start | bytes 25165832 | tf_op jit(solution)/shard_map/ppermute | solution.py:152
  40.0 362.1 %all-gather.8.cloned.1.call-start = ((), (), s32[]{:S(2)}) async-start(), calls=%async_computation.2 | async-start | bytes 4718592 | tf_op jit(solution)/shard_map/all_gather | solution.py:154
  73.0 25.8 %collective-permute-start.6 = (f32[64,2048]{1,0:T(8,128)S(1)}, f32[64,2048]{1,0:T(8,128)S(1)}, u32[]{:S(2)}, u32[]{:S(2)}) collective-permute-start(f32[64,2048]{1,0:T(8,128)S(1)} %constant_dynamic-slice_fusion.1), channel_id=1, source_target_pairs={{0,8},{8,16},{16,24},{24,28},{28,20},{20,12},{12,4},{4,0},{1,9},{9... | collective-permute-start | bytes 1572872 | tf_op jit(solution)/shard_map/ppermute | solution.py:61
  76.6 40.2 %collective-permute-start.13 = (f32[64,2048]{1,0:T(8,128)S(1)}, f32[64,2048]{1,0:T(8,128)S(1)}, u32[]{:S(2)}, u32[]{:S(2)}) collective-permute-start(f32[64,2048]{1,0:T(8,128)S(1)} %constant_dynamic-slice_fusion), channel_id=1, source_target_pairs={{0,4},{8,0},{16,8},{24,16},{28,24},{20,28},{12,20},{4,12},{1,5},{9... | collective-permute-start | bytes 1572872 | tf_op jit(solution)/shard_map/ppermute | solution.py:62
  100.0 33.9 %collective-permute-start.7 = (f32[64,2048]{1,0:T(8,128)S(1)}, f32[64,2048]{1,0:T(8,128)S(1)}, u32[]{:S(2)}, u32[]{:S(2)}) collective-permute-start(f32[64,2048]{1,0:T(8,128)S(1)} %dynamic-slice_add_fusion.12), channel_id=1, source_target_pairs={{0,8},{8,16},{16,24},{24,28},{28,20},{20,12},{12,4},{4,0},{1,9},{9... | collective-permute-start | bytes 1572872 | tf_op jit(solution)/shard_map/ppermute | solution.py:61
  117.9 25.0 %collective-permute-start.14 = (f32[64,2048]{1,0:T(8,128)S(1)}, f32[64,2048]{1,0:T(8,128)S(1)}, u32[]{:S(2)}, u32[]{:S(2)}) collective-permute-start(f32[64,2048]{1,0:T(8,128)S(1)} %dynamic-slice_add_fusion.6), channel_id=1, source_target_pairs={{0,4},{8,0},{16,8},{24,16},{28,24},{20,28},{12,20},{4,12},{1,5},{9... | collective-permute-start | bytes 1572872 | tf_op jit(solution)/shard_map/ppermute | solution.py:62
  135.0 22.2 %collective-permute-start.8 = (f32[64,2048]{1,0:T(8,128)S(1)}, f32[64,2048]{1,0:T(8,128)S(1)}, u32[]{:S(2)}, u32[]{:S(2)}) collective-permute-start(f32[64,2048]{1,0:T(8,128)S(1)} %dynamic-slice_add_fusion.11), channel_id=1, source_target_pairs={{0,8},{8,16},{16,24},{24,28},{28,20},{20,12},{12,4},{4,0},{1,9},{9... | collective-permute-start | bytes 1572872 | tf_op jit(solution)/shard_map/ppermute | solution.py:61
  144.1 16.7 %collective-permute-start.15 = (f32[64,2048]{1,0:T(8,128)S(1)}, f32[64,2048]{1,0:T(8,128)S(1)}, u32[]{:S(2)}, u32[]{:S(2)}) collective-permute-start(f32[64,2048]{1,0:T(8,128)S(1)} %dynamic-slice_add_fusion.5), channel_id=1, source_target_pairs={{0,4},{8,0},{16,8},{24,16},{28,24},{20,28},{12,20},{4,12},{1,5},{9... | collective-permute-start | bytes 1572872 | tf_op jit(solution)/shard_map/ppermute | solution.py:62
  158.3 23.3 %collective-permute-start.9 = (f32[64,2048]{1,0:T(8,128)S(1)}, f32[64,2048]{1,0:T(8,128)S(1)}, u32[]{:S(2)}, u32[]{:S(2)}) collective-permute-start(f32[64,2048]{1,0:T(8,128)S(1)} %dynamic-slice_add_fusion.10), channel_id=1, source_target_pairs={{0,8},{8,16},{16,24},{24,28},{28,20},{20,12},{12,4},{4,0},{1,9},{9... | collective-permute-start | bytes 1572872 | tf_op jit(solution)/shard_map/ppermute | solution.py:61
  161.8 36.0 %collective-permute-start.16 = (f32[64,2048]{1,0:T(8,128)S(1)}, f32[64,2048]{1,0:T(8,128)S(1)}, u32[]{:S(2)}, u32[]{:S(2)}) collective-permute-start(f32[64,2048]{1,0:T(8,128)S(1)} %dynamic-slice_add_fusion.4), channel_id=1, source_target_pairs={{0,4},{8,0},{16,8},{24,16},{28,24},{20,28},{12,20},{4,12},{1,5},{9... | collective-permute-start | bytes 1572872 | tf_op jit(solution)/shard_map/ppermute | solution.py:62
  182.6 26.5 %collective-permute-start.10 = (f32[64,2048]{1,0:T(8,128)S(1)}, f32[64,2048]{1,0:T(8,128)S(1)}, u32[]{:S(2)}, u32[]{:S(2)}) collective-permute-start(f32[64,2048]{1,0:T(8,128)S(1)} %dynamic-slice_add_fusion.9), channel_id=1, source_target_pairs={{0,8},{8,16},{16,24},{24,28},{28,20},{20,12},{12,4},{4,0},{1,9},{9... | collective-permute-start | bytes 1572872 | tf_op jit(solution)/shard_map/ppermute | solution.py:61
  198.9 12.9 %collective-permute-start.17 = (f32[64,2048]{1,0:T(8,128)S(1)}, f32[64,2048]{1,0:T(8,128)S(1)}, u32[]{:S(2)}, u32[]{:S(2)}) collective-permute-start(f32[64,2048]{1,0:T(8,128)S(1)} %dynamic-slice_add_fusion.3), channel_id=1, source_target_pairs={{0,4},{8,0},{16,8},{24,16},{28,24},{20,28},{12,20},{4,12},{1,5},{9... | collective-permute-start | bytes 1572872 | tf_op jit(solution)/shard_map/ppermute | solution.py:62
  210.3 25.9 %collective-permute-start.11 = (f32[64,2048]{1,0:T(8,128)S(1)}, f32[64,2048]{1,0:T(8,128)S(1)}, u32[]{:S(2)}, u32[]{:S(2)}) collective-permute-start(f32[64,2048]{1,0:T(8,128)S(1)} %dynamic-slice_add_fusion.8), channel_id=1, source_target_pairs={{0,8},{8,16},{16,24},{24,28},{28,20},{20,12},{12,4},{4,0},{1,9},{9... | collective-permute-start | bytes 1572872 | tf_op jit(solution)/shard_map/ppermute | solution.py:61
  212.9 37.2 %collective-permute-start.18 = (f32[64,2048]{1,0:T(8,128)S(1)}, f32[64,2048]{1,0:T(8,128)S(1)}, u32[]{:S(2)}, u32[]{:S(2)}) collective-permute-start(f32[64,2048]{1,0:T(8,128)S(1)} %dynamic-slice_add_fusion.2), channel_id=1, source_target_pairs={{0,4},{8,0},{16,8},{24,16},{28,24},{20,28},{12,20},{4,12},{1,5},{9... | collective-permute-start | bytes 1572872 | tf_op jit(solution)/shard_map/ppermute | solution.py:62
  237.4 35.3 %collective-permute-start.12 = (f32[64,2048]{1,0:T(8,128)S(1)}, f32[64,2048]{1,0:T(8,128)S(1)}, u32[]{:S(2)}, u32[]{:S(2)}) collective-permute-start(f32[64,2048]{1,0:T(8,128)S(1)} %dynamic-slice_add_fusion.7), channel_id=1, source_target_pairs={{0,8},{8,16},{16,24},{24,28},{28,20},{20,12},{12,4},{4,0},{1,9},{9... | collective-permute-start | bytes 1572872 | tf_op jit(solution)/shard_map/ppermute | solution.py:61
  251.2 37.4 %collective-permute-start.19 = (f32[64,2048]{1,0:T(8,128)S(1)}, f32[64,2048]{1,0:T(8,128)S(1)}, u32[]{:S(2)}, u32[]{:S(2)}) collective-permute-start(f32[64,2048]{1,0:T(8,128)S(1)} %dynamic-slice_add_fusion.1), channel_id=1, source_target_pairs={{0,4},{8,0},{16,8},{24,16},{28,24},{20,28},{12,20},{4,12},{1,5},{9... | collective-permute-start | bytes 1572872 | tf_op jit(solution)/shard_map/ppermute | solution.py:62
  290.5 51.2 %collective-permute-start = (bf16[256,14336]{1,0:T(8,128)(2,1)}, bf16[256,14336]{1,0:T(8,128)(2,1)}, u32[]{:S(2)}, u32[]{:S(2)}) collective-permute-start(bf16[256,14336]{1,0:T(8,128)(2,1)} %all-gather.4.cloned.1.call-done), channel_id=1, source_target_pairs={{0,2},{2,0},{1,3},{3,1},{4,6},{6,4},{5,7},{7,5},{8,10},{10,8},{9,1... | collective-permute-start | bytes 22020104 | tf_op jit(solution)/shard_map/ppermute | solution.py:119
  293.8 79.7 %collective-permute-start.2 = (bf16[256,14336]{1,0:T(8,128)(2,1)}, bf16[256,14336]{1,0:T(8,128)(2,1)}, u32[]{:S(2)}, u32[]{:S(2)}) collective-permute-start(bf16[256,14336]{1,0:T(8,128)(2,1)} %all-gather.6.cloned.1.call-done), channel_id=1, source_target_pairs={{0,2},{2,0},{1,3},{3,1},{4,6},{6,4},{5,7},{7,5},{8,10},{10,8},{9,1... | collective-permute-start | bytes 22020104 | tf_op jit(solution)/shard_map/ppermute | solution.py:119
  372.0 43.2 %collective-permute-start.1 = (bf16[1792,512]{1,0:T(8,128)(2,1)}, bf16[1792,512]{1,0:T(8,128)(2,1)}, u32[]{:S(2)}, u32[]{:S(2)}) collective-permute-start(bf16[1792,512]{1,0:T(8,128)(2,1)} %fusion.1), channel_id=1, source_target_pairs={{0,1},{1,0},{2,3},{3,2},{4,5},{5,4},{6,7},{7,6},{8,9},{9,8},{10,11... | collective-permute-start | bytes 5505032 | tf_op jit(solution)/shard_map/ppermute | solution.py:125
  401.6 52.4 %collective-permute-start.3 = (bf16[1792,512]{1,0:T(8,128)(2,1)}, bf16[1792,512]{1,0:T(8,128)(2,1)}, u32[]{:S(2)}, u32[]{:S(2)}) collective-permute-start(bf16[1792,512]{1,0:T(8,128)(2,1)} %fusion), channel_id=1, source_target_pairs={{0,1},{1,0},{2,3},{3,2},{4,5},{5,4},{6,7},{7,6},{8,9},{9,8},{10,11... | collective-permute-start | bytes 5505032 | tf_op jit(solution)/shard_map/ppermute | solution.py:125
  402.1 76.0 %collective-permute-start.20 = (bf16[512,4096]{1,0:T(8,128)(2,1)}, bf16[512,4096]{1,0:T(8,128)(2,1)}, u32[]{:S(2)}, u32[]{:S(2)}) collective-permute-start(bf16[512,4096]{1,0:T(8,128)(2,1)} %all-gather.8.cloned.1.call-done.g0_ref), channel_id=1, source_target_pairs={{0,2},{2,0},{1,3},{3,1},{4,6},{6,4},{5,7},{7,5},{8,10},{10,8},{9,1... | collective-permute-start | bytes 12582920 | tf_op jit(solution)/shard_map/ppermute | solution.py:155
  (11 other events, 127.4 us)
Sparse Core Ops, SparseCore 0:
  9.5 134.2 all-gather.3
  146.1 147.6 all-gather.5
  295.9 73.3 all-gather.7

commit v5 on v3

--- a/solution.py
+++ b/solution.py
@@ -11,7 +11,7 @@
 
 SEQ_LEN = 512
 SEQS = 2
-CHUNKS = 2
+CHUNKS = 1
 ROW = ("rchip", "core")
 
 

time: 437 us -> 429 us (0.982)
  waiting for transfers between devices: 190 us -> 221 us
  starting transfers between devices: 45.4 us -> 20.7 us
  matrix products: 75.5 us -> 66.1 us
  local copies, waits for them, and re-layouts: 26.7 us -> 21.7 us
    ppermute x2 -> x1, waiting for transfers between devices: 28.8 us -> 77.3 us  [local(): other = lax.ppermute(part.astype(jnp.bfloat16), 'col', swap_perm(2))]
    ppermute x7, waiting for transfers between devices: 46.7 us -> 2.24 us  [ring_reduce_scatter(): buf_b = lax.ppermute(buf_b, axis, left) + block(xb, p + 1 + s)]
    ppermute x7, waiting for transfers between devices: 99 us -> 125 us  [ring_reduce_scatter(): buf_a = lax.ppermute(buf_a, axis, right) + block(xa, p - 1 - s + 2 * n)]
    ppermute x7, starting transfers between devices: 32.3 us -> 11.9 us  [ring_reduce_scatter(): buf_a = lax.ppermute(buf_a, axis, right) + block(xa, p - 1 - s + 2 * n)]
    dot_general x2 -> x1, matrix products: 71 us -> 59.7 us  [local(): lax.dot_general(basis_in, gathered, (((1,), (1,)), ((), ())), preferred_e...]
    unnamed x16 -> x10, local copies, waits for them, and re-layouts: 10.6 us -> 8.58 us
  transfers between devices with their start and end apart: 21 -> 19, of which waited for: 15 -> 16; matrix products, arithmetic and copies ran while one was open for 28% -> 26% of each run, Pallas kernels for 0% -> 0%
where the time goes in v5:
time: 429 us; the launch traced here: 427 us
  waiting for transfers between devices  221 us (52%)
  matrix products  66.1 us (15%)
  Pallas kernels  33.7 us (8%)
  between operations  32.4 us (8%)
  other arithmetic  32.1 us (7%)
  local copies, waits for them, and re-layouts  21.7 us (5%)
  starting transfers between devices  20.7 us (5%)
    ppermute x7, waiting for transfers between devices, ring_reduce_scatter(): buf_a = lax.ppermute(buf_a, axis, right) + block(xa, p - 1 - s + 2 * n)  125 us
    ppermute x1, waiting for transfers between devices, local(): other = lax.ppermute(part.astype(jnp.bfloat16), 'col', swap_perm(2))  77.3 us
    dot_general x1, matrix products, local(): lax.dot_general(basis_in, gathered, (((1,), (1,)), ((), ())), preferred_e...  59.7 us
    pallas_call x1, Pallas kernels, correction(): pl.pallas_call(functools.partial(correction_kernel, seg), out_shape=jax.S...  33.7 us
    ppermute x1, waiting for transfers between devices, local(): other = lax.ppermute(grads, 'col', swap_perm(2))  12.1 us
    ppermute x7, starting transfers between devices, ring_reduce_scatter(): buf_a = lax.ppermute(buf_a, axis, right) + block(xa, p - 1 - s + 2 * n)  11.9 us
    add x1, other arithmetic, local(): summed = keep + lax.ppermute(send, 'core', swap_perm(2))  11.4 us
    unnamed x10, local copies, waits for them, and re-layouts  8.58 us
  transfers between devices with their start and end apart: 19, of which 16 were waited for; matrix products, arithmetic and copies ran while one was open for 26% of the time, Pallas kernels for 0%

profile of v5, /device:TPU:0, one launch (start us, length us, event | category | flops | bytes accessed | tf_op | source)
XLA Modules:
  0.0 427.3 jit_solution(2850778142075296750)
XLA Ops:
  7.3 3.0 collective-permute-start.1
  10.3 12.1 %collective-permute-done.1 = bf16[512,512]{1,0:T(8,128)(2,1)S(1)} collective-permute-done((bf16[512,512]{1,0:T(8,128)(2,1)}, bf16[512,512]{1,0:T(8,128)(2,1)S(1)}, u32[]{:S(2)}, u32[]{:S(2)}) %collective-permute-start.1) | collective-permute-done | bytes 524320 | tf_op jit(solution)/shard_map/ppermute | solution.py:120
  23.6 6.4 %fusion = f32[1024,4096]{1,0:T(8,128)S(1)} fusion(bf16[4096,512]{1,0:T(8,128)(2,1)} %param.10, bf16[512,512]{1,0:T(8,128)(2,1)S(1)} %get-tuple-element.8, bf16[512,512]{1,0:T(8,128)(2,1)S(1)} %get-tuple-element.7), kind=kOutput, calls=%fused_computation.2 | convolution fusion | flops 4297064448 | bytes 22020096 | tf_op jit(solution)/shard_map/dot_general | solution.py:128
  30.0 4.1 constant_dynamic-slice_fusion.2
  34.1 4.6 %copy-done.1 = f32[1024,4096]{1,0:T(8,128)} copy-done((f32[1024,4096]{1,0:T(8,128)}, f32[1024,4096]{1,0:T(8,128)S(1)}, u32[]{:S(2)}) %copy-start.1) | copy-done | bytes 16777240
  50.6 3.6 collective-permute-done.2
  54.2 11.4 %dynamic-slice_add_fusion = f32[512,4096]{1,0:T(8,128)} fusion(f32[512,4096]{1,0:T(8,128)} %collective-permute-done.2, f32[1024,4096]{1,0:T(8,128)} %copy-done.1, s32[]{:T(128)S(6)} %select_n.175), kind=kLoop, calls=%fused_computation | loop fusion | flops 2097152 | bytes 25165828 | tf_op jit(solution)/shard_map/add | solution.py:135
  65.6 6.4 %fusion.5 = (f32[512,2048]{1,0:T(8,128)S(1)}, f32[512,2048]{1,0:T(8,128)}) fusion(f32[512,4096]{1,0:T(8,128)} %dynamic-slice_add_fusion), kind=kLoop, calls=%fused_computation.27 | loop fusion | bytes 16777216 | tf_op jit(solution)/shard_map/slice | solution.py:57
  72.0 2.0 copy-done.2
  79.3 20.6 %collective-permute-done.3 = f32[64,2048]{1,0:T(8,128)S(1)} collective-permute-done((f32[64,2048]{1,0:T(8,128)S(1)}, f32[64,2048]{1,0:T(8,128)S(1)}, u32[]{:S(2)}, u32[]{:S(2)}) %collective-permute-start.3) | collective-permute-done | bytes 524320 | tf_op jit(solution)/shard_map/ppermute | solution.py:61
  106.1 20.5 %collective-permute-done.4 = f32[64,2048]{1,0:T(8,128)S(1)} collective-permute-done((f32[64,2048]{1,0:T(8,128)S(1)}, f32[64,2048]{1,0:T(8,128)S(1)}, u32[]{:S(2)}, u32[]{:S(2)}) %collective-permute-start.4) | collective-permute-done | bytes 524320 | tf_op jit(solution)/shard_map/ppermute | solution.py:61
  132.8 20.3 %collective-permute-done.5 = f32[64,2048]{1,0:T(8,128)S(1)} collective-permute-done((f32[64,2048]{1,0:T(8,128)S(1)}, f32[64,2048]{1,0:T(8,128)S(1)}, u32[]{:S(2)}, u32[]{:S(2)}) %collective-permute-start.5) | collective-permute-done | bytes 524320 | tf_op jit(solution)/shard_map/ppermute | solution.py:61
  154.2 2.0 collective-permute-start.6
  159.3 20.2 %collective-permute-done.6 = f32[64,2048]{1,0:T(8,128)S(1)} collective-permute-done((f32[64,2048]{1,0:T(8,128)S(1)}, f32[64,2048]{1,0:T(8,128)S(1)}, u32[]{:S(2)}, u32[]{:S(2)}) %collective-permute-start.6) | collective-permute-done | bytes 524320 | tf_op jit(solution)/shard_map/ppermute | solution.py:61
  180.5 2.0 collective-permute-start.7
  185.6 20.0 %collective-permute-done.7 = f32[64,2048]{1,0:T(8,128)S(1)} collective-permute-done((f32[64,2048]{1,0:T(8,128)S(1)}, f32[64,2048]{1,0:T(8,128)S(1)}, u32[]{:S(2)}, u32[]{:S(2)}) %collective-permute-start.7) | collective-permute-done | bytes 524320 | tf_op jit(solution)/shard_map/ppermute | solution.py:61
  206.7 2.0 collective-permute-start.8
  211.0 14.2 %collective-permute-done.8 = f32[64,2048]{1,0:T(8,128)S(1)} collective-permute-done((f32[64,2048]{1,0:T(8,128)S(1)}, f32[64,2048]{1,0:T(8,128)S(1)}, u32[]{:S(2)}, u32[]{:S(2)}) %collective-permute-start.8) | collective-permute-done | bytes 524320 | tf_op jit(solution)/shard_map/ppermute | solution.py:61
  230.4 8.6 %collective-permute-done.9 = f32[64,2048]{1,0:T(8,128)S(1)} collective-permute-done((f32[64,2048]{1,0:T(8,128)S(1)}, f32[64,2048]{1,0:T(8,128)S(1)}, u32[]{:S(2)}, u32[]{:S(2)}) %collective-permute-start.9) | collective-permute-done | bytes 524320 | tf_op jit(solution)/shard_map/ppermute | solution.py:61
  242.5 59.7 %fusion.7 = (bf16[1792,1024]{1,0:T(8,128)(2,1)S(1)}, f32[1792,1024]{1,0:T(8,128)S(1)}) fusion(bf16[1792,14336]{1,0:T(8,128)(2,1)} %param.9, bf16[1024,14336]{1,0:T(8,128)(2,1)} %all-gather.3.cloned.1.call-done), kind=kOutput, calls=%fused_computation.29 | convolution fusion | flops 52615184384 | bytes 91750400 | tf_op jit(solution)/shard_map/dot_general | solution.py:110
  303.9 77.3 %collective-permute-done = bf16[1792,1024]{1,0:T(8,128)(2,1)S(1)} collective-permute-done((bf16[1792,1024]{1,0:T(8,128)(2,1)S(1)}, bf16[1792,1024]{1,0:T(8,128)(2,1)S(1)}, u32[]{:S(2)}, u32[]{:S(2)}) %collective-permute-start) | collective-permute-done | bytes 3670048 | tf_op jit(solution)/shard_map/ppermute | solution.py:114
  381.3 3.4 add_convert_fusion.at_ref
  384.7 2.0 copy-done
  386.7 33.7 %shard_map.73 = f32[1792,4096]{1,0:T(8,128)} custom-call(bf16[1792,1024]{1,0:T(8,128)(2,1)S(1)} %copy-done, bf16[1024,4096]{1,0:T(8,128)(2,1)} %all-gather.5.cloned.1.call-done.g_ref, f32[1792,4096]{1,0:T(8,128)} %corr_ref.1), custom_call_target="tpu_custom_call" | custom-call | flops 15054405632 | bytes 70778880 | tf_op jit(solution)/shard_map/pallas_call | solution.py:80
  (53 shorter events, 34.7 us)
Async XLA Ops:
  6.5 235.9 %all-gather.3.cloned.1.call-start = ((), (), s32[]{:S(2)}) async-start(), calls=%async_computation | async-start | bytes 31195136 | tf_op jit(solution)/shard_map/all_gather | solution.py:109
  7.3 377.4 %all-gather.5.cloned.1.call-start = ((), (), s32[]{:S(2)}) async-start(), calls=%async_computation.1 | async-start | bytes 8912896 | tf_op jit(solution)/shard_map/all_gather | solution.py:137
  7.3 15.2 %collective-permute-start.1 = (bf16[512,512]{1,0:T(8,128)(2,1)}, bf16[512,512]{1,0:T(8,128)(2,1)S(1)}, u32[]{:S(2)}, u32[]{:S(2)}) collective-permute-start(bf16[512,512]{1,0:T(8,128)(2,1)} %param.8), channel_id=1, source_target_pairs={{0,1},{1,0},{2,3},{3,2},{4,5},{5,4},{6,7},{7,6},{8,9},{9,8},{10,11... | collective-permute-start | bytes 1572872 | tf_op jit(solution)/shard_map/ppermute | solution.py:120
  30.0 8.7 %copy-start.1 = (f32[1024,4096]{1,0:T(8,128)}, f32[1024,4096]{1,0:T(8,128)S(1)}, u32[]{:S(2)}) copy-start(f32[1024,4096]{1,0:T(8,128)S(1)} %fusion) | copy-start | bytes 50331652
  30.0 8.7 %copy-start.4 = (s32[8]{0:T(128)S(1)}, s32[8]{0:T(128)}, u32[]{:S(2)}) copy-start(s32[8]{0:T(128)} %constant.178.clone) | copy-start | bytes 100
  30.0 19.3 %copy-start.3 = (s32[8]{0:T(128)S(1)}, s32[8]{0:T(128)}, u32[]{:S(2)}) copy-start(s32[8]{0:T(128)} %constant.177.clone) | copy-start | bytes 100
  38.7 15.5 %collective-permute-start.2 = (f32[512,4096]{1,0:T(8,128)}, f32[512,4096]{1,0:T(8,128)}, u32[]{:S(2)}, u32[]{:S(2)}) collective-permute-start(f32[512,4096]{1,0:T(8,128)} %constant_dynamic-slice_fusion.2), channel_id=1, source_target_pairs={{0,2},{2,0},{1,3},{3,1},{4,6},{6,4},{5,7},{7,5},{8,10},{10,8},{9,1... | collective-permute-start | bytes 25165832 | tf_op jit(solution)/shard_map/ppermute | solution.py:135
  72.0 2.0 copy-start.2
  74.0 25.8 %collective-permute-start.3 = (f32[64,2048]{1,0:T(8,128)S(1)}, f32[64,2048]{1,0:T(8,128)S(1)}, u32[]{:S(2)}, u32[]{:S(2)}) collective-permute-start(f32[64,2048]{1,0:T(8,128)S(1)} %constant_dynamic-slice_fusion.1), channel_id=1, source_target_pairs={{0,8},{8,16},{16,24},{24,28},{28,20},{20,12},{12,4},{4,0},{1,9},{9... | collective-permute-start | bytes 1572872 | tf_op jit(solution)/shard_map/ppermute | solution.py:61
  77.7 25.8 %collective-permute-start.10 = (f32[64,2048]{1,0:T(8,128)S(1)}, f32[64,2048]{1,0:T(8,128)S(1)}, u32[]{:S(2)}, u32[]{:S(2)}) collective-permute-start(f32[64,2048]{1,0:T(8,128)S(1)} %constant_dynamic-slice_fusion), channel_id=1, source_target_pairs={{0,4},{8,0},{16,8},{24,16},{28,24},{20,28},{12,20},{4,12},{1,5},{9... | collective-permute-start | bytes 1572872 | tf_op jit(solution)/shard_map/ppermute | solution.py:62
  101.0 25.6 %collective-permute-start.4 = (f32[64,2048]{1,0:T(8,128)S(1)}, f32[64,2048]{1,0:T(8,128)S(1)}, u32[]{:S(2)}, u32[]{:S(2)}) collective-permute-start(f32[64,2048]{1,0:T(8,128)S(1)} %dynamic-slice_add_fusion.12), channel_id=1, source_target_pairs={{0,8},{8,16},{16,24},{24,28},{28,20},{20,12},{12,4},{4,0},{1,9},{9... | collective-permute-start | bytes 1572872 | tf_op jit(solution)/shard_map/ppermute | solution.py:61
  104.5 25.6 %collective-permute-start.11 = (f32[64,2048]{1,0:T(8,128)S(1)}, f32[64,2048]{1,0:T(8,128)S(1)}, u32[]{:S(2)}, u32[]{:S(2)}) collective-permute-start(f32[64,2048]{1,0:T(8,128)S(1)} %dynamic-slice_add_fusion.6), channel_id=1, source_target_pairs={{0,4},{8,0},{16,8},{24,16},{28,24},{20,28},{12,20},{4,12},{1,5},{9... | collective-permute-start | bytes 1572872 | tf_op jit(solution)/shard_map/ppermute | solution.py:62
  127.7 25.4 %collective-permute-start.5 = (f32[64,2048]{1,0:T(8,128)S(1)}, f32[64,2048]{1,0:T(8,128)S(1)}, u32[]{:S(2)}, u32[]{:S(2)}) collective-permute-start(f32[64,2048]{1,0:T(8,128)S(1)} %dynamic-slice_add_fusion.11), channel_id=1, source_target_pairs={{0,8},{8,16},{16,24},{24,28},{28,20},{20,12},{12,4},{4,0},{1,9},{9... | collective-permute-start | bytes 1572872 | tf_op jit(solution)/shard_map/ppermute | solution.py:61
  131.2 25.4 %collective-permute-start.12 = (f32[64,2048]{1,0:T(8,128)S(1)}, f32[64,2048]{1,0:T(8,128)S(1)}, u32[]{:S(2)}, u32[]{:S(2)}) collective-permute-start(f32[64,2048]{1,0:T(8,128)S(1)} %dynamic-slice_add_fusion.5), channel_id=1, source_target_pairs={{0,4},{8,0},{16,8},{24,16},{28,24},{20,28},{12,20},{4,12},{1,5},{9... | collective-permute-start | bytes 1572872 | tf_op jit(solution)/shard_map/ppermute | solution.py:62
  154.2 25.2 %collective-permute-start.6 = (f32[64,2048]{1,0:T(8,128)S(1)}, f32[64,2048]{1,0:T(8,128)S(1)}, u32[]{:S(2)}, u32[]{:S(2)}) collective-permute-start(f32[64,2048]{1,0:T(8,128)S(1)} %dynamic-slice_add_fusion.10), channel_id=1, source_target_pairs={{0,8},{8,16},{16,24},{24,28},{28,20},{20,12},{12,4},{4,0},{1,9},{9... | collective-permute-start | bytes 1572872 | tf_op jit(solution)/shard_map/ppermute | solution.py:61
  157.7 25.1 %collective-permute-start.13 = (f32[64,2048]{1,0:T(8,128)S(1)}, f32[64,2048]{1,0:T(8,128)S(1)}, u32[]{:S(2)}, u32[]{:S(2)}) collective-permute-start(f32[64,2048]{1,0:T(8,128)S(1)} %dynamic-slice_add_fusion.4), channel_id=1, source_target_pairs={{0,4},{8,0},{16,8},{24,16},{28,24},{20,28},{12,20},{4,12},{1,5},{9... | collective-permute-start | bytes 1572872 | tf_op jit(solution)/shard_map/ppermute | solution.py:62
  180.5 25.1 %collective-permute-start.7 = (f32[64,2048]{1,0:T(8,128)S(1)}, f32[64,2048]{1,0:T(8,128)S(1)}, u32[]{:S(2)}, u32[]{:S(2)}) collective-permute-start(f32[64,2048]{1,0:T(8,128)S(1)} %dynamic-slice_add_fusion.9), channel_id=1, source_target_pairs={{0,8},{8,16},{16,24},{24,28},{28,20},{20,12},{12,4},{4,0},{1,9},{9... | collective-permute-start | bytes 1572872 | tf_op jit(solution)/shard_map/ppermute | solution.py:61
  183.9 24.9 %collective-permute-start.14 = (f32[64,2048]{1,0:T(8,128)S(1)}, f32[64,2048]{1,0:T(8,128)S(1)}, u32[]{:S(2)}, u32[]{:S(2)}) collective-permute-start(f32[64,2048]{1,0:T(8,128)S(1)} %dynamic-slice_add_fusion.3), channel_id=1, source_target_pairs={{0,4},{8,0},{16,8},{24,16},{28,24},{20,28},{12,20},{4,12},{1,5},{9... | collective-permute-start | bytes 1572872 | tf_op jit(solution)/shard_map/ppermute | solution.py:62
  206.7 18.6 %collective-permute-start.8 = (f32[64,2048]{1,0:T(8,128)S(1)}, f32[64,2048]{1,0:T(8,128)S(1)}, u32[]{:S(2)}, u32[]{:S(2)}) collective-permute-start(f32[64,2048]{1,0:T(8,128)S(1)} %dynamic-slice_add_fusion.8), channel_id=1, source_target_pairs={{0,8},{8,16},{16,24},{24,28},{28,20},{20,12},{12,4},{4,0},{1,9},{9... | collective-permute-start | bytes 1572872 | tf_op jit(solution)/shard_map/ppermute | solution.py:61
  209.9 16.8 %collective-permute-start.15 = (f32[64,2048]{1,0:T(8,128)S(1)}, f32[64,2048]{1,0:T(8,128)S(1)}, u32[]{:S(2)}, u32[]{:S(2)}) collective-permute-start(f32[64,2048]{1,0:T(8,128)S(1)} %dynamic-slice_add_fusion.2), channel_id=1, source_target_pairs={{0,4},{8,0},{16,8},{24,16},{28,24},{20,28},{12,20},{4,12},{1,5},{9... | collective-permute-start | bytes 1572872 | tf_op jit(solution)/shard_map/ppermute | solution.py:62
  226.3 12.8 %collective-permute-start.9 = (f32[64,2048]{1,0:T(8,128)S(1)}, f32[64,2048]{1,0:T(8,128)S(1)}, u32[]{:S(2)}, u32[]{:S(2)}) collective-permute-start(f32[64,2048]{1,0:T(8,128)S(1)} %dynamic-slice_add_fusion.7), channel_id=1, source_target_pairs={{0,8},{8,16},{16,24},{24,28},{28,20},{20,12},{12,4},{4,0},{1,9},{9... | collective-permute-start | bytes 1572872 | tf_op jit(solution)/shard_map/ppermute | solution.py:61
  227.8 12.6 %collective-permute-start.16 = (f32[64,2048]{1,0:T(8,128)S(1)}, f32[64,2048]{1,0:T(8,128)S(1)}, u32[]{:S(2)}, u32[]{:S(2)}) collective-permute-start(f32[64,2048]{1,0:T(8,128)S(1)} %dynamic-slice_add_fusion.1), channel_id=1, source_target_pairs={{0,4},{8,0},{16,8},{24,16},{28,24},{20,28},{12,20},{4,12},{1,5},{9... | collective-permute-start | bytes 1572872 | tf_op jit(solution)/shard_map/ppermute | solution.py:62
  302.2 79.1 %collective-permute-start = (bf16[1792,1024]{1,0:T(8,128)(2,1)S(1)}, bf16[1792,1024]{1,0:T(8,128)(2,1)S(1)}, u32[]{:S(2)}, u32[]{:S(2)}) collective-permute-start(bf16[1792,1024]{1,0:T(8,128)(2,1)S(1)} %get-tuple-element.23), channel_id=1, source_target_pairs={{0,1},{1,0},{2,3},{3,2},{4,5},{5,4},{6,7},{7,6},{8,9},{9,8},{10,11... | collective-permute-start | bytes 11010056 | tf_op jit(solution)/shard_map/ppermute | solution.py:114
  384.7 2.0 copy-start
Sparse Core Ops, SparseCore 0:
  8.9 213.3 all-gather.2
  242.6 75.4 all-gather.4

commit v6 on v5

--- a/solution.py
+++ b/solution.py
@@ -12,6 +12,7 @@
 SEQ_LEN = 512
 SEQS = 2
 CHUNKS = 1
+K_PIECES = 2
 ROW = ("rchip", "core")
 
 
@@ -63,7 +64,8 @@
     return jnp.concatenate([buf_a, buf_b], axis=1)
 
 
-def correction_kernel(seg, at_ref, g_ref, corr_ref, out_ref):
+def correction_kernel(seg, at_ref, g_ref, corr_ref, *rest):
+    out_ref = rest[-1]
     total = None
     for s in range(SEQS):
         cols = slice(s * seg, (s + 1) * seg)
@@ -72,28 +74,36 @@
     out_ref[...] = corr_ref[...] + total * (1.0 / (SEQS * SEQ_LEN))
 
 
-def correction(at, g, corr, tm=256):
-    k, t = at.shape
+def correction(at, g, corr, piece, prev=None, tm=256):
+    kp, t = at.shape
     m = g.shape[1]
     tm = min(tm, m)
     seg = t // SEQS
+    in_specs = [
+        pl.BlockSpec((kp, t), lambda j: (0, 0)),
+        pl.BlockSpec((t, tm), lambda j: (0, j)),
+        pl.BlockSpec((kp, tm), lambda j: (piece, j)),
+    ]
+    args = [at, g, corr]
+    aliases = {}
+    if prev is not None:
+        in_specs.append(pl.BlockSpec(memory_space=pl.ANY))
+        args.append(prev)
+        aliases = {3: 0}
     return pl.pallas_call(
         functools.partial(correction_kernel, seg),
-        out_shape=jax.ShapeDtypeStruct((k, m), jnp.float32),
+        out_shape=jax.ShapeDtypeStruct(corr.shape, jnp.float32),
         grid=(m // tm,),
-        in_specs=[
-            pl.BlockSpec((k, t), lambda j: (0, 0)),
-            pl.BlockSpec((t, tm), lambda j: (0, j)),
-            pl.BlockSpec((k, tm), lambda j: (0, j)),
-        ],
-        out_specs=pl.BlockSpec((k, tm), lambda j: (0, j)),
+        in_specs=in_specs,
+        out_specs=pl.BlockSpec((kp, tm), lambda j: (piece, j)),
+        input_output_aliases=aliases,
         compiler_params=pltpu.CompilerParams(vmem_limit_bytes=48 * 1024 * 1024),
         cost_estimate=pl.CostEstimate(
-            flops=2 * k * t * m + 3 * k * m,
+            flops=2 * kp * t * m + 3 * kp * m,
             transcendentals=0,
-            bytes_accessed=2 * k * t + 2 * t * m + 8 * k * m,
+            bytes_accessed=2 * kp * t + 2 * t * m + 8 * kp * m,
         ),
-    )(at, g, corr)
+    )(*args)
 
 
 def local(ring, acts, grads, basis_in, basis_out, corr):
@@ -101,14 +111,18 @@
     n_row = n_chip * 2
     n_col = lax.axis_size("col")
     tok_dev = acts.shape[0]
+    assert CHUNKS == 1
     half = tok_dev // CHUNKS
     tokens = tok_dev * n_row
 
+    gathered = lax.all_gather(acts, ROW, axis=0, tiled=True)
+    k_rows = basis_in.shape[0]
+    kp = k_rows // K_PIECES
     act_t = []
-    for c in range(CHUNKS):
-        gathered = lax.all_gather(acts[c * half:(c + 1) * half], ROW, axis=0, tiled=True)
+    for i in range(K_PIECES):
         part = lax.dot_general(
-            basis_in, gathered, (((1,), (1,)), ((), ())), preferred_element_type=jnp.float32
+            basis_in[i * kp:(i + 1) * kp], gathered, (((1,), (1,)), ((), ())),
+            preferred_element_type=jnp.float32,
         )
         if n_col == 2:
             other = lax.ppermute(part.astype(jnp.bfloat16), "col", swap_perm(2))
@@ -136,11 +150,10 @@
     share = ring_reduce_scatter(summed, ring, "rchip")
     grad_rot = lax.all_gather(share.astype(jnp.bfloat16), ("core", "rchip"), axis=0, tiled=True)
 
-    seg = per_seq * half
-    at = jnp.concatenate(
-        [act_t[c][:, s * seg:(s + 1) * seg] for s in range(SEQS) for c in range(CHUNKS)], axis=1
-    )
-    return correction(at, grad_rot, corr)
+    out = None
+    for i in range(K_PIECES):
+        out = correction(act_t[i], grad_rot, corr, i, out)
+    return out
 
 
 def solution(mesh):

time: 429 us -> 411 us (0.958)
  waiting for transfers between devices: 221 us -> 182 us
  matrix products: 66.1 us -> 76.6 us
  Pallas kernels: 33.7 us -> 43.6 us
    ppermute x1 -> x2, waiting for transfers between devices: 77.3 us -> 37.4 us  [local(): other = lax.ppermute(part.astype(jnp.bfloat16), 'col', swap_perm(2))]
    dot_general x1 -> x2, matrix products: 59.7 us -> 70.2 us  [local(): lax.dot_general(basis_in[i * kp:(i + 1) * kp], gathered, (((1,), (1,)), (...]
    pallas_call x1 -> x2, Pallas kernels: 33.7 us -> 43.6 us  [correction(): pl.pallas_call(functools.partial(correction_kernel, seg), out_shape=jax.S...]
    unnamed x10 -> x14, local copies, waits for them, and re-layouts: 8.58 us -> 7.82 us
  transfers between devices with their start and end apart: 19 -> 20, of which waited for: 16 -> 17; matrix products, arithmetic and copies ran while one was open for 26% -> 30% of each run, Pallas kernels for 0% -> 0%
where the time goes in v6:
time: 411 us; the launch traced here: 409 us
  waiting for transfers between devices  182 us (44%)
  matrix products  76.6 us (19%)
  Pallas kernels  43.6 us (11%)
  other arithmetic  33.9 us (8%)
  between operations  31.4 us (8%)
  starting transfers between devices  21 us (5%)
  local copies, waits for them, and re-layouts  20.8 us (5%)
    ppermute x7, waiting for transfers between devices, ring_reduce_scatter(): buf_a = lax.ppermute(buf_a, axis, right) + block(xa, p - 1 - s + 2 * n)  125 us
    dot_general x2, matrix products, local(): lax.dot_general(basis_in[i * kp:(i + 1) * kp], gathered, (((1,), (1,)), (...  70.2 us
    pallas_call x2, Pallas kernels, correction(): pl.pallas_call(functools.partial(correction_kernel, seg), out_shape=jax.S...  43.6 us
    ppermute x2, waiting for transfers between devices, local(): other = lax.ppermute(part.astype(jnp.bfloat16), 'col', swap_perm(2))  37.4 us
    ppermute x1, waiting for transfers between devices, local(): other = lax.ppermute(grads, 'col', swap_perm(2))  12.1 us
    ppermute x7, starting transfers between devices, ring_reduce_scatter(): buf_a = lax.ppermute(buf_a, axis, right) + block(xa, p - 1 - s + 2 * n)  12 us
    add x1, other arithmetic, local(): summed = keep + lax.ppermute(send, 'core', swap_perm(2))  11.4 us
  transfers between devices with their start and end apart: 20, of which 17 were waited for; matrix products, arithmetic and copies ran while one was open for 30% of the time, Pallas kernels for 0%

profile of v6, /device:TPU:0, one launch (start us, length us, event | category | flops | bytes accessed | tf_op | source)
XLA Modules:
  0.0 409.0 jit_solution(10144489408937545411)
XLA Ops:
  7.3 3.0 collective-permute-start.1
  10.3 12.1 %collective-permute-done.1 = bf16[512,512]{1,0:T(8,128)(2,1)S(1)} collective-permute-done((bf16[512,512]{1,0:T(8,128)(2,1)}, bf16[512,512]{1,0:T(8,128)(2,1)S(1)}, u32[]{:S(2)}, u32[]{:S(2)}) %collective-permute-start.1) | collective-permute-done | bytes 524320 | tf_op jit(solution)/shard_map/ppermute | solution.py:134
  23.6 6.4 %fusion.4 = f32[1024,4096]{1,0:T(8,128)S(1)} fusion(bf16[4096,512]{1,0:T(8,128)(2,1)} %param.10, bf16[512,512]{1,0:T(8,128)(2,1)S(1)} %get-tuple-element.8, bf16[512,512]{1,0:T(8,128)(2,1)S(1)} %get-tuple-element.7), kind=kOutput, calls=%fused_computation.7 | convolution fusion | flops 4297064448 | bytes 22020096 | tf_op jit(solution)/shard_map/dot_general | solution.py:142
  30.0 4.1 %constant_dynamic-slice_fusion.2 = f32[512,4096]{1,0:T(8,128)} fusion(f32[1024,4096]{1,0:T(8,128)S(1)} %fusion.4, s32[]{:T(128)S(6)} %select_n.176), kind=kLoop, calls=%fused_computation.30 | loop fusion | bytes 16777220 | tf_op jit(solution)/shard_map/dynamic_slice | solution.py:148
  34.1 4.6 %copy-done.1 = f32[1024,4096]{1,0:T(8,128)} copy-done((f32[1024,4096]{1,0:T(8,128)}, f32[1024,4096]{1,0:T(8,128)S(1)}, u32[]{:S(2)}) %copy-start.1) | copy-done | bytes 16777240
  49.6 4.5 %collective-permute-done.2 = f32[512,4096]{1,0:T(8,128)} collective-permute-done((f32[512,4096]{1,0:T(8,128)}, f32[512,4096]{1,0:T(8,128)}, u32[]{:S(2)}, u32[]{:S(2)}) %collective-permute-start.2) | collective-permute-done | bytes 8388640 | tf_op jit(solution)/shard_map/ppermute | solution.py:149
  54.2 11.4 %dynamic-slice_add_fusion = f32[512,4096]{1,0:T(8,128)} fusion(f32[512,4096]{1,0:T(8,128)} %collective-permute-done.2, f32[1024,4096]{1,0:T(8,128)} %copy-done.1, s32[]{:T(128)S(6)} %select_n.175), kind=kLoop, calls=%fused_computation.4 | loop fusion | flops 2097152 | bytes 25165828 | tf_op jit(solution)/shard_map/add | solution.py:149
  65.6 6.4 %fusion.9 = (f32[512,2048]{1,0:T(8,128)S(1)}, f32[512,2048]{1,0:T(8,128)}) fusion(f32[512,4096]{1,0:T(8,128)} %dynamic-slice_add_fusion), kind=kLoop, calls=%fused_computation.32 | loop fusion | bytes 16777216 | tf_op jit(solution)/shard_map/slice | solution.py:58
  79.2 20.7 %collective-permute-done.3 = f32[64,2048]{1,0:T(8,128)S(1)} collective-permute-done((f32[64,2048]{1,0:T(8,128)S(1)}, f32[64,2048]{1,0:T(8,128)S(1)}, u32[]{:S(2)}, u32[]{:S(2)}) %collective-permute-start.3) | collective-permute-done | bytes 524320 | tf_op jit(solution)/shard_map/ppermute | solution.py:62
  106.1 20.5 %collective-permute-done.4 = f32[64,2048]{1,0:T(8,128)S(1)} collective-permute-done((f32[64,2048]{1,0:T(8,128)S(1)}, f32[64,2048]{1,0:T(8,128)S(1)}, u32[]{:S(2)}, u32[]{:S(2)}) %collective-permute-start.4) | collective-permute-done | bytes 524320 | tf_op jit(solution)/shard_map/ppermute | solution.py:62
  132.8 20.3 %collective-permute-done.5 = f32[64,2048]{1,0:T(8,128)S(1)} collective-permute-done((f32[64,2048]{1,0:T(8,128)S(1)}, f32[64,2048]{1,0:T(8,128)S(1)}, u32[]{:S(2)}, u32[]{:S(2)}) %collective-permute-start.5) | collective-permute-done | bytes 524320 | tf_op jit(solution)/shard_map/ppermute | solution.py:62
  154.2 2.0 collective-permute-start.6
  159.2 20.2 %collective-permute-done.6 = f32[64,2048]{1,0:T(8,128)S(1)} collective-permute-done((f32[64,2048]{1,0:T(8,128)S(1)}, f32[64,2048]{1,0:T(8,128)S(1)}, u32[]{:S(2)}, u32[]{:S(2)}) %collective-permute-start.6) | collective-permute-done | bytes 524320 | tf_op jit(solution)/shard_map/ppermute | solution.py:62
  180.5 2.0 collective-permute-start.7
  185.5 20.0 %collective-permute-done.7 = f32[64,2048]{1,0:T(8,128)S(1)} collective-permute-done((f32[64,2048]{1,0:T(8,128)S(1)}, f32[64,2048]{1,0:T(8,128)S(1)}, u32[]{:S(2)}, u32[]{:S(2)}) %collective-permute-start.7) | collective-permute-done | bytes 524320 | tf_op jit(solution)/shard_map/ppermute | solution.py:62
  211.0 14.3 %collective-permute-done.8 = f32[64,2048]{1,0:T(8,128)S(1)} collective-permute-done((f32[64,2048]{1,0:T(8,128)S(1)}, f32[64,2048]{1,0:T(8,128)S(1)}, u32[]{:S(2)}, u32[]{:S(2)}) %collective-permute-start.8) | collective-permute-done | bytes 524320 | tf_op jit(solution)/shard_map/ppermute | solution.py:62
  230.4 8.7 %collective-permute-done.9 = f32[64,2048]{1,0:T(8,128)S(1)} collective-permute-done((f32[64,2048]{1,0:T(8,128)S(1)}, f32[64,2048]{1,0:T(8,128)S(1)}, u32[]{:S(2)}, u32[]{:S(2)}) %collective-permute-start.9) | collective-permute-done | bytes 524320 | tf_op jit(solution)/shard_map/ppermute | solution.py:62
  242.4 35.0 %fusion.12 = (bf16[896,1024]{1,0:T(8,128)(2,1)}, f32[896,1024]{1,0:T(8,128)}) fusion(bf16[1024,14336]{1,0:T(8,128)(2,1)} %all-gather.3.cloned.1.call-done, bf16[1792,14336]{1,0:T(8,128)(2,1)} %param.9), kind=kOutput, calls=%fused_computation.35 | convolution fusion | flops 26307592192 | bytes 60555264 | tf_op jit(solution)/shard_map/dot_general | solution.py:123
  279.1 35.2 %fusion.11 = (bf16[896,1024]{1,0:T(8,128)(2,1)}, f32[896,1024]{1,0:T(8,128)}) fusion(bf16[1024,14336]{1,0:T(8,128)(2,1)} %all-gather.3.cloned.1.call-done, bf16[1792,14336]{1,0:T(8,128)(2,1)} %param.9), kind=kOutput, calls=%fused_computation.34 | convolution fusion | flops 26307592192 | bytes 60555264 | tf_op jit(solution)/shard_map/dot_general | solution.py:123
  314.6 5.0 %collective-permute-done.17 = bf16[896,1024]{1,0:T(8,128)(2,1)S(1)} collective-permute-done((bf16[896,1024]{1,0:T(8,128)(2,1)}, bf16[896,1024]{1,0:T(8,128)(2,1)S(1)}, u32[]{:S(2)}, u32[]{:S(2)}) %collective-permute-start.17) | collective-permute-done | bytes 1835040 | tf_op jit(solution)/shard_map/ppermute | solution.py:128
  320.9 3.3 add_convert_fusion.at_ref
  324.2 32.4 %collective-permute-done = bf16[896,1024]{1,0:T(8,128)(2,1)S(1)} collective-permute-done((bf16[896,1024]{1,0:T(8,128)(2,1)}, bf16[896,1024]{1,0:T(8,128)(2,1)S(1)}, u32[]{:S(2)}, u32[]{:S(2)}) %collective-permute-start) | collective-permute-done | bytes 1835040 | tf_op jit(solution)/shard_map/ppermute | solution.py:128
  358.5 21.9 %shard_map.73.rest_0_ = f32[1792,4096]{1,0:T(8,128)} custom-call(bf16[896,1024]{1,0:T(8,128)(2,1)S(1)} %add_convert_fusion.at_ref, bf16[1024,4096]{1,0:T(8,128)(2,1)} %all-gather.5.cloned.1.call-done.g_ref, f32[1792,4096]{1,0:T(8,128)} %corr_ref.3), custom_call_target="tpu_custom_call" | custom-call | flops 7527202816 | bytes 39583744 | tf_op jit(solution)/shard_map/pallas_call | solution.py:93
  380.4 21.8 %shard_map.74 = f32[1792,4096]{1,0:T(8,128)} custom-call(bf16[896,1024]{1,0:T(8,128)(2,1)S(1)} %copy-done, bf16[1024,4096]{1,0:T(8,128)(2,1)} %all-gather.5.cloned.1.call-done.g_ref, f32[1792,4096]{1,0:T(8,128)} %corr_ref.3, f32[1792,4096]{1,0:T(8,128)} %shard_map.73.rest_0_), custom_call_target="tpu_custom_call", output_to_operand_aliasing={{}: (3, {})} | custom-call | flops 7527202816 | bytes 39583744 | tf_op jit(solution)/shard_map/pallas_call | solution.py:93
  (62 shorter events, 41.9 us)
Async XLA Ops:
  6.5 235.9 %all-gather.3.cloned.1.call-start = ((), (), s32[]{:S(2)}) async-start(), calls=%async_computation | async-start | bytes 31195136 | tf_op jit(solution)/shard_map/all_gather | solution.py:118
  7.3 351.3 %all-gather.5.cloned.1.call-start = ((), (), s32[]{:S(2)}) async-start(), calls=%async_computation.1 | async-start | bytes 8912896 | tf_op jit(solution)/shard_map/all_gather | solution.py:151
  7.3 15.2 %collective-permute-start.1 = (bf16[512,512]{1,0:T(8,128)(2,1)}, bf16[512,512]{1,0:T(8,128)(2,1)S(1)}, u32[]{:S(2)}, u32[]{:S(2)}) collective-permute-start(bf16[512,512]{1,0:T(8,128)(2,1)} %param.8), channel_id=1, source_target_pairs={{0,1},{1,0},{2,3},{3,2},{4,5},{5,4},{6,7},{7,6},{8,9},{9,8},{10,11... | collective-permute-start | bytes 1572872 | tf_op jit(solution)/shard_map/ppermute | solution.py:134
  30.0 8.7 %copy-start.1 = (f32[1024,4096]{1,0:T(8,128)}, f32[1024,4096]{1,0:T(8,128)S(1)}, u32[]{:S(2)}) copy-start(f32[1024,4096]{1,0:T(8,128)S(1)} %fusion.4) | copy-start | bytes 50331652
  30.0 18.2 %copy-start.5 = (s32[8]{0:T(128)S(1)}, s32[8]{0:T(128)}, u32[]{:S(2)}) copy-start(s32[8]{0:T(128)} %constant.177.clone) | copy-start | bytes 100
  38.7 15.5 %collective-permute-start.2 = (f32[512,4096]{1,0:T(8,128)}, f32[512,4096]{1,0:T(8,128)}, u32[]{:S(2)}, u32[]{:S(2)}) collective-permute-start(f32[512,4096]{1,0:T(8,128)} %constant_dynamic-slice_fusion.2), channel_id=1, source_target_pairs={{0,2},{2,0},{1,3},{3,1},{4,6},{6,4},{5,7},{7,5},{8,10},{10,8},{9,1... | collective-permute-start | bytes 25165832 | tf_op jit(solution)/shard_map/ppermute | solution.py:149
  74.0 25.8 %collective-permute-start.3 = (f32[64,2048]{1,0:T(8,128)S(1)}, f32[64,2048]{1,0:T(8,128)S(1)}, u32[]{:S(2)}, u32[]{:S(2)}) collective-permute-start(f32[64,2048]{1,0:T(8,128)S(1)} %constant_dynamic-slice_fusion.1), channel_id=1, source_target_pairs={{0,8},{8,16},{16,24},{24,28},{28,20},{20,12},{12,4},{4,0},{1,9},{9... | collective-permute-start | bytes 1572872 | tf_op jit(solution)/shard_map/ppermute | solution.py:62
  77.7 25.8 %collective-permute-start.10 = (f32[64,2048]{1,0:T(8,128)S(1)}, f32[64,2048]{1,0:T(8,128)S(1)}, u32[]{:S(2)}, u32[]{:S(2)}) collective-permute-start(f32[64,2048]{1,0:T(8,128)S(1)} %constant_dynamic-slice_fusion), channel_id=1, source_target_pairs={{0,4},{8,0},{16,8},{24,16},{28,24},{20,28},{12,20},{4,12},{1,5},{9... | collective-permute-start | bytes 1572872 | tf_op jit(solution)/shard_map/ppermute | solution.py:63
  101.0 25.6 %collective-permute-start.4 = (f32[64,2048]{1,0:T(8,128)S(1)}, f32[64,2048]{1,0:T(8,128)S(1)}, u32[]{:S(2)}, u32[]{:S(2)}) collective-permute-start(f32[64,2048]{1,0:T(8,128)S(1)} %dynamic-slice_add_fusion.12), channel_id=1, source_target_pairs={{0,8},{8,16},{16,24},{24,28},{28,20},{20,12},{12,4},{4,0},{1,9},{9... | collective-permute-start | bytes 1572872 | tf_op jit(solution)/shard_map/ppermute | solution.py:62
  104.5 25.6 %collective-permute-start.11 = (f32[64,2048]{1,0:T(8,128)S(1)}, f32[64,2048]{1,0:T(8,128)S(1)}, u32[]{:S(2)}, u32[]{:S(2)}) collective-permute-start(f32[64,2048]{1,0:T(8,128)S(1)} %dynamic-slice_add_fusion.6), channel_id=1, source_target_pairs={{0,4},{8,0},{16,8},{24,16},{28,24},{20,28},{12,20},{4,12},{1,5},{9... | collective-permute-start | bytes 1572872 | tf_op jit(solution)/shard_map/ppermute | solution.py:63
  127.7 25.4 %collective-permute-start.5 = (f32[64,2048]{1,0:T(8,128)S(1)}, f32[64,2048]{1,0:T(8,128)S(1)}, u32[]{:S(2)}, u32[]{:S(2)}) collective-permute-start(f32[64,2048]{1,0:T(8,128)S(1)} %dynamic-slice_add_fusion.11), channel_id=1, source_target_pairs={{0,8},{8,16},{16,24},{24,28},{28,20},{20,12},{12,4},{4,0},{1,9},{9... | collective-permute-start | bytes 1572872 | tf_op jit(solution)/shard_map/ppermute | solution.py:62
  131.2 25.4 %collective-permute-start.12 = (f32[64,2048]{1,0:T(8,128)S(1)}, f32[64,2048]{1,0:T(8,128)S(1)}, u32[]{:S(2)}, u32[]{:S(2)}) collective-permute-start(f32[64,2048]{1,0:T(8,128)S(1)} %dynamic-slice_add_fusion.5), channel_id=1, source_target_pairs={{0,4},{8,0},{16,8},{24,16},{28,24},{20,28},{12,20},{4,12},{1,5},{9... | collective-permute-start | bytes 1572872 | tf_op jit(solution)/shard_map/ppermute | solution.py:63
  154.2 25.2 %collective-permute-start.6 = (f32[64,2048]{1,0:T(8,128)S(1)}, f32[64,2048]{1,0:T(8,128)S(1)}, u32[]{:S(2)}, u32[]{:S(2)}) collective-permute-start(f32[64,2048]{1,0:T(8,128)S(1)} %dynamic-slice_add_fusion.10), channel_id=1, source_target_pairs={{0,8},{8,16},{16,24},{24,28},{28,20},{20,12},{12,4},{4,0},{1,9},{9... | collective-permute-start | bytes 1572872 | tf_op jit(solution)/shard_map/ppermute | solution.py:62
  157.7 25.1 %collective-permute-start.13 = (f32[64,2048]{1,0:T(8,128)S(1)}, f32[64,2048]{1,0:T(8,128)S(1)}, u32[]{:S(2)}, u32[]{:S(2)}) collective-permute-start(f32[64,2048]{1,0:T(8,128)S(1)} %dynamic-slice_add_fusion.4), channel_id=1, source_target_pairs={{0,4},{8,0},{16,8},{24,16},{28,24},{20,28},{12,20},{4,12},{1,5},{9... | collective-permute-start | bytes 1572872 | tf_op jit(solution)/shard_map/ppermute | solution.py:63
  180.5 25.0 %collective-permute-start.7 = (f32[64,2048]{1,0:T(8,128)S(1)}, f32[64,2048]{1,0:T(8,128)S(1)}, u32[]{:S(2)}, u32[]{:S(2)}) collective-permute-start(f32[64,2048]{1,0:T(8,128)S(1)} %dynamic-slice_add_fusion.9), channel_id=1, source_target_pairs={{0,8},{8,16},{16,24},{24,28},{28,20},{20,12},{12,4},{4,0},{1,9},{9... | collective-permute-start | bytes 1572872 | tf_op jit(solution)/shard_map/ppermute | solution.py:62
  183.9 24.9 %collective-permute-start.14 = (f32[64,2048]{1,0:T(8,128)S(1)}, f32[64,2048]{1,0:T(8,128)S(1)}, u32[]{:S(2)}, u32[]{:S(2)}) collective-permute-start(f32[64,2048]{1,0:T(8,128)S(1)} %dynamic-slice_add_fusion.3), channel_id=1, source_target_pairs={{0,4},{8,0},{16,8},{24,16},{28,24},{20,28},{12,20},{4,12},{1,5},{9... | collective-permute-start | bytes 1572872 | tf_op jit(solution)/shard_map/ppermute | solution.py:63
  206.7 18.6 %collective-permute-start.8 = (f32[64,2048]{1,0:T(8,128)S(1)}, f32[64,2048]{1,0:T(8,128)S(1)}, u32[]{:S(2)}, u32[]{:S(2)}) collective-permute-start(f32[64,2048]{1,0:T(8,128)S(1)} %dynamic-slice_add_fusion.8), channel_id=1, source_target_pairs={{0,8},{8,16},{16,24},{24,28},{28,20},{20,12},{12,4},{4,0},{1,9},{9... | collective-permute-start | bytes 1572872 | tf_op jit(solution)/shard_map/ppermute | solution.py:62
  209.9 16.8 %collective-permute-start.15 = (f32[64,2048]{1,0:T(8,128)S(1)}, f32[64,2048]{1,0:T(8,128)S(1)}, u32[]{:S(2)}, u32[]{:S(2)}) collective-permute-start(f32[64,2048]{1,0:T(8,128)S(1)} %dynamic-slice_add_fusion.2), channel_id=1, source_target_pairs={{0,4},{8,0},{16,8},{24,16},{28,24},{20,28},{12,20},{4,12},{1,5},{9... | collective-permute-start | bytes 1572872 | tf_op jit(solution)/shard_map/ppermute | solution.py:63
  226.3 12.8 %collective-permute-start.9 = (f32[64,2048]{1,0:T(8,128)S(1)}, f32[64,2048]{1,0:T(8,128)S(1)}, u32[]{:S(2)}, u32[]{:S(2)}) collective-permute-start(f32[64,2048]{1,0:T(8,128)S(1)} %dynamic-slice_add_fusion.7), channel_id=1, source_target_pairs={{0,8},{8,16},{16,24},{24,28},{28,20},{20,12},{12,4},{4,0},{1,9},{9... | collective-permute-start | bytes 1572872 | tf_op jit(solution)/shard_map/ppermute | solution.py:62
  227.8 12.6 %collective-permute-start.16 = (f32[64,2048]{1,0:T(8,128)S(1)}, f32[64,2048]{1,0:T(8,128)S(1)}, u32[]{:S(2)}, u32[]{:S(2)}) collective-permute-start(f32[64,2048]{1,0:T(8,128)S(1)} %dynamic-slice_add_fusion.1), channel_id=1, source_target_pairs={{0,4},{8,0},{16,8},{24,16},{28,24},{20,28},{12,20},{4,12},{1,5},{9... | collective-permute-start | bytes 1572872 | tf_op jit(solution)/shard_map/ppermute | solution.py:63
  277.4 42.2 %collective-permute-start.17 = (bf16[896,1024]{1,0:T(8,128)(2,1)}, bf16[896,1024]{1,0:T(8,128)(2,1)S(1)}, u32[]{:S(2)}, u32[]{:S(2)}) collective-permute-start(bf16[896,1024]{1,0:T(8,128)(2,1)} %get-tuple-element.25), channel_id=1, source_target_pairs={{0,1},{1,0},{2,3},{3,2},{4,5},{5,4},{6,7},{7,6},{8,9},{9,8},{10,11... | collective-permute-start | bytes 5505032 | tf_op jit(solution)/shard_map/ppermute | solution.py:128
  314.3 42.3 %copy-start.3 = (f32[896,1024]{1,0:T(8,128)S(1)}, f32[896,1024]{1,0:T(8,128)}, u32[]{:S(2)}) copy-start(f32[896,1024]{1,0:T(8,128)} %get-tuple-element.24) | copy-start | bytes 11010052
  314.3 42.3 %collective-permute-start = (bf16[896,1024]{1,0:T(8,128)(2,1)}, bf16[896,1024]{1,0:T(8,128)(2,1)S(1)}, u32[]{:S(2)}, u32[]{:S(2)}) collective-permute-start(bf16[896,1024]{1,0:T(8,128)(2,1)} %get-tuple-element.23), channel_id=1, source_target_pairs={{0,1},{1,0},{2,3},{3,2},{4,5},{5,4},{6,7},{7,6},{8,9},{9,8},{10,11... | collective-permute-start | bytes 5505032 | tf_op jit(solution)/shard_map/ppermute | solution.py:128
  358.5 21.9 %copy-start = (bf16[896,1024]{1,0:T(8,128)(2,1)S(1)}, bf16[896,1024]{1,0:T(8,128)(2,1)}, u32[]{:S(2)}) copy-start(bf16[896,1024]{1,0:T(8,128)(2,1)} %add_convert_fusion.1.at_ref) | copy-start | bytes 5505028
  (3 other events, 11.9 us)
Sparse Core Ops, SparseCore 0:
  8.9 213.3 all-gather.2
  242.5 75.4 all-gather.4

commit v7 on v6

--- a/solution.py
+++ b/solution.py
@@ -74,7 +74,7 @@
     out_ref[...] = corr_ref[...] + total * (1.0 / (SEQS * SEQ_LEN))
 
 
-def correction(at, g, corr, piece, prev=None, tm=256):
+def correction(at, g, corr, piece, prev=None, tm=512):
     kp, t = at.shape
     m = g.shape[1]
     tm = min(tm, m)
@@ -118,17 +118,15 @@
     gathered = lax.all_gather(acts, ROW, axis=0, tiled=True)
     k_rows = basis_in.shape[0]
     kp = k_rows // K_PIECES
-    act_t = []
+    parts, recvs = [], []
     for i in range(K_PIECES):
         part = lax.dot_general(
             basis_in[i * kp:(i + 1) * kp], gathered, (((1,), (1,)), ((), ())),
             preferred_element_type=jnp.float32,
         )
+        parts.append(part)
         if n_col == 2:
-            other = lax.ppermute(part.astype(jnp.bfloat16), "col", swap_perm(2))
-            act_t.append((part + other.astype(jnp.float32)).astype(jnp.bfloat16))
-        else:
-            act_t.append(lax.psum(part, "col").astype(jnp.bfloat16))
+            recvs.append(lax.ppermute(part.astype(jnp.bfloat16), "col", swap_perm(2)))
 
     if n_col == 2:
         other = lax.ppermute(grads, "col", swap_perm(2))
@@ -152,7 +150,14 @@
 
     out = None
     for i in range(K_PIECES):
-        out = correction(act_t[i], grad_rot, corr, i, out)
+        if n_col == 2:
+            recv = recvs[i]
+            if out is not None:
+                out, recv = lax.optimization_barrier((out, recv))
+            act_t = (parts[i] + recv.astype(jnp.float32)).astype(jnp.bfloat16)
+        else:
+            act_t = lax.psum(parts[i], "col").astype(jnp.bfloat16)
+        out = correction(act_t, grad_rot, corr, i, out)
     return out
 
 

time: 411 us -> 386 us (0.939)
  waiting for transfers between devices: 182 us -> 162 us
  Pallas kernels: 43.6 us -> 37.4 us
    ppermute x2, waiting for transfers between devices: 37.4 us -> 18.9 us  [local(): recvs.append(lax.ppermute(part.astype(jnp.bfloat16), 'col', swap_perm(2)))]
    pallas_call x2, Pallas kernels: 43.6 us -> 37.4 us  [correction(): pl.pallas_call(functools.partial(correction_kernel, seg), out_shape=jax.S...]
  transfers between devices with their start and end apart: 20 -> 20, of which waited for: 17 -> 17; matrix products, arithmetic and copies ran while one was open for 30% -> 32% of each run, Pallas kernels for 0% -> 5%
where the time goes in v7:
time: 386 us; the launch traced here: 384 us
  waiting for transfers between devices  162 us (42%)
  matrix products  76.6 us (20%)
  Pallas kernels  37.4 us (10%)
  other arithmetic  34.2 us (9%)
  between operations  32.4 us (8%)
  starting transfers between devices  20.9 us (5%)
  local copies, waits for them, and re-layouts  20.9 us (5%)
    ppermute x7, waiting for transfers between devices, ring_reduce_scatter(): buf_a = lax.ppermute(buf_a, axis, right) + block(xa, p - 1 - s + 2 * n)  125 us
    dot_general x2, matrix products, local(): lax.dot_general(basis_in[i * kp:(i + 1) * kp], gathered, (((1,), (1,)), (...  70.2 us
    pallas_call x2, Pallas kernels, correction(): pl.pallas_call(functools.partial(correction_kernel, seg), out_shape=jax.S...  37.4 us
    ppermute x2, waiting for transfers between devices, local(): recvs.append(lax.ppermute(part.astype(jnp.bfloat16), 'col', swap_perm(2)))  18.9 us
    ppermute x1, waiting for transfers between devices, local(): other = lax.ppermute(grads, 'col', swap_perm(2))  12.1 us
    ppermute x7, starting transfers between devices, ring_reduce_scatter(): buf_a = lax.ppermute(buf_a, axis, right) + block(xa, p - 1 - s + 2 * n)  12 us
    add x1, other arithmetic, local(): summed = keep + lax.ppermute(send, 'core', swap_perm(2))  11.4 us
    unnamed x12, local copies, waits for them, and re-layouts  7.78 us
  transfers between devices with their start and end apart: 20, of which 17 were waited for; matrix products, arithmetic and copies ran while one was open for 32% of the time, Pallas kernels for 5%

profile of v7, /device:TPU:0, one launch (start us, length us, event | category | flops | bytes accessed | tf_op | source)
XLA Modules:
  0.0 384.4 jit_solution(18258142475173350156)
XLA Ops:
  7.3 3.0 collective-permute-start.1
  10.3 12.1 %collective-permute-done.1 = bf16[512,512]{1,0:T(8,128)(2,1)S(1)} collective-permute-done((bf16[512,512]{1,0:T(8,128)(2,1)}, bf16[512,512]{1,0:T(8,128)(2,1)S(1)}, u32[]{:S(2)}, u32[]{:S(2)}) %collective-permute-start.1) | collective-permute-done | bytes 524320 | tf_op jit(solution)/shard_map/ppermute | solution.py:132
  23.6 6.4 %fusion.4 = f32[1024,4096]{1,0:T(8,128)S(1)} fusion(bf16[4096,512]{1,0:T(8,128)(2,1)} %param.10, bf16[512,512]{1,0:T(8,128)(2,1)S(1)} %get-tuple-element.12, bf16[512,512]{1,0:T(8,128)(2,1)S(1)} %get-tuple-element.11), kind=kOutput, calls=%fused_computation.7 | convolution fusion | flops 4297064448 | bytes 22020096 | tf_op jit(solution)/shard_map/dot_general | solution.py:140
  30.0 4.1 %constant_dynamic-slice_fusion.2 = f32[512,4096]{1,0:T(8,128)} fusion(f32[1024,4096]{1,0:T(8,128)S(1)} %fusion.4, s32[]{:T(128)S(6)} %select_n.176), kind=kLoop, calls=%fused_computation.30 | loop fusion | bytes 16777220 | tf_op jit(solution)/shard_map/dynamic_slice | solution.py:146
  34.1 4.6 %copy-done = f32[1024,4096]{1,0:T(8,128)} copy-done((f32[1024,4096]{1,0:T(8,128)}, f32[1024,4096]{1,0:T(8,128)S(1)}, u32[]{:S(2)}) %copy-start) | copy-done | bytes 16777240
  50.7 3.5 collective-permute-done.2
  54.2 11.4 %dynamic-slice_add_fusion = f32[512,4096]{1,0:T(8,128)} fusion(f32[512,4096]{1,0:T(8,128)} %collective-permute-done.2, f32[1024,4096]{1,0:T(8,128)} %copy-done, s32[]{:T(128)S(6)} %select_n.175), kind=kLoop, calls=%fused_computation.4 | loop fusion | flops 2097152 | bytes 25165828 | tf_op jit(solution)/shard_map/add | solution.py:147
  65.6 6.4 %fusion.9 = (f32[512,2048]{1,0:T(8,128)S(1)}, f32[512,2048]{1,0:T(8,128)}) fusion(f32[512,4096]{1,0:T(8,128)} %dynamic-slice_add_fusion), kind=kLoop, calls=%fused_computation.32 | loop fusion | bytes 16777216 | tf_op jit(solution)/shard_map/slice | solution.py:58
  79.1 20.8 %collective-permute-done.3 = f32[64,2048]{1,0:T(8,128)S(1)} collective-permute-done((f32[64,2048]{1,0:T(8,128)S(1)}, f32[64,2048]{1,0:T(8,128)S(1)}, u32[]{:S(2)}, u32[]{:S(2)}) %collective-permute-start.3) | collective-permute-done | bytes 524320 | tf_op jit(solution)/shard_map/ppermute | solution.py:62
  106.1 20.5 %collective-permute-done.4 = f32[64,2048]{1,0:T(8,128)S(1)} collective-permute-done((f32[64,2048]{1,0:T(8,128)S(1)}, f32[64,2048]{1,0:T(8,128)S(1)}, u32[]{:S(2)}, u32[]{:S(2)}) %collective-permute-start.4) | collective-permute-done | bytes 524320 | tf_op jit(solution)/shard_map/ppermute | solution.py:62
  132.7 20.4 %collective-permute-done.5 = f32[64,2048]{1,0:T(8,128)S(1)} collective-permute-done((f32[64,2048]{1,0:T(8,128)S(1)}, f32[64,2048]{1,0:T(8,128)S(1)}, u32[]{:S(2)}, u32[]{:S(2)}) %collective-permute-start.5) | collective-permute-done | bytes 524320 | tf_op jit(solution)/shard_map/ppermute | solution.py:62
  159.2 20.2 %collective-permute-done.6 = f32[64,2048]{1,0:T(8,128)S(1)} collective-permute-done((f32[64,2048]{1,0:T(8,128)S(1)}, f32[64,2048]{1,0:T(8,128)S(1)}, u32[]{:S(2)}, u32[]{:S(2)}) %collective-permute-start.6) | collective-permute-done | bytes 524320 | tf_op jit(solution)/shard_map/ppermute | solution.py:62
  180.5 2.0 collective-permute-start.7
  185.5 20.1 %collective-permute-done.7 = f32[64,2048]{1,0:T(8,128)S(1)} collective-permute-done((f32[64,2048]{1,0:T(8,128)S(1)}, f32[64,2048]{1,0:T(8,128)S(1)}, u32[]{:S(2)}, u32[]{:S(2)}) %collective-permute-start.7) | collective-permute-done | bytes 524320 | tf_op jit(solution)/shard_map/ppermute | solution.py:62
  210.9 14.3 %collective-permute-done.8 = f32[64,2048]{1,0:T(8,128)S(1)} collective-permute-done((f32[64,2048]{1,0:T(8,128)S(1)}, f32[64,2048]{1,0:T(8,128)S(1)}, u32[]{:S(2)}, u32[]{:S(2)}) %collective-permute-start.8) | collective-permute-done | bytes 524320 | tf_op jit(solution)/shard_map/ppermute | solution.py:62
  230.4 8.7 %collective-permute-done.9 = f32[64,2048]{1,0:T(8,128)S(1)} collective-permute-done((f32[64,2048]{1,0:T(8,128)S(1)}, f32[64,2048]{1,0:T(8,128)S(1)}, u32[]{:S(2)}, u32[]{:S(2)}) %collective-permute-start.9) | collective-permute-done | bytes 524320 | tf_op jit(solution)/shard_map/ppermute | solution.py:62
  242.4 35.0 %fusion.11 = (bf16[896,1024]{1,0:T(8,128)(2,1)}, f32[896,1024]{1,0:T(8,128)}) fusion(bf16[1024,14336]{1,0:T(8,128)(2,1)} %all-gather.3.cloned.1.call-done, bf16[1792,14336]{1,0:T(8,128)(2,1)} %param.9), kind=kOutput, calls=%fused_computation.34 | convolution fusion | flops 26307592192 | bytes 60555264 | tf_op jit(solution)/shard_map/dot_general | solution.py:123
  279.1 35.2 %fusion.12 = (bf16[896,1024]{1,0:T(8,128)(2,1)}, f32[896,1024]{1,0:T(8,128)}) fusion(bf16[1024,14336]{1,0:T(8,128)(2,1)} %all-gather.3.cloned.1.call-done, bf16[1792,14336]{1,0:T(8,128)(2,1)} %param.9), kind=kOutput, calls=%fused_computation.35 | convolution fusion | flops 26307592192 | bytes 60555264 | tf_op jit(solution)/shard_map/dot_general | solution.py:123
  314.6 5.1 %collective-permute-done = bf16[896,1024]{1,0:T(8,128)(2,1)S(1)} collective-permute-done((bf16[896,1024]{1,0:T(8,128)(2,1)}, bf16[896,1024]{1,0:T(8,128)(2,1)S(1)}, u32[]{:S(2)}, u32[]{:S(2)}) %collective-permute-start) | collective-permute-done | bytes 1835040 | tf_op jit(solution)/shard_map/ppermute | solution.py:129
  320.9 3.3 add_convert_fusion.1.at_ref
  324.3 18.8 %shard_map.73.rest_0_ = f32[1792,4096]{1,0:T(8,128)} custom-call(bf16[896,1024]{1,0:T(8,128)(2,1)S(1)} %add_convert_fusion.1.at_ref, bf16[1024,4096]{1,0:T(8,128)(2,1)} %all-gather.5.cloned.1.call-done.g_ref, f32[1792,4096]{1,0:T(8,128)} %corr_ref.3), custom_call_target="tpu_custom_call" | custom-call | flops 7527202816 | bytes 39583744 | tf_op jit(solution)/shard_map/pallas_call | solution.py:93
  343.0 13.7 %collective-permute-done.17 = bf16[896,1024]{1,0:T(8,128)(2,1)} collective-permute-done((bf16[896,1024]{1,0:T(8,128)(2,1)}, bf16[896,1024]{1,0:T(8,128)(2,1)}, u32[]{:S(2)}, u32[]{:S(2)}) %collective-permute-start.17) | collective-permute-done | bytes 1835040 | tf_op jit(solution)/shard_map/ppermute | solution.py:129
  356.7 2.2 add_convert_fusion.at_ref
  358.9 18.6 %shard_map.74 = f32[1792,4096]{1,0:T(8,128)} custom-call(bf16[896,1024]{1,0:T(8,128)(2,1)S(1)} %add_convert_fusion.at_ref, bf16[1024,4096]{1,0:T(8,128)(2,1)} %all-gather.5.cloned.1.call-done.g_ref, f32[1792,4096]{1,0:T(8,128)} %corr_ref.3, f32[1792,4096]{1,0:T(8,128)} %shard_map.73.rest_0_), custom_call_target="tpu_custom_call", output_to_operand_aliasing={{}: (3, {})} | custom-call | flops 7527202816 | bytes 39583744 | tf_op jit(solution)/shard_map/pallas_call | solution.py:93
  (60 shorter events, 41.7 us)
Async XLA Ops:
  6.5 235.9 %all-gather.3.cloned.1.call-start = ((), (), s32[]{:S(2)}) async-start(), calls=%async_computation | async-start | bytes 31195136 | tf_op jit(solution)/shard_map/all_gather | solution.py:118
  7.3 317.0 %all-gather.5.cloned.1.call-start = ((), (), s32[]{:S(2)}) async-start(), calls=%async_computation.1 | async-start | bytes 8912896 | tf_op jit(solution)/shard_map/all_gather | solution.py:149
  7.3 15.2 %collective-permute-start.1 = (bf16[512,512]{1,0:T(8,128)(2,1)}, bf16[512,512]{1,0:T(8,128)(2,1)S(1)}, u32[]{:S(2)}, u32[]{:S(2)}) collective-permute-start(bf16[512,512]{1,0:T(8,128)(2,1)} %param.8), channel_id=1, source_target_pairs={{0,1},{1,0},{2,3},{3,2},{4,5},{5,4},{6,7},{7,6},{8,9},{9,8},{10,11... | collective-permute-start | bytes 1572872 | tf_op jit(solution)/shard_map/ppermute | solution.py:132
  30.0 8.7 %copy-start = (f32[1024,4096]{1,0:T(8,128)}, f32[1024,4096]{1,0:T(8,128)S(1)}, u32[]{:S(2)}) copy-start(f32[1024,4096]{1,0:T(8,128)S(1)} %fusion.4) | copy-start | bytes 50331652
  30.0 8.7 %copy-start.5 = (s32[8]{0:T(128)S(1)}, s32[8]{0:T(128)}, u32[]{:S(2)}) copy-start(s32[8]{0:T(128)} %constant.178.clone) | copy-start | bytes 100
  30.0 19.3 %copy-start.4 = (s32[8]{0:T(128)S(1)}, s32[8]{0:T(128)}, u32[]{:S(2)}) copy-start(s32[8]{0:T(128)} %constant.177.clone) | copy-start | bytes 100
  38.7 15.5 %collective-permute-start.2 = (f32[512,4096]{1,0:T(8,128)}, f32[512,4096]{1,0:T(8,128)}, u32[]{:S(2)}, u32[]{:S(2)}) collective-permute-start(f32[512,4096]{1,0:T(8,128)} %constant_dynamic-slice_fusion.2), channel_id=1, source_target_pairs={{0,2},{2,0},{1,3},{3,1},{4,6},{6,4},{5,7},{7,5},{8,10},{10,8},{9,1... | collective-permute-start | bytes 25165832 | tf_op jit(solution)/shard_map/ppermute | solution.py:147
  74.0 25.8 %collective-permute-start.3 = (f32[64,2048]{1,0:T(8,128)S(1)}, f32[64,2048]{1,0:T(8,128)S(1)}, u32[]{:S(2)}, u32[]{:S(2)}) collective-permute-start(f32[64,2048]{1,0:T(8,128)S(1)} %constant_dynamic-slice_fusion.1), channel_id=1, source_target_pairs={{0,8},{8,16},{16,24},{24,28},{28,20},{20,12},{12,4},{4,0},{1,9},{9... | collective-permute-start | bytes 1572872 | tf_op jit(solution)/shard_map/ppermute | solution.py:62
  77.6 25.8 %collective-permute-start.10 = (f32[64,2048]{1,0:T(8,128)S(1)}, f32[64,2048]{1,0:T(8,128)S(1)}, u32[]{:S(2)}, u32[]{:S(2)}) collective-permute-start(f32[64,2048]{1,0:T(8,128)S(1)} %constant_dynamic-slice_fusion), channel_id=1, source_target_pairs={{0,4},{8,0},{16,8},{24,16},{28,24},{20,28},{12,20},{4,12},{1,5},{9... | collective-permute-start | bytes 1572872 | tf_op jit(solution)/shard_map/ppermute | solution.py:63
  101.0 25.6 %collective-permute-start.4 = (f32[64,2048]{1,0:T(8,128)S(1)}, f32[64,2048]{1,0:T(8,128)S(1)}, u32[]{:S(2)}, u32[]{:S(2)}) collective-permute-start(f32[64,2048]{1,0:T(8,128)S(1)} %dynamic-slice_add_fusion.12), channel_id=1, source_target_pairs={{0,8},{8,16},{16,24},{24,28},{28,20},{20,12},{12,4},{4,0},{1,9},{9... | collective-permute-start | bytes 1572872 | tf_op jit(solution)/shard_map/ppermute | solution.py:62
  104.5 25.6 %collective-permute-start.11 = (f32[64,2048]{1,0:T(8,128)S(1)}, f32[64,2048]{1,0:T(8,128)S(1)}, u32[]{:S(2)}, u32[]{:S(2)}) collective-permute-start(f32[64,2048]{1,0:T(8,128)S(1)} %dynamic-slice_add_fusion.6), channel_id=1, source_target_pairs={{0,4},{8,0},{16,8},{24,16},{28,24},{20,28},{12,20},{4,12},{1,5},{9... | collective-permute-start | bytes 1572872 | tf_op jit(solution)/shard_map/ppermute | solution.py:63
  127.7 25.4 %collective-permute-start.5 = (f32[64,2048]{1,0:T(8,128)S(1)}, f32[64,2048]{1,0:T(8,128)S(1)}, u32[]{:S(2)}, u32[]{:S(2)}) collective-permute-start(f32[64,2048]{1,0:T(8,128)S(1)} %dynamic-slice_add_fusion.11), channel_id=1, source_target_pairs={{0,8},{8,16},{16,24},{24,28},{28,20},{20,12},{12,4},{4,0},{1,9},{9... | collective-permute-start | bytes 1572872 | tf_op jit(solution)/shard_map/ppermute | solution.py:62
  131.1 25.4 %collective-permute-start.12 = (f32[64,2048]{1,0:T(8,128)S(1)}, f32[64,2048]{1,0:T(8,128)S(1)}, u32[]{:S(2)}, u32[]{:S(2)}) collective-permute-start(f32[64,2048]{1,0:T(8,128)S(1)} %dynamic-slice_add_fusion.5), channel_id=1, source_target_pairs={{0,4},{8,0},{16,8},{24,16},{28,24},{20,28},{12,20},{4,12},{1,5},{9... | collective-permute-start | bytes 1572872 | tf_op jit(solution)/shard_map/ppermute | solution.py:63
  154.2 25.2 %collective-permute-start.6 = (f32[64,2048]{1,0:T(8,128)S(1)}, f32[64,2048]{1,0:T(8,128)S(1)}, u32[]{:S(2)}, u32[]{:S(2)}) collective-permute-start(f32[64,2048]{1,0:T(8,128)S(1)} %dynamic-slice_add_fusion.10), channel_id=1, source_target_pairs={{0,8},{8,16},{16,24},{24,28},{28,20},{20,12},{12,4},{4,0},{1,9},{9... | collective-permute-start | bytes 1572872 | tf_op jit(solution)/shard_map/ppermute | solution.py:62
  157.6 25.1 %collective-permute-start.13 = (f32[64,2048]{1,0:T(8,128)S(1)}, f32[64,2048]{1,0:T(8,128)S(1)}, u32[]{:S(2)}, u32[]{:S(2)}) collective-permute-start(f32[64,2048]{1,0:T(8,128)S(1)} %dynamic-slice_add_fusion.4), channel_id=1, source_target_pairs={{0,4},{8,0},{16,8},{24,16},{28,24},{20,28},{12,20},{4,12},{1,5},{9... | collective-permute-start | bytes 1572872 | tf_op jit(solution)/shard_map/ppermute | solution.py:63
  180.5 25.0 %collective-permute-start.7 = (f32[64,2048]{1,0:T(8,128)S(1)}, f32[64,2048]{1,0:T(8,128)S(1)}, u32[]{:S(2)}, u32[]{:S(2)}) collective-permute-start(f32[64,2048]{1,0:T(8,128)S(1)} %dynamic-slice_add_fusion.9), channel_id=1, source_target_pairs={{0,8},{8,16},{16,24},{24,28},{28,20},{20,12},{12,4},{4,0},{1,9},{9... | collective-permute-start | bytes 1572872 | tf_op jit(solution)/shard_map/ppermute | solution.py:62
  183.8 24.9 %collective-permute-start.14 = (f32[64,2048]{1,0:T(8,128)S(1)}, f32[64,2048]{1,0:T(8,128)S(1)}, u32[]{:S(2)}, u32[]{:S(2)}) collective-permute-start(f32[64,2048]{1,0:T(8,128)S(1)} %dynamic-slice_add_fusion.3), channel_id=1, source_target_pairs={{0,4},{8,0},{16,8},{24,16},{28,24},{20,28},{12,20},{4,12},{1,5},{9... | collective-permute-start | bytes 1572872 | tf_op jit(solution)/shard_map/ppermute | solution.py:63
  206.7 18.6 %collective-permute-start.8 = (f32[64,2048]{1,0:T(8,128)S(1)}, f32[64,2048]{1,0:T(8,128)S(1)}, u32[]{:S(2)}, u32[]{:S(2)}) collective-permute-start(f32[64,2048]{1,0:T(8,128)S(1)} %dynamic-slice_add_fusion.8), channel_id=1, source_target_pairs={{0,8},{8,16},{16,24},{24,28},{28,20},{20,12},{12,4},{4,0},{1,9},{9... | collective-permute-start | bytes 1572872 | tf_op jit(solution)/shard_map/ppermute | solution.py:62
  209.9 16.9 %collective-permute-start.15 = (f32[64,2048]{1,0:T(8,128)S(1)}, f32[64,2048]{1,0:T(8,128)S(1)}, u32[]{:S(2)}, u32[]{:S(2)}) collective-permute-start(f32[64,2048]{1,0:T(8,128)S(1)} %dynamic-slice_add_fusion.2), channel_id=1, source_target_pairs={{0,4},{8,0},{16,8},{24,16},{28,24},{20,28},{12,20},{4,12},{1,5},{9... | collective-permute-start | bytes 1572872 | tf_op jit(solution)/shard_map/ppermute | solution.py:63
  226.3 12.8 %collective-permute-start.9 = (f32[64,2048]{1,0:T(8,128)S(1)}, f32[64,2048]{1,0:T(8,128)S(1)}, u32[]{:S(2)}, u32[]{:S(2)}) collective-permute-start(f32[64,2048]{1,0:T(8,128)S(1)} %dynamic-slice_add_fusion.7), channel_id=1, source_target_pairs={{0,8},{8,16},{16,24},{24,28},{28,20},{20,12},{12,4},{4,0},{1,9},{9... | collective-permute-start | bytes 1572872 | tf_op jit(solution)/shard_map/ppermute | solution.py:62
  227.8 12.6 %collective-permute-start.16 = (f32[64,2048]{1,0:T(8,128)S(1)}, f32[64,2048]{1,0:T(8,128)S(1)}, u32[]{:S(2)}, u32[]{:S(2)}) collective-permute-start(f32[64,2048]{1,0:T(8,128)S(1)} %dynamic-slice_add_fusion.1), channel_id=1, source_target_pairs={{0,4},{8,0},{16,8},{24,16},{28,24},{20,28},{12,20},{4,12},{1,5},{9... | collective-permute-start | bytes 1572872 | tf_op jit(solution)/shard_map/ppermute | solution.py:63
  277.4 42.3 %collective-permute-start = (bf16[896,1024]{1,0:T(8,128)(2,1)}, bf16[896,1024]{1,0:T(8,128)(2,1)S(1)}, u32[]{:S(2)}, u32[]{:S(2)}) collective-permute-start(bf16[896,1024]{1,0:T(8,128)(2,1)} %get-tuple-element.27), channel_id=1, source_target_pairs={{0,1},{1,0},{2,3},{3,2},{4,5},{5,4},{6,7},{7,6},{8,9},{9,8},{10,11... | collective-permute-start | bytes 5505032 | tf_op jit(solution)/shard_map/ppermute | solution.py:129
  314.3 42.4 %collective-permute-start.17 = (bf16[896,1024]{1,0:T(8,128)(2,1)}, bf16[896,1024]{1,0:T(8,128)(2,1)}, u32[]{:S(2)}, u32[]{:S(2)}) collective-permute-start(bf16[896,1024]{1,0:T(8,128)(2,1)} %get-tuple-element.29), channel_id=1, source_target_pairs={{0,1},{1,0},{2,3},{3,2},{4,5},{5,4},{6,7},{7,6},{8,9},{9,8},{10,11... | collective-permute-start | bytes 5505032 | tf_op jit(solution)/shard_map/ppermute | solution.py:129
  324.3 32.5 %copy-start.2 = (f32[896,1024]{1,0:T(8,128)S(1)}, f32[896,1024]{1,0:T(8,128)}, u32[]{:S(2)}) copy-start(f32[896,1024]{1,0:T(8,128)} %get-tuple-element.30) | copy-start | bytes 11010052
  (2 other events, 3.2 us)
Sparse Core Ops, SparseCore 0:
  8.9 213.3 all-gather.2
  242.5 75.4 all-gather.4

commit v8 on v7

--- a/solution.py
+++ b/solution.py
@@ -12,7 +12,7 @@
 SEQ_LEN = 512
 SEQS = 2
 CHUNKS = 1
-K_PIECES = 2
+K_PIECES = 4
 ROW = ("rchip", "core")
 
 

time: 386 us -> 398 us (1.031)
  waiting for transfers between devices: 162 us -> 144 us
  matrix products: 76.6 us -> 92.2 us
  Pallas kernels: 37.4 us -> 49.9 us
    ppermute x2 -> x4, waiting for transfers between devices: 18.9 us -> 0.01 us  [local(): recvs.append(lax.ppermute(part.astype(jnp.bfloat16), 'col', swap_perm(2)))]
    dot_general x2 -> x4, matrix products: 70.2 us -> 85.8 us  [local(): lax.dot_general(basis_in[i * kp:(i + 1) * kp], gathered, (((1,), (1,)), (...]
    pallas_call x2 -> x4, Pallas kernels: 37.4 us -> 49.9 us  [correction(): pl.pallas_call(functools.partial(correction_kernel, seg), out_shape=jax.S...]
  transfers between devices with their start and end apart: 20 -> 22, of which waited for: 17 -> 15; matrix products, arithmetic and copies ran while one was open for 32% -> 35% of each run, Pallas kernels for 5% -> 9%
where the time goes in v8:
time: 398 us; the launch traced here: 396 us
  waiting for transfers between devices  144 us (36%)
  matrix products  92.2 us (23%)
  Pallas kernels  49.9 us (13%)
  other arithmetic  35.2 us (9%)
  between operations  31.7 us (8%)
  starting transfers between devices  22.9 us (6%)
  local copies, waits for them, and re-layouts  20.5 us (5%)
    ppermute x7, waiting for transfers between devices, ring_reduce_scatter(): buf_a = lax.ppermute(buf_a, axis, right) + block(xa, p - 1 - s + 2 * n)  125 us
    dot_general x4, matrix products, local(): lax.dot_general(basis_in[i * kp:(i + 1) * kp], gathered, (((1,), (1,)), (...  85.8 us
    pallas_call x4, Pallas kernels, correction(): pl.pallas_call(functools.partial(correction_kernel, seg), out_shape=jax.S...  49.9 us
    ppermute x1, waiting for transfers between devices, local(): other = lax.ppermute(grads, 'col', swap_perm(2))  12.1 us
    ppermute x7, starting transfers between devices, ring_reduce_scatter(): buf_a = lax.ppermute(buf_a, axis, right) + block(xa, p - 1 - s + 2 * n)  12 us
    add x1, other arithmetic, local(): summed = keep + lax.ppermute(send, 'core', swap_perm(2))  11.4 us
  transfers between devices with their start and end apart: 22, of which 15 were waited for; matrix products, arithmetic and copies ran while one was open for 35% of the time, Pallas kernels for 9%

profile of v8, /device:TPU:0, one launch (start us, length us, event | category | flops | bytes accessed | tf_op | source)
XLA Modules:
  0.0 396.4 jit_solution(9153577093087981460)
XLA Ops:
  7.3 3.0 collective-permute-start.1
  10.3 12.1 %collective-permute-done.1 = bf16[512,512]{1,0:T(8,128)(2,1)S(1)} collective-permute-done((bf16[512,512]{1,0:T(8,128)(2,1)}, bf16[512,512]{1,0:T(8,128)(2,1)S(1)}, u32[]{:S(2)}, u32[]{:S(2)}) %collective-permute-start.1) | collective-permute-done | bytes 524320 | tf_op jit(solution)/shard_map/ppermute | solution.py:132
  23.6 6.4 %fusion.8 = f32[1024,4096]{1,0:T(8,128)S(1)} fusion(bf16[4096,512]{1,0:T(8,128)(2,1)} %param.10, bf16[512,512]{1,0:T(8,128)(2,1)S(1)} %get-tuple-element.20, bf16[512,512]{1,0:T(8,128)(2,1)S(1)} %get-tuple-element.19), kind=kOutput, calls=%fused_computation.13 | convolution fusion | flops 4297064448 | bytes 22020096 | tf_op jit(solution)/shard_map/dot_general | solution.py:140
  30.0 4.1 %constant_dynamic-slice_fusion.2 = f32[512,4096]{1,0:T(8,128)} fusion(f32[1024,4096]{1,0:T(8,128)S(1)} %fusion.8, s32[]{:T(128)S(6)} %select_n.176), kind=kLoop, calls=%fused_computation.36 | loop fusion | bytes 16777220 | tf_op jit(solution)/shard_map/dynamic_slice | solution.py:146
  34.1 4.6 %copy-done = f32[1024,4096]{1,0:T(8,128)} copy-done((f32[1024,4096]{1,0:T(8,128)}, f32[1024,4096]{1,0:T(8,128)S(1)}, u32[]{:S(2)}) %copy-start) | copy-done | bytes 16777240
  49.9 4.2 %collective-permute-done.2 = f32[512,4096]{1,0:T(8,128)} collective-permute-done((f32[512,4096]{1,0:T(8,128)}, f32[512,4096]{1,0:T(8,128)}, u32[]{:S(2)}, u32[]{:S(2)}) %collective-permute-start.2) | collective-permute-done | bytes 8388640 | tf_op jit(solution)/shard_map/ppermute | solution.py:147
  54.2 11.4 %dynamic-slice_add_fusion = f32[512,4096]{1,0:T(8,128)} fusion(f32[512,4096]{1,0:T(8,128)} %collective-permute-done.2, f32[1024,4096]{1,0:T(8,128)} %copy-done, s32[]{:T(128)S(6)} %select_n.175), kind=kLoop, calls=%fused_computation.8 | loop fusion | flops 2097152 | bytes 25165828 | tf_op jit(solution)/shard_map/add | solution.py:147
  65.6 6.4 %fusion.13 = (f32[512,2048]{1,0:T(8,128)S(1)}, f32[512,2048]{1,0:T(8,128)}) fusion(f32[512,4096]{1,0:T(8,128)} %dynamic-slice_add_fusion), kind=kLoop, calls=%fused_computation.38 | loop fusion | bytes 16777216 | tf_op jit(solution)/shard_map/slice | solution.py:58
  79.2 20.7 %collective-permute-done.3 = f32[64,2048]{1,0:T(8,128)S(1)} collective-permute-done((f32[64,2048]{1,0:T(8,128)S(1)}, f32[64,2048]{1,0:T(8,128)S(1)}, u32[]{:S(2)}, u32[]{:S(2)}) %collective-permute-start.3) | collective-permute-done | bytes 524320 | tf_op jit(solution)/shard_map/ppermute | solution.py:62
  106.1 20.5 %collective-permute-done.4 = f32[64,2048]{1,0:T(8,128)S(1)} collective-permute-done((f32[64,2048]{1,0:T(8,128)S(1)}, f32[64,2048]{1,0:T(8,128)S(1)}, u32[]{:S(2)}, u32[]{:S(2)}) %collective-permute-start.4) | collective-permute-done | bytes 524320 | tf_op jit(solution)/shard_map/ppermute | solution.py:62
  132.7 20.4 %collective-permute-done.5 = f32[64,2048]{1,0:T(8,128)S(1)} collective-permute-done((f32[64,2048]{1,0:T(8,128)S(1)}, f32[64,2048]{1,0:T(8,128)S(1)}, u32[]{:S(2)}, u32[]{:S(2)}) %collective-permute-start.5) | collective-permute-done | bytes 524320 | tf_op jit(solution)/shard_map/ppermute | solution.py:62
  159.2 20.3 %collective-permute-done.6 = f32[64,2048]{1,0:T(8,128)S(1)} collective-permute-done((f32[64,2048]{1,0:T(8,128)S(1)}, f32[64,2048]{1,0:T(8,128)S(1)}, u32[]{:S(2)}, u32[]{:S(2)}) %collective-permute-start.6) | collective-permute-done | bytes 524320 | tf_op jit(solution)/shard_map/ppermute | solution.py:62
  185.5 20.1 %collective-permute-done.7 = f32[64,2048]{1,0:T(8,128)S(1)} collective-permute-done((f32[64,2048]{1,0:T(8,128)S(1)}, f32[64,2048]{1,0:T(8,128)S(1)}, u32[]{:S(2)}, u32[]{:S(2)}) %collective-permute-start.7) | collective-permute-done | bytes 524320 | tf_op jit(solution)/shard_map/ppermute | solution.py:62
  210.8 14.4 %collective-permute-done.8 = f32[64,2048]{1,0:T(8,128)S(1)} collective-permute-done((f32[64,2048]{1,0:T(8,128)S(1)}, f32[64,2048]{1,0:T(8,128)S(1)}, u32[]{:S(2)}, u32[]{:S(2)}) %collective-permute-start.8) | collective-permute-done | bytes 524320 | tf_op jit(solution)/shard_map/ppermute | solution.py:62
  230.2 8.9 %collective-permute-done.9 = f32[64,2048]{1,0:T(8,128)S(1)} collective-permute-done((f32[64,2048]{1,0:T(8,128)S(1)}, f32[64,2048]{1,0:T(8,128)S(1)}, u32[]{:S(2)}, u32[]{:S(2)}) %collective-permute-start.9) | collective-permute-done | bytes 524320 | tf_op jit(solution)/shard_map/ppermute | solution.py:62
  242.3 21.5 %fusion.15 = (bf16[448,1024]{1,0:T(8,128)(2,1)}, f32[448,1024]{1,0:T(8,128)}) fusion(bf16[1024,14336]{1,0:T(8,128)(2,1)} %all-gather.3.cloned.1.call-done, bf16[1792,14336]{1,0:T(8,128)(2,1)} %param.9), kind=kOutput, calls=%fused_computation.40 | convolution fusion | flops 13153796096 | bytes 44957696 | tf_op jit(solution)/shard_map/dot_general | solution.py:123
  265.5 22.2 %fusion.16 = (bf16[448,1024]{1,0:T(8,128)(2,1)}, f32[448,1024]{1,0:T(8,128)}) fusion(bf16[1024,14336]{1,0:T(8,128)(2,1)} %all-gather.3.cloned.1.call-done, bf16[1792,14336]{1,0:T(8,128)(2,1)} %param.9), kind=kOutput, calls=%fused_computation.41 | convolution fusion | flops 13153796096 | bytes 44957696 | tf_op jit(solution)/shard_map/dot_general | solution.py:123
  288.1 21.4 %fusion.17 = (bf16[448,1024]{1,0:T(8,128)(2,1)}, f32[448,1024]{1,0:T(8,128)}) fusion(bf16[1024,14336]{1,0:T(8,128)(2,1)} %all-gather.3.cloned.1.call-done, bf16[1792,14336]{1,0:T(8,128)(2,1)} %param.9), kind=kOutput, calls=%fused_computation.42 | convolution fusion | flops 13153796096 | bytes 44957696 | tf_op jit(solution)/shard_map/dot_general | solution.py:123
  311.1 20.8 %fusion.18 = (bf16[448,1024]{1,0:T(8,128)(2,1)}, f32[448,1024]{1,0:T(8,128)S(1)}) fusion(bf16[1024,14336]{1,0:T(8,128)(2,1)} %all-gather.3.cloned.1.call-done, bf16[1792,14336]{1,0:T(8,128)(2,1)} %param.9), kind=kOutput, calls=%fused_computation.43 | convolution fusion | flops 13153796096 | bytes 44957696 | tf_op jit(solution)/shard_map/dot_general | solution.py:123
  333.1 2.0 add_convert_fusion.3.at_ref
  335.2 12.7 %shard_map.73.rest_0_ = f32[1792,4096]{1,0:T(8,128)} custom-call(bf16[448,1024]{1,0:T(8,128)(2,1)S(1)} %add_convert_fusion.3.at_ref, bf16[1024,4096]{1,0:T(8,128)(2,1)} %all-gather.5.cloned.1.call-done.g_ref, f32[1792,4096]{1,0:T(8,128)} %corr_ref.7), custom_call_target="tpu_custom_call" | custom-call | flops 3763601408 | bytes 23986176 | tf_op jit(solution)/shard_map/pallas_call | solution.py:93
  349.4 12.5 %shard_map.74.rest_0_ = f32[1792,4096]{1,0:T(8,128)} custom-call(bf16[448,1024]{1,0:T(8,128)(2,1)S(1)} %add_convert_fusion.2.at_ref, bf16[1024,4096]{1,0:T(8,128)(2,1)} %all-gather.5.cloned.1.call-done.g_ref, f32[1792,4096]{1,0:T(8,128)} %corr_ref.7, f32[1792,4096]{1,0:T(8,128)} %shard_map.73.rest_0_), custom_call_target="tpu_custom_call", output_to_operand_aliasing={{}: (3, {})} | custom-call | flops 3763601408 | bytes 23986176 | tf_op jit(solution)/shard_map/pallas_call | solution.py:93
  363.4 12.4 %shard_map.75.rest_0_ = f32[1792,4096]{1,0:T(8,128)} custom-call(bf16[448,1024]{1,0:T(8,128)(2,1)S(1)} %add_convert_fusion.1.at_ref, bf16[1024,4096]{1,0:T(8,128)(2,1)} %all-gather.5.cloned.1.call-done.g_ref, f32[1792,4096]{1,0:T(8,128)} %corr_ref.7, f32[1792,4096]{1,0:T(8,128)} %shard_map.74.rest_0_), custom_call_target="tpu_custom_call", output_to_operand_aliasing={{}: (3, {})} | custom-call | flops 3763601408 | bytes 23986176 | tf_op jit(solution)/shard_map/pallas_call | solution.py:93
  377.2 12.4 %shard_map.76 = f32[1792,4096]{1,0:T(8,128)} custom-call(bf16[448,1024]{1,0:T(8,128)(2,1)S(1)} %add_convert_fusion.at_ref, bf16[1024,4096]{1,0:T(8,128)(2,1)} %all-gather.5.cloned.1.call-done.g_ref, f32[1792,4096]{1,0:T(8,128)} %corr_ref.7, f32[1792,4096]{1,0:T(8,128)} %shard_map.75.rest_0_), custom_call_target="tpu_custom_call", output_to_operand_aliasing={{}: (3, {})} | custom-call | flops 3763601408 | bytes 23986176 | tf_op jit(solution)/shard_map/pallas_call | solution.py:93
  (72 shorter events, 49.3 us)
Async XLA Ops:
  6.5 235.7 %all-gather.3.cloned.1.call-start = ((), (), s32[]{:S(2)}) async-start(), calls=%async_computation | async-start | bytes 31195136 | tf_op jit(solution)/shard_map/all_gather | solution.py:118
  7.3 328.0 %all-gather.5.cloned.1.call-start = ((), (), s32[]{:S(2)}) async-start(), calls=%async_computation.1 | async-start | bytes 8912896 | tf_op jit(solution)/shard_map/all_gather | solution.py:149
  7.3 15.2 %collective-permute-start.1 = (bf16[512,512]{1,0:T(8,128)(2,1)}, bf16[512,512]{1,0:T(8,128)(2,1)S(1)}, u32[]{:S(2)}, u32[]{:S(2)}) collective-permute-start(bf16[512,512]{1,0:T(8,128)(2,1)} %param.8), channel_id=1, source_target_pairs={{0,1},{1,0},{2,3},{3,2},{4,5},{5,4},{6,7},{7,6},{8,9},{9,8},{10,11... | collective-permute-start | bytes 1572872 | tf_op jit(solution)/shard_map/ppermute | solution.py:132
  30.0 18.5 %copy-start.5 = (s32[8]{0:T(128)S(1)}, s32[8]{0:T(128)}, u32[]{:S(2)}) copy-start(s32[8]{0:T(128)} %constant.177.clone) | copy-start | bytes 100
  38.7 15.5 %collective-permute-start.2 = (f32[512,4096]{1,0:T(8,128)}, f32[512,4096]{1,0:T(8,128)}, u32[]{:S(2)}, u32[]{:S(2)}) collective-permute-start(f32[512,4096]{1,0:T(8,128)} %constant_dynamic-slice_fusion.2), channel_id=1, source_target_pairs={{0,2},{2,0},{1,3},{3,1},{4,6},{6,4},{5,7},{7,5},{8,10},{10,8},{9,1... | collective-permute-start | bytes 25165832 | tf_op jit(solution)/shard_map/ppermute | solution.py:147
  74.1 25.8 %collective-permute-start.3 = (f32[64,2048]{1,0:T(8,128)S(1)}, f32[64,2048]{1,0:T(8,128)S(1)}, u32[]{:S(2)}, u32[]{:S(2)}) collective-permute-start(f32[64,2048]{1,0:T(8,128)S(1)} %constant_dynamic-slice_fusion.1), channel_id=1, source_target_pairs={{0,8},{8,16},{16,24},{24,28},{28,20},{20,12},{12,4},{4,0},{1,9},{9... | collective-permute-start | bytes 1572872 | tf_op jit(solution)/shard_map/ppermute | solution.py:62
  77.6 25.8 %collective-permute-start.10 = (f32[64,2048]{1,0:T(8,128)S(1)}, f32[64,2048]{1,0:T(8,128)S(1)}, u32[]{:S(2)}, u32[]{:S(2)}) collective-permute-start(f32[64,2048]{1,0:T(8,128)S(1)} %constant_dynamic-slice_fusion), channel_id=1, source_target_pairs={{0,4},{8,0},{16,8},{24,16},{28,24},{20,28},{12,20},{4,12},{1,5},{9... | collective-permute-start | bytes 1572872 | tf_op jit(solution)/shard_map/ppermute | solution.py:63
  101.0 25.6 %collective-permute-start.4 = (f32[64,2048]{1,0:T(8,128)S(1)}, f32[64,2048]{1,0:T(8,128)S(1)}, u32[]{:S(2)}, u32[]{:S(2)}) collective-permute-start(f32[64,2048]{1,0:T(8,128)S(1)} %dynamic-slice_add_fusion.12), channel_id=1, source_target_pairs={{0,8},{8,16},{16,24},{24,28},{28,20},{20,12},{12,4},{4,0},{1,9},{9... | collective-permute-start | bytes 1572872 | tf_op jit(solution)/shard_map/ppermute | solution.py:62
  104.5 25.6 %collective-permute-start.11 = (f32[64,2048]{1,0:T(8,128)S(1)}, f32[64,2048]{1,0:T(8,128)S(1)}, u32[]{:S(2)}, u32[]{:S(2)}) collective-permute-start(f32[64,2048]{1,0:T(8,128)S(1)} %dynamic-slice_add_fusion.6), channel_id=1, source_target_pairs={{0,4},{8,0},{16,8},{24,16},{28,24},{20,28},{12,20},{4,12},{1,5},{9... | collective-permute-start | bytes 1572872 | tf_op jit(solution)/shard_map/ppermute | solution.py:63
  127.7 25.4 %collective-permute-start.5 = (f32[64,2048]{1,0:T(8,128)S(1)}, f32[64,2048]{1,0:T(8,128)S(1)}, u32[]{:S(2)}, u32[]{:S(2)}) collective-permute-start(f32[64,2048]{1,0:T(8,128)S(1)} %dynamic-slice_add_fusion.11), channel_id=1, source_target_pairs={{0,8},{8,16},{16,24},{24,28},{28,20},{20,12},{12,4},{4,0},{1,9},{9... | collective-permute-start | bytes 1572872 | tf_op jit(solution)/shard_map/ppermute | solution.py:62
  131.1 25.4 %collective-permute-start.12 = (f32[64,2048]{1,0:T(8,128)S(1)}, f32[64,2048]{1,0:T(8,128)S(1)}, u32[]{:S(2)}, u32[]{:S(2)}) collective-permute-start(f32[64,2048]{1,0:T(8,128)S(1)} %dynamic-slice_add_fusion.5), channel_id=1, source_target_pairs={{0,4},{8,0},{16,8},{24,16},{28,24},{20,28},{12,20},{4,12},{1,5},{9... | collective-permute-start | bytes 1572872 | tf_op jit(solution)/shard_map/ppermute | solution.py:63
  154.2 25.2 %collective-permute-start.6 = (f32[64,2048]{1,0:T(8,128)S(1)}, f32[64,2048]{1,0:T(8,128)S(1)}, u32[]{:S(2)}, u32[]{:S(2)}) collective-permute-start(f32[64,2048]{1,0:T(8,128)S(1)} %dynamic-slice_add_fusion.10), channel_id=1, source_target_pairs={{0,8},{8,16},{16,24},{24,28},{28,20},{20,12},{12,4},{4,0},{1,9},{9... | collective-permute-start | bytes 1572872 | tf_op jit(solution)/shard_map/ppermute | solution.py:62
  157.6 25.1 %collective-permute-start.13 = (f32[64,2048]{1,0:T(8,128)S(1)}, f32[64,2048]{1,0:T(8,128)S(1)}, u32[]{:S(2)}, u32[]{:S(2)}) collective-permute-start(f32[64,2048]{1,0:T(8,128)S(1)} %dynamic-slice_add_fusion.4), channel_id=1, source_target_pairs={{0,4},{8,0},{16,8},{24,16},{28,24},{20,28},{12,20},{4,12},{1,5},{9... | collective-permute-start | bytes 1572872 | tf_op jit(solution)/shard_map/ppermute | solution.py:63
  180.6 25.0 %collective-permute-start.7 = (f32[64,2048]{1,0:T(8,128)S(1)}, f32[64,2048]{1,0:T(8,128)S(1)}, u32[]{:S(2)}, u32[]{:S(2)}) collective-permute-start(f32[64,2048]{1,0:T(8,128)S(1)} %dynamic-slice_add_fusion.9), channel_id=1, source_target_pairs={{0,8},{8,16},{16,24},{24,28},{28,20},{20,12},{12,4},{4,0},{1,9},{9... | collective-permute-start | bytes 1572872 | tf_op jit(solution)/shard_map/ppermute | solution.py:62
  183.8 24.9 %collective-permute-start.14 = (f32[64,2048]{1,0:T(8,128)S(1)}, f32[64,2048]{1,0:T(8,128)S(1)}, u32[]{:S(2)}, u32[]{:S(2)}) collective-permute-start(f32[64,2048]{1,0:T(8,128)S(1)} %dynamic-slice_add_fusion.3), channel_id=1, source_target_pairs={{0,4},{8,0},{16,8},{24,16},{28,24},{20,28},{12,20},{4,12},{1,5},{9... | collective-permute-start | bytes 1572872 | tf_op jit(solution)/shard_map/ppermute | solution.py:63
  206.7 18.5 %collective-permute-start.8 = (f32[64,2048]{1,0:T(8,128)S(1)}, f32[64,2048]{1,0:T(8,128)S(1)}, u32[]{:S(2)}, u32[]{:S(2)}) collective-permute-start(f32[64,2048]{1,0:T(8,128)S(1)} %dynamic-slice_add_fusion.8), channel_id=1, source_target_pairs={{0,8},{8,16},{16,24},{24,28},{28,20},{20,12},{12,4},{4,0},{1,9},{9... | collective-permute-start | bytes 1572872 | tf_op jit(solution)/shard_map/ppermute | solution.py:62
  209.9 16.9 %collective-permute-start.15 = (f32[64,2048]{1,0:T(8,128)S(1)}, f32[64,2048]{1,0:T(8,128)S(1)}, u32[]{:S(2)}, u32[]{:S(2)}) collective-permute-start(f32[64,2048]{1,0:T(8,128)S(1)} %dynamic-slice_add_fusion.2), channel_id=1, source_target_pairs={{0,4},{8,0},{16,8},{24,16},{28,24},{20,28},{12,20},{4,12},{1,5},{9... | collective-permute-start | bytes 1572872 | tf_op jit(solution)/shard_map/ppermute | solution.py:63
  226.3 12.8 %collective-permute-start.9 = (f32[64,2048]{1,0:T(8,128)S(1)}, f32[64,2048]{1,0:T(8,128)S(1)}, u32[]{:S(2)}, u32[]{:S(2)}) collective-permute-start(f32[64,2048]{1,0:T(8,128)S(1)} %dynamic-slice_add_fusion.7), channel_id=1, source_target_pairs={{0,8},{8,16},{16,24},{24,28},{28,20},{20,12},{12,4},{4,0},{1,9},{9... | collective-permute-start | bytes 1572872 | tf_op jit(solution)/shard_map/ppermute | solution.py:62
  227.8 12.5 %collective-permute-start.16 = (f32[64,2048]{1,0:T(8,128)S(1)}, f32[64,2048]{1,0:T(8,128)S(1)}, u32[]{:S(2)}, u32[]{:S(2)}) collective-permute-start(f32[64,2048]{1,0:T(8,128)S(1)} %dynamic-slice_add_fusion.1), channel_id=1, source_target_pairs={{0,4},{8,0},{16,8},{24,16},{28,24},{20,28},{12,20},{4,12},{1,5},{9... | collective-permute-start | bytes 1572872 | tf_op jit(solution)/shard_map/ppermute | solution.py:63
  263.8 68.4 %collective-permute-start = (bf16[448,1024]{1,0:T(8,128)(2,1)}, bf16[448,1024]{1,0:T(8,128)(2,1)S(1)}, u32[]{:S(2)}, u32[]{:S(2)}) collective-permute-start(bf16[448,1024]{1,0:T(8,128)(2,1)} %get-tuple-element.35), channel_id=1, source_target_pairs={{0,1},{1,0},{2,3},{3,2},{4,5},{5,4},{6,7},{7,6},{8,9},{9,8},{10,11... | collective-permute-start | bytes 2752520 | tf_op jit(solution)/shard_map/ppermute | solution.py:129
  287.7 60.2 %collective-permute-start.17 = (bf16[448,1024]{1,0:T(8,128)(2,1)}, bf16[448,1024]{1,0:T(8,128)(2,1)}, u32[]{:S(2)}, u32[]{:S(2)}) collective-permute-start(bf16[448,1024]{1,0:T(8,128)(2,1)} %get-tuple-element.37), channel_id=1, source_target_pairs={{0,1},{1,0},{2,3},{3,2},{4,5},{5,4},{6,7},{7,6},{8,9},{9,8},{10,11... | collective-permute-start | bytes 2752520 | tf_op jit(solution)/shard_map/ppermute | solution.py:129
  309.4 52.5 %collective-permute-start.18 = (bf16[448,1024]{1,0:T(8,128)(2,1)}, bf16[448,1024]{1,0:T(8,128)(2,1)}, u32[]{:S(2)}, u32[]{:S(2)}) collective-permute-start(bf16[448,1024]{1,0:T(8,128)(2,1)} %get-tuple-element.39), channel_id=1, source_target_pairs={{0,1},{1,0},{2,3},{3,2},{4,5},{5,4},{6,7},{7,6},{8,9},{9,8},{10,11... | collective-permute-start | bytes 2752520 | tf_op jit(solution)/shard_map/ppermute | solution.py:129
  331.8 43.9 %collective-permute-start.19 = (bf16[448,1024]{1,0:T(8,128)(2,1)}, bf16[448,1024]{1,0:T(8,128)(2,1)}, u32[]{:S(2)}, u32[]{:S(2)}) collective-permute-start(bf16[448,1024]{1,0:T(8,128)(2,1)} %get-tuple-element.41), channel_id=1, source_target_pairs={{0,1},{1,0},{2,3},{3,2},{4,5},{5,4},{6,7},{7,6},{8,9},{9,8},{10,11... | collective-permute-start | bytes 2752520 | tf_op jit(solution)/shard_map/ppermute | solution.py:129
  335.2 12.7 %copy-start.3 = (f32[448,1024]{1,0:T(8,128)S(1)}, f32[448,1024]{1,0:T(8,128)}, u32[]{:S(2)}) copy-start(f32[448,1024]{1,0:T(8,128)} %get-tuple-element.38) | copy-start | bytes 5505028
  (5 other events, 32.8 us)
Sparse Core Ops, SparseCore 0:
  8.9 213.2 all-gather.2
  242.4 75.4 all-gather.4

commit v9 on v7

--- a/solution.py
+++ b/solution.py
@@ -74,15 +74,15 @@
     out_ref[...] = corr_ref[...] + total * (1.0 / (SEQS * SEQ_LEN))
 
 
-def correction(at, g, corr, piece, prev=None, tm=512):
+def correction(at, g, corr, row0, tk, prev=None):
     kp, t = at.shape
     m = g.shape[1]
-    tm = min(tm, m)
     seg = t // SEQS
+    first = row0 // tk
     in_specs = [
-        pl.BlockSpec((kp, t), lambda j: (0, 0)),
-        pl.BlockSpec((t, tm), lambda j: (0, j)),
-        pl.BlockSpec((kp, tm), lambda j: (piece, j)),
+        pl.BlockSpec((tk, t), lambda i: (i, 0)),
+        pl.BlockSpec((t, m), lambda i: (0, 0)),
+        pl.BlockSpec((tk, m), lambda i: (first + i, 0)),
     ]
     args = [at, g, corr]
     aliases = {}
@@ -93,11 +93,11 @@
     return pl.pallas_call(
         functools.partial(correction_kernel, seg),
         out_shape=jax.ShapeDtypeStruct(corr.shape, jnp.float32),
-        grid=(m // tm,),
+        grid=(kp // tk,),
         in_specs=in_specs,
-        out_specs=pl.BlockSpec((kp, tm), lambda j: (piece, j)),
+        out_specs=pl.BlockSpec((tk, m), lambda i: (first + i, 0)),
         input_output_aliases=aliases,
-        compiler_params=pltpu.CompilerParams(vmem_limit_bytes=48 * 1024 * 1024),
+        compiler_params=pltpu.CompilerParams(vmem_limit_bytes=56 * 1024 * 1024),
         cost_estimate=pl.CostEstimate(
             flops=2 * kp * t * m + 3 * kp * m,
             transcendentals=0,
@@ -107,6 +107,7 @@
 
 
 def local(ring, acts, grads, basis_in, basis_out, corr):
+    assert K_PIECES == 2
     n_chip = lax.axis_size("rchip")
     n_row = n_chip * 2
     n_col = lax.axis_size("col")
@@ -117,11 +118,12 @@
 
     gathered = lax.all_gather(acts, ROW, axis=0, tiled=True)
     k_rows = basis_in.shape[0]
-    kp = k_rows // K_PIECES
+    tk = k_rows // 14
+    bounds = [0, 9 * tk, k_rows]
     parts, recvs = [], []
     for i in range(K_PIECES):
         part = lax.dot_general(
-            basis_in[i * kp:(i + 1) * kp], gathered, (((1,), (1,)), ((), ())),
+            basis_in[bounds[i]:bounds[i + 1]], gathered, (((1,), (1,)), ((), ())),
             preferred_element_type=jnp.float32,
         )
         parts.append(part)
@@ -157,7 +159,7 @@
             act_t = (parts[i] + recv.astype(jnp.float32)).astype(jnp.bfloat16)
         else:
             act_t = lax.psum(parts[i], "col").astype(jnp.bfloat16)
-        out = correction(act_t, grad_rot, corr, i, out)
+        out = correction(act_t, grad_rot, corr, bounds[i], tk, out)
     return out
 
 

time: 386 us -> 391 us (1.013)
  waiting for transfers between devices: 162 us -> 171 us
    ppermute x2, waiting for transfers between devices: 18.9 us -> 26.9 us  [local(): recvs.append(lax.ppermute(part.astype(jnp.bfloat16), 'col', swap_perm(2)))]
  transfers between devices with their start and end apart: 20 -> 20, of which waited for: 17 -> 16; matrix products, arithmetic and copies ran while one was open for 32% -> 31% of each run, Pallas kernels for 5% -> 6%
where the time goes in v9:
time: 391 us; the launch traced here: 390 us
  waiting for transfers between devices  171 us (44%)
  matrix products  73.8 us (19%)
  Pallas kernels  37 us (9%)
  other arithmetic  35.7 us (9%)
  between operations  31.6 us (8%)
  starting transfers between devices  21.1 us (5%)
  local copies, waits for them, and re-layouts  19.6 us (5%)
    ppermute x7, waiting for transfers between devices, ring_reduce_scatter(): buf_a = lax.ppermute(buf_a, axis, right) + block(xa, p - 1 - s + 2 * n)  125 us
    dot_general x2, matrix products, local(): lax.dot_general(basis_in[bounds[i]:bounds[i + 1]], gathered, (((1,), (1,)...  67.5 us
    pallas_call x2, Pallas kernels, correction(): pl.pallas_call(functools.partial(correction_kernel, seg), out_shape=jax.S...  37 us
    ppermute x2, waiting for transfers between devices, local(): recvs.append(lax.ppermute(part.astype(jnp.bfloat16), 'col', swap_perm(2)))  26.9 us
    ppermute x1, waiting for transfers between devices, local(): other = lax.ppermute(grads, 'col', swap_perm(2))  12.1 us
    ppermute x7, starting transfers between devices, ring_reduce_scatter(): buf_a = lax.ppermute(buf_a, axis, right) + block(xa, p - 1 - s + 2 * n)  12 us
    add x1, other arithmetic, local(): summed = keep + lax.ppermute(send, 'core', swap_perm(2))  11.4 us
  transfers between devices with their start and end apart: 20, of which 16 were waited for; matrix products, arithmetic and copies ran while one was open for 31% of the time, Pallas kernels for 6%

profile of v9, /device:TPU:0, one launch (start us, length us, event | category | flops | bytes accessed | tf_op | source)
XLA Modules:
  0.0 389.7 jit_solution(11360266841428643442)
XLA Ops:
  7.3 3.0 collective-permute-start.1
  10.3 12.1 %collective-permute-done.1 = bf16[512,512]{1,0:T(8,128)(2,1)S(1)} collective-permute-done((bf16[512,512]{1,0:T(8,128)(2,1)}, bf16[512,512]{1,0:T(8,128)(2,1)S(1)}, u32[]{:S(2)}, u32[]{:S(2)}) %collective-permute-start.1) | collective-permute-done | bytes 524320 | tf_op jit(solution)/shard_map/ppermute | solution.py:134
  23.6 6.4 %fusion.4 = f32[1024,4096]{1,0:T(8,128)S(1)} fusion(bf16[4096,512]{1,0:T(8,128)(2,1)} %param.10, bf16[512,512]{1,0:T(8,128)(2,1)S(1)} %get-tuple-element.12, bf16[512,512]{1,0:T(8,128)(2,1)S(1)} %get-tuple-element.11), kind=kOutput, calls=%fused_computation.7 | convolution fusion | flops 4297064448 | bytes 22020096 | tf_op jit(solution)/shard_map/dot_general | solution.py:142
  30.0 4.1 %constant_dynamic-slice_fusion.2 = f32[512,4096]{1,0:T(8,128)} fusion(f32[1024,4096]{1,0:T(8,128)S(1)} %fusion.4, s32[]{:T(128)S(6)} %select_n.176), kind=kLoop, calls=%fused_computation.30 | loop fusion | bytes 16777220 | tf_op jit(solution)/shard_map/dynamic_slice | solution.py:148
  34.1 4.6 %copy-done = f32[1024,4096]{1,0:T(8,128)} copy-done((f32[1024,4096]{1,0:T(8,128)}, f32[1024,4096]{1,0:T(8,128)S(1)}, u32[]{:S(2)}) %copy-start) | copy-done | bytes 16777240
  49.9 4.2 %collective-permute-done.2 = f32[512,4096]{1,0:T(8,128)} collective-permute-done((f32[512,4096]{1,0:T(8,128)}, f32[512,4096]{1,0:T(8,128)}, u32[]{:S(2)}, u32[]{:S(2)}) %collective-permute-start.2) | collective-permute-done | bytes 8388640 | tf_op jit(solution)/shard_map/ppermute | solution.py:149
  54.2 11.4 %dynamic-slice_add_fusion = f32[512,4096]{1,0:T(8,128)} fusion(f32[512,4096]{1,0:T(8,128)} %collective-permute-done.2, f32[1024,4096]{1,0:T(8,128)} %copy-done, s32[]{:T(128)S(6)} %select_n.175), kind=kLoop, calls=%fused_computation.4 | loop fusion | flops 2097152 | bytes 25165828 | tf_op jit(solution)/shard_map/add | solution.py:149
  65.6 6.4 %fusion.9 = (f32[512,2048]{1,0:T(8,128)S(1)}, f32[512,2048]{1,0:T(8,128)}) fusion(f32[512,4096]{1,0:T(8,128)} %dynamic-slice_add_fusion), kind=kLoop, calls=%fused_computation.32 | loop fusion | bytes 16777216 | tf_op jit(solution)/shard_map/slice | solution.py:58
  79.2 20.7 %collective-permute-done.3 = f32[64,2048]{1,0:T(8,128)S(1)} collective-permute-done((f32[64,2048]{1,0:T(8,128)S(1)}, f32[64,2048]{1,0:T(8,128)S(1)}, u32[]{:S(2)}, u32[]{:S(2)}) %collective-permute-start.3) | collective-permute-done | bytes 524320 | tf_op jit(solution)/shard_map/ppermute | solution.py:62
  106.0 20.6 %collective-permute-done.4 = f32[64,2048]{1,0:T(8,128)S(1)} collective-permute-done((f32[64,2048]{1,0:T(8,128)S(1)}, f32[64,2048]{1,0:T(8,128)S(1)}, u32[]{:S(2)}, u32[]{:S(2)}) %collective-permute-start.4) | collective-permute-done | bytes 524320 | tf_op jit(solution)/shard_map/ppermute | solution.py:62
  132.7 20.4 %collective-permute-done.5 = f32[64,2048]{1,0:T(8,128)S(1)} collective-permute-done((f32[64,2048]{1,0:T(8,128)S(1)}, f32[64,2048]{1,0:T(8,128)S(1)}, u32[]{:S(2)}, u32[]{:S(2)}) %collective-permute-start.5) | collective-permute-done | bytes 524320 | tf_op jit(solution)/shard_map/ppermute | solution.py:62
  154.2 2.0 collective-permute-start.6
  159.2 20.3 %collective-permute-done.6 = f32[64,2048]{1,0:T(8,128)S(1)} collective-permute-done((f32[64,2048]{1,0:T(8,128)S(1)}, f32[64,2048]{1,0:T(8,128)S(1)}, u32[]{:S(2)}, u32[]{:S(2)}) %collective-permute-start.6) | collective-permute-done | bytes 524320 | tf_op jit(solution)/shard_map/ppermute | solution.py:62
  180.5 2.0 collective-permute-start.7
  185.5 20.1 %collective-permute-done.7 = f32[64,2048]{1,0:T(8,128)S(1)} collective-permute-done((f32[64,2048]{1,0:T(8,128)S(1)}, f32[64,2048]{1,0:T(8,128)S(1)}, u32[]{:S(2)}, u32[]{:S(2)}) %collective-permute-start.7) | collective-permute-done | bytes 524320 | tf_op jit(solution)/shard_map/ppermute | solution.py:62
  210.8 14.5 %collective-permute-done.8 = f32[64,2048]{1,0:T(8,128)S(1)} collective-permute-done((f32[64,2048]{1,0:T(8,128)S(1)}, f32[64,2048]{1,0:T(8,128)S(1)}, u32[]{:S(2)}, u32[]{:S(2)}) %collective-permute-start.8) | collective-permute-done | bytes 524320 | tf_op jit(solution)/shard_map/ppermute | solution.py:62
  230.4 8.7 %collective-permute-done.9 = f32[64,2048]{1,0:T(8,128)S(1)} collective-permute-done((f32[64,2048]{1,0:T(8,128)S(1)}, f32[64,2048]{1,0:T(8,128)S(1)}, u32[]{:S(2)}, u32[]{:S(2)}) %collective-permute-start.9) | collective-permute-done | bytes 524320 | tf_op jit(solution)/shard_map/ppermute | solution.py:62
  242.5 42.0 %fusion.11 = (bf16[1152,1024]{1,0:T(8,128)(2,1)}, f32[1152,1024]{1,0:T(8,128)S(1)}) fusion(bf16[1024,14336]{1,0:T(8,128)(2,1)} %all-gather.3.cloned.1.call-done, bf16[1792,14336]{1,0:T(8,128)(2,1)} %param.9), kind=kOutput, calls=%fused_computation.34 | convolution fusion | flops 33824047104 | bytes 69468160 | tf_op jit(solution)/shard_map/dot_general | solution.py:125
  286.1 25.5 %fusion.12 = (bf16[640,1024]{1,0:T(8,128)(2,1)}, f32[640,1024]{1,0:T(8,128)S(1)}) fusion(bf16[1024,14336]{1,0:T(8,128)(2,1)} %all-gather.3.cloned.1.call-done, bf16[1792,14336]{1,0:T(8,128)(2,1)} %param.9), kind=kOutput, calls=%fused_computation.35 | convolution fusion | flops 18791137280 | bytes 51642368 | tf_op jit(solution)/shard_map/dot_general | solution.py:125
  312.0 26.9 %collective-permute-done = bf16[1152,1024]{1,0:T(8,128)(2,1)} collective-permute-done((bf16[1152,1024]{1,0:T(8,128)(2,1)}, bf16[1152,1024]{1,0:T(8,128)(2,1)}, u32[]{:S(2)}, u32[]{:S(2)}) %collective-permute-start) | collective-permute-done | bytes 2359328 | tf_op jit(solution)/shard_map/ppermute | solution.py:131
  338.9 4.1 %add_convert_fusion.at_ref = bf16[1152,1024]{1,0:T(8,128)(2,1)} fusion(f32[1152,1024]{1,0:T(8,128)S(1)} %get-tuple-element.28, bf16[1152,1024]{1,0:T(8,128)(2,1)} %collective-permute-done), kind=kLoop, calls=%fused_computation.5 | loop fusion | flops 3538944 | bytes 9437184 | tf_op jit(solution)/shard_map/convert_element_type | solution.py:159
  342.9 22.4 %shard_map.73.rest_0_ = f32[1792,4096]{1,0:T(8,128)} custom-call(bf16[1152,1024]{1,0:T(8,128)(2,1)} %add_convert_fusion.at_ref, bf16[1024,4096]{1,0:T(8,128)(2,1)} %all-gather.5.cloned.1.call-done.g_ref, f32[1792,4096]{1,0:T(8,128)} %corr_ref.3), custom_call_target="tpu_custom_call" | custom-call | flops 9677832192 | bytes 48496640 | tf_op jit(solution)/shard_map/pallas_call | solution.py:93
  365.4 2.9 add_convert_fusion.1.at_ref
  368.2 14.6 %shard_map.74 = f32[1792,4096]{1,0:T(8,128)} custom-call(bf16[640,1024]{1,0:T(8,128)(2,1)} %add_convert_fusion.1.at_ref, bf16[1024,4096]{1,0:T(8,128)(2,1)} %all-gather.5.cloned.1.call-done.g_ref, f32[1792,4096]{1,0:T(8,128)} %corr_ref.3, f32[1792,4096]{1,0:T(8,128)} %shard_map.73.rest_0_), custom_call_target="tpu_custom_call", output_to_operand_aliasing={{}: (3, {})} | custom-call | flops 5376573440 | bytes 30670848 | tf_op jit(solution)/shard_map/pallas_call | solution.py:93
  (56 shorter events, 38.3 us)
Async XLA Ops:
  6.5 235.9 %all-gather.3.cloned.1.call-start = ((), (), s32[]{:S(2)}) async-start(), calls=%async_computation | async-start | bytes 31195136 | tf_op jit(solution)/shard_map/all_gather | solution.py:119
  7.3 335.7 %all-gather.5.cloned.1.call-start = ((), (), s32[]{:S(2)}) async-start(), calls=%async_computation.1 | async-start | bytes 8912896 | tf_op jit(solution)/shard_map/all_gather | solution.py:151
  7.3 15.2 %collective-permute-start.1 = (bf16[512,512]{1,0:T(8,128)(2,1)}, bf16[512,512]{1,0:T(8,128)(2,1)S(1)}, u32[]{:S(2)}, u32[]{:S(2)}) collective-permute-start(bf16[512,512]{1,0:T(8,128)(2,1)} %param.8), channel_id=1, source_target_pairs={{0,1},{1,0},{2,3},{3,2},{4,5},{5,4},{6,7},{7,6},{8,9},{9,8},{10,11... | collective-permute-start | bytes 1572872 | tf_op jit(solution)/shard_map/ppermute | solution.py:134
  30.0 8.7 %copy-start = (f32[1024,4096]{1,0:T(8,128)}, f32[1024,4096]{1,0:T(8,128)S(1)}, u32[]{:S(2)}) copy-start(f32[1024,4096]{1,0:T(8,128)S(1)} %fusion.4) | copy-start | bytes 50331652
  30.0 8.7 %copy-start.3 = (s32[8]{0:T(128)S(1)}, s32[8]{0:T(128)}, u32[]{:S(2)}) copy-start(s32[8]{0:T(128)} %constant.178.clone) | copy-start | bytes 100
  30.0 18.5 %copy-start.2 = (s32[8]{0:T(128)S(1)}, s32[8]{0:T(128)}, u32[]{:S(2)}) copy-start(s32[8]{0:T(128)} %constant.177.clone) | copy-start | bytes 100
  38.7 15.5 %collective-permute-start.2 = (f32[512,4096]{1,0:T(8,128)}, f32[512,4096]{1,0:T(8,128)}, u32[]{:S(2)}, u32[]{:S(2)}) collective-permute-start(f32[512,4096]{1,0:T(8,128)} %constant_dynamic-slice_fusion.2), channel_id=1, source_target_pairs={{0,2},{2,0},{1,3},{3,1},{4,6},{6,4},{5,7},{7,5},{8,10},{10,8},{9,1... | collective-permute-start | bytes 25165832 | tf_op jit(solution)/shard_map/ppermute | solution.py:149
  72.0 2.0 copy-start.1
  74.0 25.8 %collective-permute-start.3 = (f32[64,2048]{1,0:T(8,128)S(1)}, f32[64,2048]{1,0:T(8,128)S(1)}, u32[]{:S(2)}, u32[]{:S(2)}) collective-permute-start(f32[64,2048]{1,0:T(8,128)S(1)} %constant_dynamic-slice_fusion.1), channel_id=1, source_target_pairs={{0,8},{8,16},{16,24},{24,28},{28,20},{20,12},{12,4},{4,0},{1,9},{9... | collective-permute-start | bytes 1572872 | tf_op jit(solution)/shard_map/ppermute | solution.py:62
  77.5 25.8 %collective-permute-start.10 = (f32[64,2048]{1,0:T(8,128)S(1)}, f32[64,2048]{1,0:T(8,128)S(1)}, u32[]{:S(2)}, u32[]{:S(2)}) collective-permute-start(f32[64,2048]{1,0:T(8,128)S(1)} %constant_dynamic-slice_fusion), channel_id=1, source_target_pairs={{0,4},{8,0},{16,8},{24,16},{28,24},{20,28},{12,20},{4,12},{1,5},{9... | collective-permute-start | bytes 1572872 | tf_op jit(solution)/shard_map/ppermute | solution.py:63
  101.0 25.6 %collective-permute-start.4 = (f32[64,2048]{1,0:T(8,128)S(1)}, f32[64,2048]{1,0:T(8,128)S(1)}, u32[]{:S(2)}, u32[]{:S(2)}) collective-permute-start(f32[64,2048]{1,0:T(8,128)S(1)} %dynamic-slice_add_fusion.12), channel_id=1, source_target_pairs={{0,8},{8,16},{16,24},{24,28},{28,20},{20,12},{12,4},{4,0},{1,9},{9... | collective-permute-start | bytes 1572872 | tf_op jit(solution)/shard_map/ppermute | solution.py:62
  104.4 25.6 %collective-permute-start.11 = (f32[64,2048]{1,0:T(8,128)S(1)}, f32[64,2048]{1,0:T(8,128)S(1)}, u32[]{:S(2)}, u32[]{:S(2)}) collective-permute-start(f32[64,2048]{1,0:T(8,128)S(1)} %dynamic-slice_add_fusion.6), channel_id=1, source_target_pairs={{0,4},{8,0},{16,8},{24,16},{28,24},{20,28},{12,20},{4,12},{1,5},{9... | collective-permute-start | bytes 1572872 | tf_op jit(solution)/shard_map/ppermute | solution.py:63
  127.7 25.4 %collective-permute-start.5 = (f32[64,2048]{1,0:T(8,128)S(1)}, f32[64,2048]{1,0:T(8,128)S(1)}, u32[]{:S(2)}, u32[]{:S(2)}) collective-permute-start(f32[64,2048]{1,0:T(8,128)S(1)} %dynamic-slice_add_fusion.11), channel_id=1, source_target_pairs={{0,8},{8,16},{16,24},{24,28},{28,20},{20,12},{12,4},{4,0},{1,9},{9... | collective-permute-start | bytes 1572872 | tf_op jit(solution)/shard_map/ppermute | solution.py:62
  131.1 25.4 %collective-permute-start.12 = (f32[64,2048]{1,0:T(8,128)S(1)}, f32[64,2048]{1,0:T(8,128)S(1)}, u32[]{:S(2)}, u32[]{:S(2)}) collective-permute-start(f32[64,2048]{1,0:T(8,128)S(1)} %dynamic-slice_add_fusion.5), channel_id=1, source_target_pairs={{0,4},{8,0},{16,8},{24,16},{28,24},{20,28},{12,20},{4,12},{1,5},{9... | collective-permute-start | bytes 1572872 | tf_op jit(solution)/shard_map/ppermute | solution.py:63
  154.2 25.2 %collective-permute-start.6 = (f32[64,2048]{1,0:T(8,128)S(1)}, f32[64,2048]{1,0:T(8,128)S(1)}, u32[]{:S(2)}, u32[]{:S(2)}) collective-permute-start(f32[64,2048]{1,0:T(8,128)S(1)} %dynamic-slice_add_fusion.10), channel_id=1, source_target_pairs={{0,8},{8,16},{16,24},{24,28},{28,20},{20,12},{12,4},{4,0},{1,9},{9... | collective-permute-start | bytes 1572872 | tf_op jit(solution)/shard_map/ppermute | solution.py:62
  157.5 25.1 %collective-permute-start.13 = (f32[64,2048]{1,0:T(8,128)S(1)}, f32[64,2048]{1,0:T(8,128)S(1)}, u32[]{:S(2)}, u32[]{:S(2)}) collective-permute-start(f32[64,2048]{1,0:T(8,128)S(1)} %dynamic-slice_add_fusion.4), channel_id=1, source_target_pairs={{0,4},{8,0},{16,8},{24,16},{28,24},{20,28},{12,20},{4,12},{1,5},{9... | collective-permute-start | bytes 1572872 | tf_op jit(solution)/shard_map/ppermute | solution.py:63
  180.5 25.1 %collective-permute-start.7 = (f32[64,2048]{1,0:T(8,128)S(1)}, f32[64,2048]{1,0:T(8,128)S(1)}, u32[]{:S(2)}, u32[]{:S(2)}) collective-permute-start(f32[64,2048]{1,0:T(8,128)S(1)} %dynamic-slice_add_fusion.9), channel_id=1, source_target_pairs={{0,8},{8,16},{16,24},{24,28},{28,20},{20,12},{12,4},{4,0},{1,9},{9... | collective-permute-start | bytes 1572872 | tf_op jit(solution)/shard_map/ppermute | solution.py:62
  183.8 24.9 %collective-permute-start.14 = (f32[64,2048]{1,0:T(8,128)S(1)}, f32[64,2048]{1,0:T(8,128)S(1)}, u32[]{:S(2)}, u32[]{:S(2)}) collective-permute-start(f32[64,2048]{1,0:T(8,128)S(1)} %dynamic-slice_add_fusion.3), channel_id=1, source_target_pairs={{0,4},{8,0},{16,8},{24,16},{28,24},{20,28},{12,20},{4,12},{1,5},{9... | collective-permute-start | bytes 1572872 | tf_op jit(solution)/shard_map/ppermute | solution.py:63
  206.7 18.6 %collective-permute-start.8 = (f32[64,2048]{1,0:T(8,128)S(1)}, f32[64,2048]{1,0:T(8,128)S(1)}, u32[]{:S(2)}, u32[]{:S(2)}) collective-permute-start(f32[64,2048]{1,0:T(8,128)S(1)} %dynamic-slice_add_fusion.8), channel_id=1, source_target_pairs={{0,8},{8,16},{16,24},{24,28},{28,20},{20,12},{12,4},{4,0},{1,9},{9... | collective-permute-start | bytes 1572872 | tf_op jit(solution)/shard_map/ppermute | solution.py:62
  209.8 16.9 %collective-permute-start.15 = (f32[64,2048]{1,0:T(8,128)S(1)}, f32[64,2048]{1,0:T(8,128)S(1)}, u32[]{:S(2)}, u32[]{:S(2)}) collective-permute-start(f32[64,2048]{1,0:T(8,128)S(1)} %dynamic-slice_add_fusion.2), channel_id=1, source_target_pairs={{0,4},{8,0},{16,8},{24,16},{28,24},{20,28},{12,20},{4,12},{1,5},{9... | collective-permute-start | bytes 1572872 | tf_op jit(solution)/shard_map/ppermute | solution.py:63
  226.3 12.8 %collective-permute-start.9 = (f32[64,2048]{1,0:T(8,128)S(1)}, f32[64,2048]{1,0:T(8,128)S(1)}, u32[]{:S(2)}, u32[]{:S(2)}) collective-permute-start(f32[64,2048]{1,0:T(8,128)S(1)} %dynamic-slice_add_fusion.7), channel_id=1, source_target_pairs={{0,8},{8,16},{16,24},{24,28},{28,20},{20,12},{12,4},{4,0},{1,9},{9... | collective-permute-start | bytes 1572872 | tf_op jit(solution)/shard_map/ppermute | solution.py:62
  227.8 12.6 %collective-permute-start.16 = (f32[64,2048]{1,0:T(8,128)S(1)}, f32[64,2048]{1,0:T(8,128)S(1)}, u32[]{:S(2)}, u32[]{:S(2)}) collective-permute-start(f32[64,2048]{1,0:T(8,128)S(1)} %dynamic-slice_add_fusion.1), channel_id=1, source_target_pairs={{0,4},{8,0},{16,8},{24,16},{28,24},{20,28},{12,20},{4,12},{1,5},{9... | collective-permute-start | bytes 1572872 | tf_op jit(solution)/shard_map/ppermute | solution.py:63
  284.4 54.4 %collective-permute-start = (bf16[1152,1024]{1,0:T(8,128)(2,1)}, bf16[1152,1024]{1,0:T(8,128)(2,1)}, u32[]{:S(2)}, u32[]{:S(2)}) collective-permute-start(bf16[1152,1024]{1,0:T(8,128)(2,1)} %get-tuple-element.27), channel_id=1, source_target_pairs={{0,1},{1,0},{2,3},{3,2},{4,5},{5,4},{6,7},{7,6},{8,9},{9,8},{10,11... | collective-permute-start | bytes 7077896 | tf_op jit(solution)/shard_map/ppermute | solution.py:131
  311.6 53.7 %collective-permute-start.17 = (bf16[640,1024]{1,0:T(8,128)(2,1)}, bf16[640,1024]{1,0:T(8,128)(2,1)}, u32[]{:S(2)}, u32[]{:S(2)}) collective-permute-start(bf16[640,1024]{1,0:T(8,128)(2,1)} %get-tuple-element.29), channel_id=1, source_target_pairs={{0,1},{1,0},{2,3},{3,2},{4,5},{5,4},{6,7},{7,6},{8,9},{9,8},{10,11... | collective-permute-start | bytes 3932168 | tf_op jit(solution)/shard_map/ppermute | solution.py:131
Sparse Core Ops, SparseCore 0:
  8.9 213.3 all-gather.2
  242.6 75.4 all-gather.4

commit v10 on v7

--- a/solution.py
+++ b/solution.py
@@ -74,7 +74,7 @@
     out_ref[...] = corr_ref[...] + total * (1.0 / (SEQS * SEQ_LEN))
 
 
-def correction(at, g, corr, piece, prev=None, tm=512):
+def correction(at, g, corr, piece, prev=None, tm=1024):
     kp, t = at.shape
     m = g.shape[1]
     tm = min(tm, m)

time: 386 us -> 384 us (level)
  Pallas kernels: 37.4 us -> 33.3 us
    pallas_call x2, Pallas kernels: 37.4 us -> 33.3 us  [correction(): pl.pallas_call(functools.partial(correction_kernel, seg), out_shape=jax.S...]
  transfers between devices with their start and end apart: 20 -> 20, of which waited for: 17 -> 17; matrix products, arithmetic and copies ran while one was open for 32% -> 32% of each run, Pallas kernels for 5% -> 4%
where the time goes in v10:
time: 384 us; the launch traced here: 382 us
  waiting for transfers between devices  164 us (43%)
  matrix products  76.6 us (20%)
  other arithmetic  34.2 us (9%)
  Pallas kernels  33.3 us (9%)
  between operations  32.4 us (8%)
  starting transfers between devices  20.9 us (5%)
  local copies, waits for them, and re-layouts  20.9 us (5%)
    ppermute x7, waiting for transfers between devices, ring_reduce_scatter(): buf_a = lax.ppermute(buf_a, axis, right) + block(xa, p - 1 - s + 2 * n)  125 us
    dot_general x2, matrix products, local(): lax.dot_general(basis_in[i * kp:(i + 1) * kp], gathered, (((1,), (1,)), (...  70.2 us
    pallas_call x2, Pallas kernels, correction(): pl.pallas_call(functools.partial(correction_kernel, seg), out_shape=jax.S...  33.3 us
    ppermute x2, waiting for transfers between devices, local(): recvs.append(lax.ppermute(part.astype(jnp.bfloat16), 'col', swap_perm(2)))  20.9 us
    ppermute x1, waiting for transfers between devices, local(): other = lax.ppermute(grads, 'col', swap_perm(2))  12.1 us
    ppermute x7, starting transfers between devices, ring_reduce_scatter(): buf_a = lax.ppermute(buf_a, axis, right) + block(xa, p - 1 - s + 2 * n)  12 us
    add x1, other arithmetic, local(): summed = keep + lax.ppermute(send, 'core', swap_perm(2))  11.4 us
    unnamed x12, local copies, waits for them, and re-layouts  7.78 us
  transfers between devices with their start and end apart: 20, of which 17 were waited for; matrix products, arithmetic and copies ran while one was open for 32% of the time, Pallas kernels for 4%

profile of v10, /device:TPU:0, one launch (start us, length us, event | category | flops | bytes accessed | tf_op | source)
XLA Modules:
  0.0 382.4 jit_solution(11127374612140462005)
XLA Ops:
  7.3 3.0 collective-permute-start.1
  10.3 12.1 %collective-permute-done.1 = bf16[512,512]{1,0:T(8,128)(2,1)S(1)} collective-permute-done((bf16[512,512]{1,0:T(8,128)(2,1)}, bf16[512,512]{1,0:T(8,128)(2,1)S(1)}, u32[]{:S(2)}, u32[]{:S(2)}) %collective-permute-start.1) | collective-permute-done | bytes 524320 | tf_op jit(solution)/shard_map/ppermute | solution.py:132
  23.6 6.4 %fusion.4 = f32[1024,4096]{1,0:T(8,128)S(1)} fusion(bf16[4096,512]{1,0:T(8,128)(2,1)} %param.10, bf16[512,512]{1,0:T(8,128)(2,1)S(1)} %get-tuple-element.12, bf16[512,512]{1,0:T(8,128)(2,1)S(1)} %get-tuple-element.11), kind=kOutput, calls=%fused_computation.7 | convolution fusion | flops 4297064448 | bytes 22020096 | tf_op jit(solution)/shard_map/dot_general | solution.py:140
  30.0 4.1 %constant_dynamic-slice_fusion.2 = f32[512,4096]{1,0:T(8,128)} fusion(f32[1024,4096]{1,0:T(8,128)S(1)} %fusion.4, s32[]{:T(128)S(6)} %select_n.176), kind=kLoop, calls=%fused_computation.30 | loop fusion | bytes 16777220 | tf_op jit(solution)/shard_map/dynamic_slice | solution.py:146
  34.1 4.6 %copy-done = f32[1024,4096]{1,0:T(8,128)} copy-done((f32[1024,4096]{1,0:T(8,128)}, f32[1024,4096]{1,0:T(8,128)S(1)}, u32[]{:S(2)}) %copy-start) | copy-done | bytes 16777240
  50.7 3.5 collective-permute-done.2
  54.2 11.4 %dynamic-slice_add_fusion = f32[512,4096]{1,0:T(8,128)} fusion(f32[512,4096]{1,0:T(8,128)} %collective-permute-done.2, f32[1024,4096]{1,0:T(8,128)} %copy-done, s32[]{:T(128)S(6)} %select_n.175), kind=kLoop, calls=%fused_computation.4 | loop fusion | flops 2097152 | bytes 25165828 | tf_op jit(solution)/shard_map/add | solution.py:147
  65.6 6.4 %fusion.9 = (f32[512,2048]{1,0:T(8,128)S(1)}, f32[512,2048]{1,0:T(8,128)}) fusion(f32[512,4096]{1,0:T(8,128)} %dynamic-slice_add_fusion), kind=kLoop, calls=%fused_computation.32 | loop fusion | bytes 16777216 | tf_op jit(solution)/shard_map/slice | solution.py:58
  79.1 20.8 %collective-permute-done.3 = f32[64,2048]{1,0:T(8,128)S(1)} collective-permute-done((f32[64,2048]{1,0:T(8,128)S(1)}, f32[64,2048]{1,0:T(8,128)S(1)}, u32[]{:S(2)}, u32[]{:S(2)}) %collective-permute-start.3) | collective-permute-done | bytes 524320 | tf_op jit(solution)/shard_map/ppermute | solution.py:62
  106.1 20.5 %collective-permute-done.4 = f32[64,2048]{1,0:T(8,128)S(1)} collective-permute-done((f32[64,2048]{1,0:T(8,128)S(1)}, f32[64,2048]{1,0:T(8,128)S(1)}, u32[]{:S(2)}, u32[]{:S(2)}) %collective-permute-start.4) | collective-permute-done | bytes 524320 | tf_op jit(solution)/shard_map/ppermute | solution.py:62
  132.7 20.4 %collective-permute-done.5 = f32[64,2048]{1,0:T(8,128)S(1)} collective-permute-done((f32[64,2048]{1,0:T(8,128)S(1)}, f32[64,2048]{1,0:T(8,128)S(1)}, u32[]{:S(2)}, u32[]{:S(2)}) %collective-permute-start.5) | collective-permute-done | bytes 524320 | tf_op jit(solution)/shard_map/ppermute | solution.py:62
  159.2 20.2 %collective-permute-done.6 = f32[64,2048]{1,0:T(8,128)S(1)} collective-permute-done((f32[64,2048]{1,0:T(8,128)S(1)}, f32[64,2048]{1,0:T(8,128)S(1)}, u32[]{:S(2)}, u32[]{:S(2)}) %collective-permute-start.6) | collective-permute-done | bytes 524320 | tf_op jit(solution)/shard_map/ppermute | solution.py:62
  180.5 2.0 collective-permute-start.7
  185.5 20.1 %collective-permute-done.7 = f32[64,2048]{1,0:T(8,128)S(1)} collective-permute-done((f32[64,2048]{1,0:T(8,128)S(1)}, f32[64,2048]{1,0:T(8,128)S(1)}, u32[]{:S(2)}, u32[]{:S(2)}) %collective-permute-start.7) | collective-permute-done | bytes 524320 | tf_op jit(solution)/shard_map/ppermute | solution.py:62
  210.9 14.3 %collective-permute-done.8 = f32[64,2048]{1,0:T(8,128)S(1)} collective-permute-done((f32[64,2048]{1,0:T(8,128)S(1)}, f32[64,2048]{1,0:T(8,128)S(1)}, u32[]{:S(2)}, u32[]{:S(2)}) %collective-permute-start.8) | collective-permute-done | bytes 524320 | tf_op jit(solution)/shard_map/ppermute | solution.py:62
  230.4 8.7 %collective-permute-done.9 = f32[64,2048]{1,0:T(8,128)S(1)} collective-permute-done((f32[64,2048]{1,0:T(8,128)S(1)}, f32[64,2048]{1,0:T(8,128)S(1)}, u32[]{:S(2)}, u32[]{:S(2)}) %collective-permute-start.9) | collective-permute-done | bytes 524320 | tf_op jit(solution)/shard_map/ppermute | solution.py:62
  242.4 35.0 %fusion.11 = (bf16[896,1024]{1,0:T(8,128)(2,1)}, f32[896,1024]{1,0:T(8,128)}) fusion(bf16[1024,14336]{1,0:T(8,128)(2,1)} %all-gather.3.cloned.1.call-done, bf16[1792,14336]{1,0:T(8,128)(2,1)} %param.9), kind=kOutput, calls=%fused_computation.34 | convolution fusion | flops 26307592192 | bytes 60555264 | tf_op jit(solution)/shard_map/dot_general | solution.py:123
  279.1 35.2 %fusion.12 = (bf16[896,1024]{1,0:T(8,128)(2,1)}, f32[896,1024]{1,0:T(8,128)}) fusion(bf16[1024,14336]{1,0:T(8,128)(2,1)} %all-gather.3.cloned.1.call-done, bf16[1792,14336]{1,0:T(8,128)(2,1)} %param.9), kind=kOutput, calls=%fused_computation.35 | convolution fusion | flops 26307592192 | bytes 60555264 | tf_op jit(solution)/shard_map/dot_general | solution.py:123
  314.6 5.1 %collective-permute-done = bf16[896,1024]{1,0:T(8,128)(2,1)S(1)} collective-permute-done((bf16[896,1024]{1,0:T(8,128)(2,1)}, bf16[896,1024]{1,0:T(8,128)(2,1)S(1)}, u32[]{:S(2)}, u32[]{:S(2)}) %collective-permute-start) | collective-permute-done | bytes 1835040 | tf_op jit(solution)/shard_map/ppermute | solution.py:129
  320.9 3.3 add_convert_fusion.1.at_ref
  324.3 16.7 %shard_map.73.rest_0_ = f32[1792,4096]{1,0:T(8,128)} custom-call(bf16[896,1024]{1,0:T(8,128)(2,1)S(1)} %add_convert_fusion.1.at_ref, bf16[1024,4096]{1,0:T(8,128)(2,1)} %all-gather.5.cloned.1.call-done.g_ref, f32[1792,4096]{1,0:T(8,128)} %corr_ref.3), custom_call_target="tpu_custom_call" | custom-call | flops 7527202816 | bytes 39583744 | tf_op jit(solution)/shard_map/pallas_call | solution.py:93
  341.0 15.7 %collective-permute-done.17 = bf16[896,1024]{1,0:T(8,128)(2,1)} collective-permute-done((bf16[896,1024]{1,0:T(8,128)(2,1)}, bf16[896,1024]{1,0:T(8,128)(2,1)}, u32[]{:S(2)}, u32[]{:S(2)}) %collective-permute-start.17) | collective-permute-done | bytes 1835040 | tf_op jit(solution)/shard_map/ppermute | solution.py:129
  356.7 2.2 add_convert_fusion.at_ref
  358.9 16.6 %shard_map.74 = f32[1792,4096]{1,0:T(8,128)} custom-call(bf16[896,1024]{1,0:T(8,128)(2,1)S(1)} %add_convert_fusion.at_ref, bf16[1024,4096]{1,0:T(8,128)(2,1)} %all-gather.5.cloned.1.call-done.g_ref, f32[1792,4096]{1,0:T(8,128)} %corr_ref.3, f32[1792,4096]{1,0:T(8,128)} %shard_map.73.rest_0_), custom_call_target="tpu_custom_call", output_to_operand_aliasing={{}: (3, {})} | custom-call | flops 7527202816 | bytes 39583744 | tf_op jit(solution)/shard_map/pallas_call | solution.py:93
  (60 shorter events, 41.7 us)
Async XLA Ops:
  6.5 235.9 %all-gather.3.cloned.1.call-start = ((), (), s32[]{:S(2)}) async-start(), calls=%async_computation | async-start | bytes 31195136 | tf_op jit(solution)/shard_map/all_gather | solution.py:118
  7.3 317.0 %all-gather.5.cloned.1.call-start = ((), (), s32[]{:S(2)}) async-start(), calls=%async_computation.1 | async-start | bytes 8912896 | tf_op jit(solution)/shard_map/all_gather | solution.py:149
  7.3 15.2 %collective-permute-start.1 = (bf16[512,512]{1,0:T(8,128)(2,1)}, bf16[512,512]{1,0:T(8,128)(2,1)S(1)}, u32[]{:S(2)}, u32[]{:S(2)}) collective-permute-start(bf16[512,512]{1,0:T(8,128)(2,1)} %param.8), channel_id=1, source_target_pairs={{0,1},{1,0},{2,3},{3,2},{4,5},{5,4},{6,7},{7,6},{8,9},{9,8},{10,11... | collective-permute-start | bytes 1572872 | tf_op jit(solution)/shard_map/ppermute | solution.py:132
  30.0 8.7 %copy-start = (f32[1024,4096]{1,0:T(8,128)}, f32[1024,4096]{1,0:T(8,128)S(1)}, u32[]{:S(2)}) copy-start(f32[1024,4096]{1,0:T(8,128)S(1)} %fusion.4) | copy-start | bytes 50331652
  30.0 8.7 %copy-start.5 = (s32[8]{0:T(128)S(1)}, s32[8]{0:T(128)}, u32[]{:S(2)}) copy-start(s32[8]{0:T(128)} %constant.178.clone) | copy-start | bytes 100
  30.0 19.3 %copy-start.4 = (s32[8]{0:T(128)S(1)}, s32[8]{0:T(128)}, u32[]{:S(2)}) copy-start(s32[8]{0:T(128)} %constant.177.clone) | copy-start | bytes 100
  38.7 15.5 %collective-permute-start.2 = (f32[512,4096]{1,0:T(8,128)}, f32[512,4096]{1,0:T(8,128)}, u32[]{:S(2)}, u32[]{:S(2)}) collective-permute-start(f32[512,4096]{1,0:T(8,128)} %constant_dynamic-slice_fusion.2), channel_id=1, source_target_pairs={{0,2},{2,0},{1,3},{3,1},{4,6},{6,4},{5,7},{7,5},{8,10},{10,8},{9,1... | collective-permute-start | bytes 25165832 | tf_op jit(solution)/shard_map/ppermute | solution.py:147
  74.0 25.8 %collective-permute-start.3 = (f32[64,2048]{1,0:T(8,128)S(1)}, f32[64,2048]{1,0:T(8,128)S(1)}, u32[]{:S(2)}, u32[]{:S(2)}) collective-permute-start(f32[64,2048]{1,0:T(8,128)S(1)} %constant_dynamic-slice_fusion.1), channel_id=1, source_target_pairs={{0,8},{8,16},{16,24},{24,28},{28,20},{20,12},{12,4},{4,0},{1,9},{9... | collective-permute-start | bytes 1572872 | tf_op jit(solution)/shard_map/ppermute | solution.py:62
  77.6 25.8 %collective-permute-start.10 = (f32[64,2048]{1,0:T(8,128)S(1)}, f32[64,2048]{1,0:T(8,128)S(1)}, u32[]{:S(2)}, u32[]{:S(2)}) collective-permute-start(f32[64,2048]{1,0:T(8,128)S(1)} %constant_dynamic-slice_fusion), channel_id=1, source_target_pairs={{0,4},{8,0},{16,8},{24,16},{28,24},{20,28},{12,20},{4,12},{1,5},{9... | collective-permute-start | bytes 1572872 | tf_op jit(solution)/shard_map/ppermute | solution.py:63
  101.0 25.6 %collective-permute-start.4 = (f32[64,2048]{1,0:T(8,128)S(1)}, f32[64,2048]{1,0:T(8,128)S(1)}, u32[]{:S(2)}, u32[]{:S(2)}) collective-permute-start(f32[64,2048]{1,0:T(8,128)S(1)} %dynamic-slice_add_fusion.12), channel_id=1, source_target_pairs={{0,8},{8,16},{16,24},{24,28},{28,20},{20,12},{12,4},{4,0},{1,9},{9... | collective-permute-start | bytes 1572872 | tf_op jit(solution)/shard_map/ppermute | solution.py:62
  104.5 25.6 %collective-permute-start.11 = (f32[64,2048]{1,0:T(8,128)S(1)}, f32[64,2048]{1,0:T(8,128)S(1)}, u32[]{:S(2)}, u32[]{:S(2)}) collective-permute-start(f32[64,2048]{1,0:T(8,128)S(1)} %dynamic-slice_add_fusion.6), channel_id=1, source_target_pairs={{0,4},{8,0},{16,8},{24,16},{28,24},{20,28},{12,20},{4,12},{1,5},{9... | collective-permute-start | bytes 1572872 | tf_op jit(solution)/shard_map/ppermute | solution.py:63
  127.7 25.4 %collective-permute-start.5 = (f32[64,2048]{1,0:T(8,128)S(1)}, f32[64,2048]{1,0:T(8,128)S(1)}, u32[]{:S(2)}, u32[]{:S(2)}) collective-permute-start(f32[64,2048]{1,0:T(8,128)S(1)} %dynamic-slice_add_fusion.11), channel_id=1, source_target_pairs={{0,8},{8,16},{16,24},{24,28},{28,20},{20,12},{12,4},{4,0},{1,9},{9... | collective-permute-start | bytes 1572872 | tf_op jit(solution)/shard_map/ppermute | solution.py:62
  131.1 25.4 %collective-permute-start.12 = (f32[64,2048]{1,0:T(8,128)S(1)}, f32[64,2048]{1,0:T(8,128)S(1)}, u32[]{:S(2)}, u32[]{:S(2)}) collective-permute-start(f32[64,2048]{1,0:T(8,128)S(1)} %dynamic-slice_add_fusion.5), channel_id=1, source_target_pairs={{0,4},{8,0},{16,8},{24,16},{28,24},{20,28},{12,20},{4,12},{1,5},{9... | collective-permute-start | bytes 1572872 | tf_op jit(solution)/shard_map/ppermute | solution.py:63
  154.2 25.2 %collective-permute-start.6 = (f32[64,2048]{1,0:T(8,128)S(1)}, f32[64,2048]{1,0:T(8,128)S(1)}, u32[]{:S(2)}, u32[]{:S(2)}) collective-permute-start(f32[64,2048]{1,0:T(8,128)S(1)} %dynamic-slice_add_fusion.10), channel_id=1, source_target_pairs={{0,8},{8,16},{16,24},{24,28},{28,20},{20,12},{12,4},{4,0},{1,9},{9... | collective-permute-start | bytes 1572872 | tf_op jit(solution)/shard_map/ppermute | solution.py:62
  157.6 25.1 %collective-permute-start.13 = (f32[64,2048]{1,0:T(8,128)S(1)}, f32[64,2048]{1,0:T(8,128)S(1)}, u32[]{:S(2)}, u32[]{:S(2)}) collective-permute-start(f32[64,2048]{1,0:T(8,128)S(1)} %dynamic-slice_add_fusion.4), channel_id=1, source_target_pairs={{0,4},{8,0},{16,8},{24,16},{28,24},{20,28},{12,20},{4,12},{1,5},{9... | collective-permute-start | bytes 1572872 | tf_op jit(solution)/shard_map/ppermute | solution.py:63
  180.5 25.0 %collective-permute-start.7 = (f32[64,2048]{1,0:T(8,128)S(1)}, f32[64,2048]{1,0:T(8,128)S(1)}, u32[]{:S(2)}, u32[]{:S(2)}) collective-permute-start(f32[64,2048]{1,0:T(8,128)S(1)} %dynamic-slice_add_fusion.9), channel_id=1, source_target_pairs={{0,8},{8,16},{16,24},{24,28},{28,20},{20,12},{12,4},{4,0},{1,9},{9... | collective-permute-start | bytes 1572872 | tf_op jit(solution)/shard_map/ppermute | solution.py:62
  183.8 24.9 %collective-permute-start.14 = (f32[64,2048]{1,0:T(8,128)S(1)}, f32[64,2048]{1,0:T(8,128)S(1)}, u32[]{:S(2)}, u32[]{:S(2)}) collective-permute-start(f32[64,2048]{1,0:T(8,128)S(1)} %dynamic-slice_add_fusion.3), channel_id=1, source_target_pairs={{0,4},{8,0},{16,8},{24,16},{28,24},{20,28},{12,20},{4,12},{1,5},{9... | collective-permute-start | bytes 1572872 | tf_op jit(solution)/shard_map/ppermute | solution.py:63
  206.7 18.6 %collective-permute-start.8 = (f32[64,2048]{1,0:T(8,128)S(1)}, f32[64,2048]{1,0:T(8,128)S(1)}, u32[]{:S(2)}, u32[]{:S(2)}) collective-permute-start(f32[64,2048]{1,0:T(8,128)S(1)} %dynamic-slice_add_fusion.8), channel_id=1, source_target_pairs={{0,8},{8,16},{16,24},{24,28},{28,20},{20,12},{12,4},{4,0},{1,9},{9... | collective-permute-start | bytes 1572872 | tf_op jit(solution)/shard_map/ppermute | solution.py:62
  209.9 16.9 %collective-permute-start.15 = (f32[64,2048]{1,0:T(8,128)S(1)}, f32[64,2048]{1,0:T(8,128)S(1)}, u32[]{:S(2)}, u32[]{:S(2)}) collective-permute-start(f32[64,2048]{1,0:T(8,128)S(1)} %dynamic-slice_add_fusion.2), channel_id=1, source_target_pairs={{0,4},{8,0},{16,8},{24,16},{28,24},{20,28},{12,20},{4,12},{1,5},{9... | collective-permute-start | bytes 1572872 | tf_op jit(solution)/shard_map/ppermute | solution.py:63
  226.3 12.8 %collective-permute-start.9 = (f32[64,2048]{1,0:T(8,128)S(1)}, f32[64,2048]{1,0:T(8,128)S(1)}, u32[]{:S(2)}, u32[]{:S(2)}) collective-permute-start(f32[64,2048]{1,0:T(8,128)S(1)} %dynamic-slice_add_fusion.7), channel_id=1, source_target_pairs={{0,8},{8,16},{16,24},{24,28},{28,20},{20,12},{12,4},{4,0},{1,9},{9... | collective-permute-start | bytes 1572872 | tf_op jit(solution)/shard_map/ppermute | solution.py:62
  227.8 12.6 %collective-permute-start.16 = (f32[64,2048]{1,0:T(8,128)S(1)}, f32[64,2048]{1,0:T(8,128)S(1)}, u32[]{:S(2)}, u32[]{:S(2)}) collective-permute-start(f32[64,2048]{1,0:T(8,128)S(1)} %dynamic-slice_add_fusion.1), channel_id=1, source_target_pairs={{0,4},{8,0},{16,8},{24,16},{28,24},{20,28},{12,20},{4,12},{1,5},{9... | collective-permute-start | bytes 1572872 | tf_op jit(solution)/shard_map/ppermute | solution.py:63
  277.4 42.3 %collective-permute-start = (bf16[896,1024]{1,0:T(8,128)(2,1)}, bf16[896,1024]{1,0:T(8,128)(2,1)S(1)}, u32[]{:S(2)}, u32[]{:S(2)}) collective-permute-start(bf16[896,1024]{1,0:T(8,128)(2,1)} %get-tuple-element.27), channel_id=1, source_target_pairs={{0,1},{1,0},{2,3},{3,2},{4,5},{5,4},{6,7},{7,6},{8,9},{9,8},{10,11... | collective-permute-start | bytes 5505032 | tf_op jit(solution)/shard_map/ppermute | solution.py:129
  314.3 42.4 %collective-permute-start.17 = (bf16[896,1024]{1,0:T(8,128)(2,1)}, bf16[896,1024]{1,0:T(8,128)(2,1)}, u32[]{:S(2)}, u32[]{:S(2)}) collective-permute-start(bf16[896,1024]{1,0:T(8,128)(2,1)} %get-tuple-element.29), channel_id=1, source_target_pairs={{0,1},{1,0},{2,3},{3,2},{4,5},{5,4},{6,7},{7,6},{8,9},{9,8},{10,11... | collective-permute-start | bytes 5505032 | tf_op jit(solution)/shard_map/ppermute | solution.py:129
  324.3 32.5 %copy-start.2 = (f32[896,1024]{1,0:T(8,128)S(1)}, f32[896,1024]{1,0:T(8,128)}, u32[]{:S(2)}) copy-start(f32[896,1024]{1,0:T(8,128)} %get-tuple-element.30) | copy-start | bytes 11010052
  (2 other events, 3.2 us)
Sparse Core Ops, SparseCore 0:
  8.9 213.3 all-gather.2
  242.5 75.4 all-gather.4

commit v11 on v10

--- a/solution.py
+++ b/solution.py
@@ -137,14 +137,15 @@
     per_seq = n_row // SEQS
     g_all = g_all.reshape(SEQS, per_seq, CHUNKS, half, g_all.shape[1]).transpose(0, 2, 1, 3, 4)
     g_all = g_all.reshape(tokens, grads.shape[1])
-    g_part = lax.dot_general(
-        g_all, basis_out, (((1,), (1,)), ((), ())), preferred_element_type=jnp.float32
-    )
     core = lax.axis_index("core")
     pair = tokens // 2
-    keep = lax.dynamic_slice_in_dim(g_part, core * pair, pair, axis=0)
-    send = lax.dynamic_slice_in_dim(g_part, (1 - core) * pair, pair, axis=0)
-    summed = keep + lax.ppermute(send, "core", swap_perm(2))
+    dims = (((1,), (1,)), ((), ()))
+    send_rows = lax.dynamic_slice_in_dim(g_all, (1 - core) * pair, pair, axis=0)
+    send = lax.dot_general(send_rows, basis_out, dims, preferred_element_type=jnp.float32)
+    received = lax.ppermute(send, "core", swap_perm(2))
+    keep_rows = lax.dynamic_slice_in_dim(g_all, core * pair, pair, axis=0)
+    keep = lax.dot_general(keep_rows, basis_out, dims, preferred_element_type=jnp.float32)
+    summed = keep + received
     share = ring_reduce_scatter(summed, ring, "rchip")
     grad_rot = lax.all_gather(share.astype(jnp.bfloat16), ("core", "rchip"), axis=0, tiled=True)
 

time: 384 us -> 382 us (level)
  waiting for transfers between devices: 164 us -> 178 us
  local copies, waits for them, and re-layouts: 20.9 us -> 8.51 us
  other arithmetic: 34.2 us -> 22.7 us
  matrix products: 76.6 us -> 86.5 us
    ppermute x7, waiting for transfers between devices: 125 us -> 137 us  [ring_reduce_scatter(): buf_a = lax.ppermute(buf_a, axis, right) + block(xa, p - 1 - s + 2 * n)]
    add x1 -> x0, other arithmetic: 11.4 us -> none  [local(): summed = keep + lax.ppermute(send, 'core', swap_perm(2))]
    dot_general x1 -> x2, matrix products: 6.39 us -> 15.9 us  [the longest x1 8.32 us: local(): lax.dot_general(send_rows, basis_out, dims, preferred_element_type=jnp.fl...]
    unnamed x12 -> x10, local copies, waits for them, and re-layouts: 7.78 us -> 3.2 us
    dynamic_slice x1 -> x0, local copies, waits for them, and re-layouts: 4.11 us -> none  [local(): send = lax.dynamic_slice_in_dim(g_part, (1 - core) * pair, pair, axis=0)]
  transfers between devices with their start and end apart: 20 -> 20, of which waited for: 17 -> 16; matrix products, arithmetic and copies ran while one was open for 32% -> 30% of each run, Pallas kernels for 4% -> 4%
where the time goes in v11:
time: 382 us; the launch traced here: 380 us
  waiting for transfers between devices  178 us (47%)
  matrix products  86.5 us (23%)
  Pallas kernels  33.3 us (9%)
  between operations  31.3 us (8%)
  other arithmetic  22.7 us (6%)
  starting transfers between devices  20.3 us (5%)
  local copies, waits for them, and re-layouts  8.51 us (2%)
    ppermute x7, waiting for transfers between devices, ring_reduce_scatter(): buf_a = lax.ppermute(buf_a, axis, right) + block(xa, p - 1 - s + 2 * n)  137 us
    dot_general x2, matrix products, local(): lax.dot_general(basis_in[i * kp:(i + 1) * kp], gathered, (((1,), (1,)), (...  70.5 us
    pallas_call x2, Pallas kernels, correction(): pl.pallas_call(functools.partial(correction_kernel, seg), out_shape=jax.S...  33.3 us
    ppermute x2, waiting for transfers between devices, local(): recvs.append(lax.ppermute(part.astype(jnp.bfloat16), 'col', swap_perm(2)))  21.4 us
    ppermute x1, waiting for transfers between devices, local(): other = lax.ppermute(grads, 'col', swap_perm(2))  12.1 us
    ppermute x7, starting transfers between devices, ring_reduce_scatter(): buf_a = lax.ppermute(buf_a, axis, right) + block(xa, p - 1 - s + 2 * n)  12 us
    dot_general x1, matrix products, local(): lax.dot_general(send_rows, basis_out, dims, preferred_element_type=jnp.fl...  8.32 us
  transfers between devices with their start and end apart: 20, of which 16 were waited for; matrix products, arithmetic and copies ran while one was open for 30% of the time, Pallas kernels for 4%

profile of v11, /device:TPU:0, one launch (start us, length us, event | category | flops | bytes accessed | tf_op | source)
XLA Modules:
  0.0 380.4 jit_solution(2071559733476119735)
XLA Ops:
  7.3 3.0 collective-permute-start.1
  10.3 12.1 %collective-permute-done.1 = bf16[512,512]{1,0:T(8,128)(2,1)S(1)} collective-permute-done((bf16[512,512]{1,0:T(8,128)(2,1)}, bf16[512,512]{1,0:T(8,128)(2,1)S(1)}, u32[]{:S(2)}, u32[]{:S(2)}) %collective-permute-start.1) | collective-permute-done | bytes 524320 | tf_op jit(solution)/shard_map/ppermute | solution.py:132
  23.6 8.3 %fusion.5 = f32[512,4096]{1,0:T(8,128)} fusion(bf16[4096,512]{1,0:T(8,128)(2,1)} %param.10, s32[]{:T(128)S(6)} %select_n.176, bf16[512,512]{1,0:T(8,128)(2,1)S(1)} %get-tuple-element.12, bf16[512,512]{1,0:T(8,128)(2,1)S(1)} %get-tuple-element.11), kind=kOutput, calls=%fused_computation.12 | convolution fusion | flops 2148532224 | bytes 13631492 | tf_op jit(solution)/shard_map/dot_general | solution.py:144
  42.8 4.6 %collective-permute-done.2 = f32[512,4096]{1,0:T(8,128)} collective-permute-done((f32[512,4096]{1,0:T(8,128)}, f32[512,4096]{1,0:T(8,128)}, u32[]{:S(2)}, u32[]{:S(2)}) %collective-permute-start.2) | collective-permute-done | bytes 8388640 | tf_op jit(solution)/shard_map/ppermute | solution.py:145
  47.4 7.6 %convolution_add_fusion = f32[512,4096]{1,0:T(8,128)S(1)} fusion(f32[512,4096]{1,0:T(8,128)} %collective-permute-done.2, bf16[4096,512]{1,0:T(8,128)(2,1)} %param.10, s32[]{:T(128)S(6)} %select_n.175, bf16[512,512]{1,0:T(8,128)(2,1)S(1)} %get-tuple-element.12, bf16[512,512]{1,0:T(8,128)(2,1)S(1)} %get-tuple-element.11), kind=kOutput, calls=%fused_computation.4 | convolution fusion | flops 2150629376 | bytes 22020100 | tf_op jit(solution)/shard_map/dot_general | solution.py:147
  55.0 2.9 fusion.13
  57.9 2.0 copy-done
  59.9 1.9 collective-permute-start.3
  65.0 20.7 %collective-permute-done.3 = f32[64,2048]{1,0:T(8,128)S(1)} collective-permute-done((f32[64,2048]{1,0:T(8,128)S(1)}, f32[64,2048]{1,0:T(8,128)S(1)}, u32[]{:S(2)}, u32[]{:S(2)}) %collective-permute-start.3) | collective-permute-done | bytes 524320 | tf_op jit(solution)/shard_map/ppermute | solution.py:62
  86.9 1.8 collective-permute-start.4
  92.0 20.7 %collective-permute-done.4 = f32[64,2048]{1,0:T(8,128)S(1)} collective-permute-done((f32[64,2048]{1,0:T(8,128)S(1)}, f32[64,2048]{1,0:T(8,128)S(1)}, u32[]{:S(2)}, u32[]{:S(2)}) %collective-permute-start.4) | collective-permute-done | bytes 524320 | tf_op jit(solution)/shard_map/ppermute | solution.py:62
  118.7 20.5 %collective-permute-done.5 = f32[64,2048]{1,0:T(8,128)S(1)} collective-permute-done((f32[64,2048]{1,0:T(8,128)S(1)}, f32[64,2048]{1,0:T(8,128)S(1)}, u32[]{:S(2)}, u32[]{:S(2)}) %collective-permute-start.5) | collective-permute-done | bytes 524320 | tf_op jit(solution)/shard_map/ppermute | solution.py:62
  145.1 20.5 %collective-permute-done.6 = f32[64,2048]{1,0:T(8,128)S(1)} collective-permute-done((f32[64,2048]{1,0:T(8,128)S(1)}, f32[64,2048]{1,0:T(8,128)S(1)}, u32[]{:S(2)}, u32[]{:S(2)}) %collective-permute-start.6) | collective-permute-done | bytes 524320 | tf_op jit(solution)/shard_map/ppermute | solution.py:62
  171.4 20.4 %collective-permute-done.7 = f32[64,2048]{1,0:T(8,128)S(1)} collective-permute-done((f32[64,2048]{1,0:T(8,128)S(1)}, f32[64,2048]{1,0:T(8,128)S(1)}, u32[]{:S(2)}, u32[]{:S(2)}) %collective-permute-start.7) | collective-permute-done | bytes 524320 | tf_op jit(solution)/shard_map/ppermute | solution.py:62
  197.0 20.8 %collective-permute-done.8 = f32[64,2048]{1,0:T(8,128)S(1)} collective-permute-done((f32[64,2048]{1,0:T(8,128)S(1)}, f32[64,2048]{1,0:T(8,128)S(1)}, u32[]{:S(2)}, u32[]{:S(2)}) %collective-permute-start.8) | collective-permute-done | bytes 524320 | tf_op jit(solution)/shard_map/ppermute | solution.py:62
  223.0 13.4 %collective-permute-done.9 = f32[64,2048]{1,0:T(8,128)S(1)} collective-permute-done((f32[64,2048]{1,0:T(8,128)S(1)}, f32[64,2048]{1,0:T(8,128)S(1)}, u32[]{:S(2)}, u32[]{:S(2)}) %collective-permute-start.9) | collective-permute-done | bytes 524320 | tf_op jit(solution)/shard_map/ppermute | solution.py:62
  239.5 35.5 %fusion.15 = (bf16[896,1024]{1,0:T(8,128)(2,1)}, f32[896,1024]{1,0:T(8,128)}) fusion(bf16[1024,14336]{1,0:T(8,128)(2,1)} %all-gather.3.cloned.1.call-done, bf16[1792,14336]{1,0:T(8,128)(2,1)} %param.9), kind=kOutput, calls=%fused_computation.39 | convolution fusion | flops 26307592192 | bytes 60555264 | tf_op jit(solution)/shard_map/dot_general | solution.py:123
  276.5 35.1 %fusion.16 = (bf16[896,1024]{1,0:T(8,128)(2,1)}, f32[896,1024]{1,0:T(8,128)}) fusion(bf16[1024,14336]{1,0:T(8,128)(2,1)} %all-gather.3.cloned.1.call-done, bf16[1792,14336]{1,0:T(8,128)(2,1)} %param.9), kind=kOutput, calls=%fused_computation.40 | convolution fusion | flops 26307592192 | bytes 60555264 | tf_op jit(solution)/shard_map/dot_general | solution.py:123
  312.1 6.0 %collective-permute-done = bf16[896,1024]{1,0:T(8,128)(2,1)S(1)} collective-permute-done((bf16[896,1024]{1,0:T(8,128)(2,1)}, bf16[896,1024]{1,0:T(8,128)(2,1)S(1)}, u32[]{:S(2)}, u32[]{:S(2)}) %collective-permute-start) | collective-permute-done | bytes 1835040 | tf_op jit(solution)/shard_map/ppermute | solution.py:129
  319.3 3.3 add_convert_fusion.1.at_ref
  322.7 16.7 %shard_map.73.rest_0_ = f32[1792,4096]{1,0:T(8,128)} custom-call(bf16[896,1024]{1,0:T(8,128)(2,1)S(1)} %add_convert_fusion.1.at_ref, bf16[1024,4096]{1,0:T(8,128)(2,1)} %all-gather.5.cloned.1.call-done.g_ref, f32[1792,4096]{1,0:T(8,128)} %corr_ref.3), custom_call_target="tpu_custom_call" | custom-call | flops 7527202816 | bytes 39583744 | tf_op jit(solution)/shard_map/pallas_call | solution.py:93
  339.4 15.4 %collective-permute-done.17 = bf16[896,1024]{1,0:T(8,128)(2,1)} collective-permute-done((bf16[896,1024]{1,0:T(8,128)(2,1)}, bf16[896,1024]{1,0:T(8,128)(2,1)}, u32[]{:S(2)}, u32[]{:S(2)}) %collective-permute-start.17) | collective-permute-done | bytes 1835040 | tf_op jit(solution)/shard_map/ppermute | solution.py:129
  354.8 2.2 add_convert_fusion.at_ref
  357.0 16.6 %shard_map.74 = f32[1792,4096]{1,0:T(8,128)} custom-call(bf16[896,1024]{1,0:T(8,128)(2,1)S(1)} %add_convert_fusion.at_ref, bf16[1024,4096]{1,0:T(8,128)(2,1)} %all-gather.5.cloned.1.call-done.g_ref, f32[1792,4096]{1,0:T(8,128)} %corr_ref.3, f32[1792,4096]{1,0:T(8,128)} %shard_map.73.rest_0_), custom_call_target="tpu_custom_call", output_to_operand_aliasing={{}: (3, {})} | custom-call | flops 7527202816 | bytes 39583744 | tf_op jit(solution)/shard_map/pallas_call | solution.py:93
  (57 shorter events, 37.0 us)
Async XLA Ops:
  6.5 233.0 %all-gather.3.cloned.1.call-start = ((), (), s32[]{:S(2)}) async-start(), calls=%async_computation | async-start | bytes 31195136 | tf_op jit(solution)/shard_map/all_gather | solution.py:118
  7.3 315.4 %all-gather.5.cloned.1.call-start = ((), (), s32[]{:S(2)}) async-start(), calls=%async_computation.1 | async-start | bytes 8912896 | tf_op jit(solution)/shard_map/all_gather | solution.py:150
  7.3 15.2 %collective-permute-start.1 = (bf16[512,512]{1,0:T(8,128)(2,1)}, bf16[512,512]{1,0:T(8,128)(2,1)S(1)}, u32[]{:S(2)}, u32[]{:S(2)}) collective-permute-start(bf16[512,512]{1,0:T(8,128)(2,1)} %param.8), channel_id=1, source_target_pairs={{0,1},{1,0},{2,3},{3,2},{4,5},{5,4},{6,7},{7,6},{8,9},{9,8},{10,11... | collective-permute-start | bytes 1572872 | tf_op jit(solution)/shard_map/ppermute | solution.py:132
  23.6 8.3 %copy-start.4 = (s32[8]{0:T(128)S(1)}, s32[8]{0:T(128)}, u32[]{:S(2)}) copy-start(s32[8]{0:T(128)} %constant.178.clone) | copy-start | bytes 100
  23.6 17.9 %copy-start.3 = (s32[8]{0:T(128)S(1)}, s32[8]{0:T(128)}, u32[]{:S(2)}) copy-start(s32[8]{0:T(128)} %constant.177.clone) | copy-start | bytes 100
  31.9 15.5 %collective-permute-start.2 = (f32[512,4096]{1,0:T(8,128)}, f32[512,4096]{1,0:T(8,128)}, u32[]{:S(2)}, u32[]{:S(2)}) collective-permute-start(f32[512,4096]{1,0:T(8,128)} %fusion.5), channel_id=1, source_target_pairs={{0,2},{2,0},{1,3},{3,1},{4,6},{6,4},{5,7},{7,5},{8,10},{10,8},{9,1... | collective-permute-start | bytes 25165832 | tf_op jit(solution)/shard_map/ppermute | solution.py:145
  57.9 2.0 copy-start
  59.9 25.9 %collective-permute-start.3 = (f32[64,2048]{1,0:T(8,128)S(1)}, f32[64,2048]{1,0:T(8,128)S(1)}, u32[]{:S(2)}, u32[]{:S(2)}) collective-permute-start(f32[64,2048]{1,0:T(8,128)S(1)} %constant_dynamic-slice_fusion.1), channel_id=1, source_target_pairs={{0,8},{8,16},{16,24},{24,28},{28,20},{20,12},{12,4},{4,0},{1,9},{9... | collective-permute-start | bytes 1572872 | tf_op jit(solution)/shard_map/ppermute | solution.py:62
  63.5 25.8 %collective-permute-start.10 = (f32[64,2048]{1,0:T(8,128)S(1)}, f32[64,2048]{1,0:T(8,128)S(1)}, u32[]{:S(2)}, u32[]{:S(2)}) collective-permute-start(f32[64,2048]{1,0:T(8,128)S(1)} %constant_dynamic-slice_fusion), channel_id=1, source_target_pairs={{0,4},{8,0},{16,8},{24,16},{28,24},{20,28},{12,20},{4,12},{1,5},{9... | collective-permute-start | bytes 1572872 | tf_op jit(solution)/shard_map/ppermute | solution.py:63
  86.9 25.7 %collective-permute-start.4 = (f32[64,2048]{1,0:T(8,128)S(1)}, f32[64,2048]{1,0:T(8,128)S(1)}, u32[]{:S(2)}, u32[]{:S(2)}) collective-permute-start(f32[64,2048]{1,0:T(8,128)S(1)} %dynamic-slice_add_fusion.11), channel_id=1, source_target_pairs={{0,8},{8,16},{16,24},{24,28},{28,20},{20,12},{12,4},{4,0},{1,9},{9... | collective-permute-start | bytes 1572872 | tf_op jit(solution)/shard_map/ppermute | solution.py:62
  90.4 25.6 %collective-permute-start.11 = (f32[64,2048]{1,0:T(8,128)S(1)}, f32[64,2048]{1,0:T(8,128)S(1)}, u32[]{:S(2)}, u32[]{:S(2)}) collective-permute-start(f32[64,2048]{1,0:T(8,128)S(1)} %dynamic-slice_add_fusion.5), channel_id=1, source_target_pairs={{0,4},{8,0},{16,8},{24,16},{28,24},{20,28},{12,20},{4,12},{1,5},{9... | collective-permute-start | bytes 1572872 | tf_op jit(solution)/shard_map/ppermute | solution.py:63
  113.7 25.5 %collective-permute-start.5 = (f32[64,2048]{1,0:T(8,128)S(1)}, f32[64,2048]{1,0:T(8,128)S(1)}, u32[]{:S(2)}, u32[]{:S(2)}) collective-permute-start(f32[64,2048]{1,0:T(8,128)S(1)} %dynamic-slice_add_fusion.10), channel_id=1, source_target_pairs={{0,8},{8,16},{16,24},{24,28},{28,20},{20,12},{12,4},{4,0},{1,9},{9... | collective-permute-start | bytes 1572872 | tf_op jit(solution)/shard_map/ppermute | solution.py:62
  117.0 25.3 %collective-permute-start.12 = (f32[64,2048]{1,0:T(8,128)S(1)}, f32[64,2048]{1,0:T(8,128)S(1)}, u32[]{:S(2)}, u32[]{:S(2)}) collective-permute-start(f32[64,2048]{1,0:T(8,128)S(1)} %dynamic-slice_add_fusion.4), channel_id=1, source_target_pairs={{0,4},{8,0},{16,8},{24,16},{28,24},{20,28},{12,20},{4,12},{1,5},{9... | collective-permute-start | bytes 1572872 | tf_op jit(solution)/shard_map/ppermute | solution.py:63
  140.3 25.3 %collective-permute-start.6 = (f32[64,2048]{1,0:T(8,128)S(1)}, f32[64,2048]{1,0:T(8,128)S(1)}, u32[]{:S(2)}, u32[]{:S(2)}) collective-permute-start(f32[64,2048]{1,0:T(8,128)S(1)} %dynamic-slice_add_fusion.9), channel_id=1, source_target_pairs={{0,8},{8,16},{16,24},{24,28},{28,20},{20,12},{12,4},{4,0},{1,9},{9... | collective-permute-start | bytes 1572872 | tf_op jit(solution)/shard_map/ppermute | solution.py:62
  143.5 25.1 %collective-permute-start.13 = (f32[64,2048]{1,0:T(8,128)S(1)}, f32[64,2048]{1,0:T(8,128)S(1)}, u32[]{:S(2)}, u32[]{:S(2)}) collective-permute-start(f32[64,2048]{1,0:T(8,128)S(1)} %dynamic-slice_add_fusion.3), channel_id=1, source_target_pairs={{0,4},{8,0},{16,8},{24,16},{28,24},{20,28},{12,20},{4,12},{1,5},{9... | collective-permute-start | bytes 1572872 | tf_op jit(solution)/shard_map/ppermute | solution.py:63
  166.7 25.1 %collective-permute-start.7 = (f32[64,2048]{1,0:T(8,128)S(1)}, f32[64,2048]{1,0:T(8,128)S(1)}, u32[]{:S(2)}, u32[]{:S(2)}) collective-permute-start(f32[64,2048]{1,0:T(8,128)S(1)} %dynamic-slice_add_fusion.8), channel_id=1, source_target_pairs={{0,8},{8,16},{16,24},{24,28},{28,20},{20,12},{12,4},{4,0},{1,9},{9... | collective-permute-start | bytes 1572872 | tf_op jit(solution)/shard_map/ppermute | solution.py:62
  169.7 24.9 %collective-permute-start.14 = (f32[64,2048]{1,0:T(8,128)S(1)}, f32[64,2048]{1,0:T(8,128)S(1)}, u32[]{:S(2)}, u32[]{:S(2)}) collective-permute-start(f32[64,2048]{1,0:T(8,128)S(1)} %dynamic-slice_add_fusion.2), channel_id=1, source_target_pairs={{0,4},{8,0},{16,8},{24,16},{28,24},{20,28},{12,20},{4,12},{1,5},{9... | collective-permute-start | bytes 1572872 | tf_op jit(solution)/shard_map/ppermute | solution.py:63
  192.9 24.9 %collective-permute-start.8 = (f32[64,2048]{1,0:T(8,128)S(1)}, f32[64,2048]{1,0:T(8,128)S(1)}, u32[]{:S(2)}, u32[]{:S(2)}) collective-permute-start(f32[64,2048]{1,0:T(8,128)S(1)} %dynamic-slice_add_fusion.7), channel_id=1, source_target_pairs={{0,8},{8,16},{16,24},{24,28},{28,20},{20,12},{12,4},{4,0},{1,9},{9... | collective-permute-start | bytes 1572872 | tf_op jit(solution)/shard_map/ppermute | solution.py:62
  195.7 24.7 %collective-permute-start.15 = (f32[64,2048]{1,0:T(8,128)S(1)}, f32[64,2048]{1,0:T(8,128)S(1)}, u32[]{:S(2)}, u32[]{:S(2)}) collective-permute-start(f32[64,2048]{1,0:T(8,128)S(1)} %dynamic-slice_add_fusion.1), channel_id=1, source_target_pairs={{0,4},{8,0},{16,8},{24,16},{28,24},{20,28},{12,20},{4,12},{1,5},{9... | collective-permute-start | bytes 1572872 | tf_op jit(solution)/shard_map/ppermute | solution.py:63
  218.9 17.6 %collective-permute-start.9 = (f32[64,2048]{1,0:T(8,128)S(1)}, f32[64,2048]{1,0:T(8,128)S(1)}, u32[]{:S(2)}, u32[]{:S(2)}) collective-permute-start(f32[64,2048]{1,0:T(8,128)S(1)} %dynamic-slice_add_fusion.6), channel_id=1, source_target_pairs={{0,8},{8,16},{16,24},{24,28},{28,20},{20,12},{12,4},{4,0},{1,9},{9... | collective-permute-start | bytes 1572872 | tf_op jit(solution)/shard_map/ppermute | solution.py:62
  221.6 16.0 %collective-permute-start.16 = (f32[64,2048]{1,0:T(8,128)S(1)}, f32[64,2048]{1,0:T(8,128)S(1)}, u32[]{:S(2)}, u32[]{:S(2)}) collective-permute-start(f32[64,2048]{1,0:T(8,128)S(1)} %dynamic-slice_add_fusion), channel_id=1, source_target_pairs={{0,4},{8,0},{16,8},{24,16},{28,24},{20,28},{12,20},{4,12},{1,5},{9... | collective-permute-start | bytes 1572872 | tf_op jit(solution)/shard_map/ppermute | solution.py:63
  275.0 43.1 %collective-permute-start = (bf16[896,1024]{1,0:T(8,128)(2,1)}, bf16[896,1024]{1,0:T(8,128)(2,1)S(1)}, u32[]{:S(2)}, u32[]{:S(2)}) collective-permute-start(bf16[896,1024]{1,0:T(8,128)(2,1)} %get-tuple-element.27), channel_id=1, source_target_pairs={{0,1},{1,0},{2,3},{3,2},{4,5},{5,4},{6,7},{7,6},{8,9},{9,8},{10,11... | collective-permute-start | bytes 5505032 | tf_op jit(solution)/shard_map/ppermute | solution.py:129
  311.5 43.2 %collective-permute-start.17 = (bf16[896,1024]{1,0:T(8,128)(2,1)}, bf16[896,1024]{1,0:T(8,128)(2,1)}, u32[]{:S(2)}, u32[]{:S(2)}) collective-permute-start(bf16[896,1024]{1,0:T(8,128)(2,1)} %get-tuple-element.29), channel_id=1, source_target_pairs={{0,1},{1,0},{2,3},{3,2},{4,5},{5,4},{6,7},{7,6},{8,9},{9,8},{10,11... | collective-permute-start | bytes 5505032 | tf_op jit(solution)/shard_map/ppermute | solution.py:129
  322.6 32.2 %copy-start.1 = (f32[896,1024]{1,0:T(8,128)S(1)}, f32[896,1024]{1,0:T(8,128)}, u32[]{:S(2)}) copy-start(f32[896,1024]{1,0:T(8,128)} %get-tuple-element.30) | copy-start | bytes 11010052
  (1 other events, 1.2 us)
Sparse Core Ops, SparseCore 0:
  8.9 223.9 all-gather.2
  239.6 74.2 all-gather.4

commit v12 on v11

--- a/solution.py
+++ b/solution.py
@@ -64,8 +64,13 @@
     return jnp.concatenate([buf_a, buf_b], axis=1)
 
 
-def correction_kernel(seg, at_ref, g_ref, corr_ref, *rest):
-    out_ref = rest[-1]
+def correction_kernel(seg, part_ref, recv_ref, g_ref, corr_ref, *rest):
+    out_ref, at_ref = rest[-2], rest[-1]
+
+    @pl.when(pl.program_id(0) == 0)
+    def _():
+        at_ref[...] = (part_ref[...] + recv_ref[...].astype(jnp.float32)).astype(jnp.bfloat16)
+
     total = None
     for s in range(SEQS):
         cols = slice(s * seg, (s + 1) * seg)
@@ -74,34 +79,38 @@
     out_ref[...] = corr_ref[...] + total * (1.0 / (SEQS * SEQ_LEN))
 
 
-def correction(at, g, corr, piece, prev=None, tm=1024):
-    kp, t = at.shape
+def correction(part, recv, g, corr, piece, prev=None, tm=1024):
+    kp, t = part.shape
     m = g.shape[1]
     tm = min(tm, m)
     seg = t // SEQS
     in_specs = [
         pl.BlockSpec((kp, t), lambda j: (0, 0)),
+        pl.BlockSpec((kp, t), lambda j: (0, 0)),
         pl.BlockSpec((t, tm), lambda j: (0, j)),
         pl.BlockSpec((kp, tm), lambda j: (piece, j)),
     ]
-    args = [at, g, corr]
+    args = [part, recv, g, corr]
     aliases = {}
     if prev is not None:
         in_specs.append(pl.BlockSpec(memory_space=pl.ANY))
         args.append(prev)
-        aliases = {3: 0}
+        aliases = {4: 0}
     return pl.pallas_call(
         functools.partial(correction_kernel, seg),
         out_shape=jax.ShapeDtypeStruct(corr.shape, jnp.float32),
         grid=(m // tm,),
         in_specs=in_specs,
         out_specs=pl.BlockSpec((kp, tm), lambda j: (piece, j)),
+        scratch_shapes=[pltpu.VMEM((kp, t), jnp.bfloat16)],
         input_output_aliases=aliases,
-        compiler_params=pltpu.CompilerParams(vmem_limit_bytes=48 * 1024 * 1024),
+        compiler_params=pltpu.CompilerParams(
+            vmem_limit_bytes=56 * 1024 * 1024, dimension_semantics=("arbitrary",)
+        ),
         cost_estimate=pl.CostEstimate(
             flops=2 * kp * t * m + 3 * kp * m,
             transcendentals=0,
-            bytes_accessed=2 * kp * t + 2 * t * m + 8 * kp * m,
+            bytes_accessed=6 * kp * t + 2 * t * m + 8 * kp * m,
         ),
     )(*args)
 
@@ -155,10 +164,11 @@
             recv = recvs[i]
             if out is not None:
                 out, recv = lax.optimization_barrier((out, recv))
-            act_t = (parts[i] + recv.astype(jnp.float32)).astype(jnp.bfloat16)
+            part = parts[i]
         else:
-            act_t = lax.psum(parts[i], "col").astype(jnp.bfloat16)
-        out = correction(act_t, grad_rot, corr, i, out)
+            part = lax.psum(parts[i], "col")
+            recv = jnp.zeros(part.shape, jnp.bfloat16)
+        out = correction(part, recv, grad_rot, corr, i, out)
     return out
 
 

time: 382 us -> 383 us (level)
  other arithmetic: 22.7 us -> 17.8 us
    convert_element_type x2 -> x0, other arithmetic: 5.45 us -> none  [local(): act_t = (parts[i] + recv.astype(jnp.float32)).astype(jnp.bfloat16)]
  transfers between devices with their start and end apart: 20 -> 20, of which waited for: 16 -> 18; matrix products, arithmetic and copies ran while one was open for 30% -> 29% of each run, Pallas kernels for 4% -> 5%
where the time goes in v12:
time: 383 us; the launch traced here: 381 us
  waiting for transfers between devices  181 us (47%)
  matrix products  86.6 us (23%)
  Pallas kernels  37 us (10%)
  between operations  30.6 us (8%)
  starting transfers between devices  20.2 us (5%)
  other arithmetic  17.8 us (5%)
  local copies, waits for them, and re-layouts  8.52 us (2%)
    ppermute x7, waiting for transfers between devices, ring_reduce_scatter(): buf_a = lax.ppermute(buf_a, axis, right) + block(xa, p - 1 - s + 2 * n)  136 us
    dot_general x2, matrix products, local(): lax.dot_general(basis_in[i * kp:(i + 1) * kp], gathered, (((1,), (1,)), (...  70.6 us
    pallas_call x2, Pallas kernels, correction(): pl.pallas_call(functools.partial(correction_kernel, seg), out_shape=jax.S...  37 us
    ppermute x2, waiting for transfers between devices, local(): recvs.append(lax.ppermute(part.astype(jnp.bfloat16), 'col', swap_perm(2)))  22.2 us
    ppermute x1, waiting for transfers between devices, local(): other = lax.ppermute(grads, 'col', swap_perm(2))  12.1 us
    ppermute x7, starting transfers between devices, ring_reduce_scatter(): buf_a = lax.ppermute(buf_a, axis, right) + block(xa, p - 1 - s + 2 * n)  11.9 us
    dot_general x1, matrix products, local(): lax.dot_general(send_rows, basis_out, dims, preferred_element_type=jnp.fl...  8.32 us
  transfers between devices with their start and end apart: 20, of which 18 were waited for; matrix products, arithmetic and copies ran while one was open for 29% of the time, Pallas kernels for 5%

profile of v12, /device:TPU:0, one launch (start us, length us, event | category | flops | bytes accessed | tf_op | source)
XLA Modules:
  0.0 381.4 jit_solution(12216994235245648685)
XLA Ops:
  7.3 3.0 collective-permute-start.1
  10.3 12.1 %collective-permute-done.1 = bf16[512,512]{1,0:T(8,128)(2,1)S(1)} collective-permute-done((bf16[512,512]{1,0:T(8,128)(2,1)}, bf16[512,512]{1,0:T(8,128)(2,1)S(1)}, u32[]{:S(2)}, u32[]{:S(2)}) %collective-permute-start.1) | collective-permute-done | bytes 524320 | tf_op jit(solution)/shard_map/ppermute | solution.py:141
  23.6 8.3 %fusion.5 = f32[512,4096]{1,0:T(8,128)} fusion(bf16[4096,512]{1,0:T(8,128)(2,1)} %param.10, s32[]{:T(128)S(6)} %select_n.176, bf16[512,512]{1,0:T(8,128)(2,1)S(1)} %get-tuple-element.12, bf16[512,512]{1,0:T(8,128)(2,1)S(1)} %get-tuple-element.11), kind=kOutput, calls=%fused_computation.10 | convolution fusion | flops 2148532224 | bytes 13631492 | tf_op jit(solution)/shard_map/dot_general | solution.py:153
  42.2 5.2 %collective-permute-done.2 = f32[512,4096]{1,0:T(8,128)} collective-permute-done((f32[512,4096]{1,0:T(8,128)}, f32[512,4096]{1,0:T(8,128)}, u32[]{:S(2)}, u32[]{:S(2)}) %collective-permute-start.2) | collective-permute-done | bytes 8388640 | tf_op jit(solution)/shard_map/ppermute | solution.py:154
  47.4 7.6 %convolution_add_fusion = f32[512,4096]{1,0:T(8,128)S(1)} fusion(f32[512,4096]{1,0:T(8,128)} %collective-permute-done.2, bf16[4096,512]{1,0:T(8,128)(2,1)} %param.10, s32[]{:T(128)S(6)} %select_n.175, bf16[512,512]{1,0:T(8,128)(2,1)S(1)} %get-tuple-element.12, bf16[512,512]{1,0:T(8,128)(2,1)S(1)} %get-tuple-element.11), kind=kOutput, calls=%fused_computation.4 | convolution fusion | flops 2150629376 | bytes 22020100 | tf_op jit(solution)/shard_map/dot_general | solution.py:156
  55.0 2.9 fusion.13
  57.9 2.0 copy-done
  59.9 1.9 collective-permute-start.3
  65.1 20.7 %collective-permute-done.3 = f32[64,2048]{1,0:T(8,128)S(1)} collective-permute-done((f32[64,2048]{1,0:T(8,128)S(1)}, f32[64,2048]{1,0:T(8,128)S(1)}, u32[]{:S(2)}, u32[]{:S(2)}) %collective-permute-start.3) | collective-permute-done | bytes 524320 | tf_op jit(solution)/shard_map/ppermute | solution.py:62
  86.9 1.8 collective-permute-start.4
  92.0 20.6 %collective-permute-done.4 = f32[64,2048]{1,0:T(8,128)S(1)} collective-permute-done((f32[64,2048]{1,0:T(8,128)S(1)}, f32[64,2048]{1,0:T(8,128)S(1)}, u32[]{:S(2)}, u32[]{:S(2)}) %collective-permute-start.4) | collective-permute-done | bytes 524320 | tf_op jit(solution)/shard_map/ppermute | solution.py:62
  113.7 1.8 collective-permute-start.5
  118.8 20.5 %collective-permute-done.5 = f32[64,2048]{1,0:T(8,128)S(1)} collective-permute-done((f32[64,2048]{1,0:T(8,128)S(1)}, f32[64,2048]{1,0:T(8,128)S(1)}, u32[]{:S(2)}, u32[]{:S(2)}) %collective-permute-start.5) | collective-permute-done | bytes 524320 | tf_op jit(solution)/shard_map/ppermute | solution.py:62
  145.3 20.3 %collective-permute-done.6 = f32[64,2048]{1,0:T(8,128)S(1)} collective-permute-done((f32[64,2048]{1,0:T(8,128)S(1)}, f32[64,2048]{1,0:T(8,128)S(1)}, u32[]{:S(2)}, u32[]{:S(2)}) %collective-permute-start.6) | collective-permute-done | bytes 524320 | tf_op jit(solution)/shard_map/ppermute | solution.py:62
  171.7 20.2 %collective-permute-done.7 = f32[64,2048]{1,0:T(8,128)S(1)} collective-permute-done((f32[64,2048]{1,0:T(8,128)S(1)}, f32[64,2048]{1,0:T(8,128)S(1)}, u32[]{:S(2)}, u32[]{:S(2)}) %collective-permute-start.7) | collective-permute-done | bytes 524320 | tf_op jit(solution)/shard_map/ppermute | solution.py:62
  197.2 20.7 %collective-permute-done.8 = f32[64,2048]{1,0:T(8,128)S(1)} collective-permute-done((f32[64,2048]{1,0:T(8,128)S(1)}, f32[64,2048]{1,0:T(8,128)S(1)}, u32[]{:S(2)}, u32[]{:S(2)}) %collective-permute-start.8) | collective-permute-done | bytes 524320 | tf_op jit(solution)/shard_map/ppermute | solution.py:62
  223.2 13.3 %collective-permute-done.9 = f32[64,2048]{1,0:T(8,128)S(1)} collective-permute-done((f32[64,2048]{1,0:T(8,128)S(1)}, f32[64,2048]{1,0:T(8,128)S(1)}, u32[]{:S(2)}, u32[]{:S(2)}) %collective-permute-start.9) | collective-permute-done | bytes 524320 | tf_op jit(solution)/shard_map/ppermute | solution.py:62
  239.6 35.5 %fusion.15 = (bf16[896,1024]{1,0:T(8,128)(2,1)}, f32[896,1024]{1,0:T(8,128)}) fusion(bf16[1024,14336]{1,0:T(8,128)(2,1)} %all-gather.3.cloned.1.call-done, bf16[1792,14336]{1,0:T(8,128)(2,1)} %param.9), kind=kOutput, calls=%fused_computation.37 | convolution fusion | flops 26307592192 | bytes 60555264 | tf_op jit(solution)/shard_map/dot_general | solution.py:132
  276.5 35.2 %fusion.16 = (bf16[896,1024]{1,0:T(8,128)(2,1)}, f32[896,1024]{1,0:T(8,128)}) fusion(bf16[1024,14336]{1,0:T(8,128)(2,1)} %all-gather.3.cloned.1.call-done, bf16[1792,14336]{1,0:T(8,128)(2,1)} %param.9), kind=kOutput, calls=%fused_computation.38 | convolution fusion | flops 26307592192 | bytes 60555264 | tf_op jit(solution)/shard_map/dot_general | solution.py:132
  312.2 1.8 all-gather.5.cloned.1.call-done.g_ref
  314.0 4.2 %collective-permute-done.recv_ref = bf16[896,1024]{1,0:T(8,128)(2,1)} collective-permute-done((bf16[896,1024]{1,0:T(8,128)(2,1)}, bf16[896,1024]{1,0:T(8,128)(2,1)}, u32[]{:S(2)}, u32[]{:S(2)}) %collective-permute-start) | collective-permute-done | bytes 1835040 | tf_op jit(solution)/shard_map/ppermute | solution.py:138
  318.3 18.5 %shard_map.73.rest_0_ = f32[1792,4096]{1,0:T(8,128)} custom-call(f32[896,1024]{1,0:T(8,128)} %get-tuple-element.28.part_ref, bf16[896,1024]{1,0:T(8,128)(2,1)} %collective-permute-done.recv_ref, bf16[1024,4096]{1,0:T(8,128)(2,1)} %all-gather.5.cloned.1.call-done.g_ref, f32[1792,4096]{1,0:T(8,128)} %corr_ref.3), custom_call_target="tpu_custom_call" | custom-call | flops 7527202816 | bytes 43253760 | tf_op jit(solution)/shard_map/pallas_call | solution.py:99
  336.8 18.0 %collective-permute-done.17.recv_ref = bf16[896,1024]{1,0:T(8,128)(2,1)S(1)} collective-permute-done((bf16[896,1024]{1,0:T(8,128)(2,1)}, bf16[896,1024]{1,0:T(8,128)(2,1)S(1)}, u32[]{:S(2)}, u32[]{:S(2)}) %collective-permute-start.17) | collective-permute-done | bytes 1835040 | tf_op jit(solution)/shard_map/ppermute | solution.py:138
  356.0 18.5 %shard_map.74 = f32[1792,4096]{1,0:T(8,128)} custom-call(f32[896,1024]{1,0:T(8,128)} %get-tuple-element.30.part_ref, bf16[896,1024]{1,0:T(8,128)(2,1)} %copy-done.1, bf16[1024,4096]{1,0:T(8,128)(2,1)} %all-gather.5.cloned.1.call-done.g_ref, f32[1792,4096]{1,0:T(8,128)} %corr_ref.3, f32[1792,4096]{1,0:T(8,128)} %shard_map.73.rest_0_), custom_call_target="tpu_custom_call", output_to_operand_aliasing={{}: (4, {})} | custom-call | flops 7527202816 | bytes 43253760 | tf_op jit(solution)/shard_map/pallas_call | solution.py:99
  (53 shorter events, 36.1 us)
Async XLA Ops:
  6.5 233.1 %all-gather.3.cloned.1.call-start = ((), (), s32[]{:S(2)}) async-start(), calls=%async_computation | async-start | bytes 31195136 | tf_op jit(solution)/shard_map/all_gather | solution.py:127
  7.3 306.8 %all-gather.5.cloned.1.call-start = ((), (), s32[]{:S(2)}) async-start(), calls=%async_computation.1 | async-start | bytes 8912896 | tf_op jit(solution)/shard_map/all_gather | solution.py:159
  7.3 15.2 %collective-permute-start.1 = (bf16[512,512]{1,0:T(8,128)(2,1)}, bf16[512,512]{1,0:T(8,128)(2,1)S(1)}, u32[]{:S(2)}, u32[]{:S(2)}) collective-permute-start(bf16[512,512]{1,0:T(8,128)(2,1)} %param.8), channel_id=1, source_target_pairs={{0,1},{1,0},{2,3},{3,2},{4,5},{5,4},{6,7},{7,6},{8,9},{9,8},{10,11... | collective-permute-start | bytes 1572872 | tf_op jit(solution)/shard_map/ppermute | solution.py:141
  23.6 8.4 %copy-start.3 = (s32[8]{0:T(128)S(1)}, s32[8]{0:T(128)}, u32[]{:S(2)}) copy-start(s32[8]{0:T(128)} %constant.178.clone) | copy-start | bytes 100
  23.6 17.3 %copy-start.2 = (s32[8]{0:T(128)S(1)}, s32[8]{0:T(128)}, u32[]{:S(2)}) copy-start(s32[8]{0:T(128)} %constant.177.clone) | copy-start | bytes 100
  31.9 15.5 %collective-permute-start.2 = (f32[512,4096]{1,0:T(8,128)}, f32[512,4096]{1,0:T(8,128)}, u32[]{:S(2)}, u32[]{:S(2)}) collective-permute-start(f32[512,4096]{1,0:T(8,128)} %fusion.5), channel_id=1, source_target_pairs={{0,2},{2,0},{1,3},{3,1},{4,6},{6,4},{5,7},{7,5},{8,10},{10,8},{9,1... | collective-permute-start | bytes 25165832 | tf_op jit(solution)/shard_map/ppermute | solution.py:154
  57.9 2.0 copy-start
  59.9 25.9 %collective-permute-start.3 = (f32[64,2048]{1,0:T(8,128)S(1)}, f32[64,2048]{1,0:T(8,128)S(1)}, u32[]{:S(2)}, u32[]{:S(2)}) collective-permute-start(f32[64,2048]{1,0:T(8,128)S(1)} %constant_dynamic-slice_fusion.1), channel_id=1, source_target_pairs={{0,8},{8,16},{16,24},{24,28},{28,20},{20,12},{12,4},{4,0},{1,9},{9... | collective-permute-start | bytes 1572872 | tf_op jit(solution)/shard_map/ppermute | solution.py:62
  63.5 25.8 %collective-permute-start.10 = (f32[64,2048]{1,0:T(8,128)S(1)}, f32[64,2048]{1,0:T(8,128)S(1)}, u32[]{:S(2)}, u32[]{:S(2)}) collective-permute-start(f32[64,2048]{1,0:T(8,128)S(1)} %constant_dynamic-slice_fusion), channel_id=1, source_target_pairs={{0,4},{8,0},{16,8},{24,16},{28,24},{20,28},{12,20},{4,12},{1,5},{9... | collective-permute-start | bytes 1572872 | tf_op jit(solution)/shard_map/ppermute | solution.py:63
  86.9 25.7 %collective-permute-start.4 = (f32[64,2048]{1,0:T(8,128)S(1)}, f32[64,2048]{1,0:T(8,128)S(1)}, u32[]{:S(2)}, u32[]{:S(2)}) collective-permute-start(f32[64,2048]{1,0:T(8,128)S(1)} %dynamic-slice_add_fusion.11), channel_id=1, source_target_pairs={{0,8},{8,16},{16,24},{24,28},{28,20},{20,12},{12,4},{4,0},{1,9},{9... | collective-permute-start | bytes 1572872 | tf_op jit(solution)/shard_map/ppermute | solution.py:62
  90.5 25.6 %collective-permute-start.11 = (f32[64,2048]{1,0:T(8,128)S(1)}, f32[64,2048]{1,0:T(8,128)S(1)}, u32[]{:S(2)}, u32[]{:S(2)}) collective-permute-start(f32[64,2048]{1,0:T(8,128)S(1)} %dynamic-slice_add_fusion.5), channel_id=1, source_target_pairs={{0,4},{8,0},{16,8},{24,16},{28,24},{20,28},{12,20},{4,12},{1,5},{9... | collective-permute-start | bytes 1572872 | tf_op jit(solution)/shard_map/ppermute | solution.py:63
  113.7 25.5 %collective-permute-start.5 = (f32[64,2048]{1,0:T(8,128)S(1)}, f32[64,2048]{1,0:T(8,128)S(1)}, u32[]{:S(2)}, u32[]{:S(2)}) collective-permute-start(f32[64,2048]{1,0:T(8,128)S(1)} %dynamic-slice_add_fusion.10), channel_id=1, source_target_pairs={{0,8},{8,16},{16,24},{24,28},{28,20},{20,12},{12,4},{4,0},{1,9},{9... | collective-permute-start | bytes 1572872 | tf_op jit(solution)/shard_map/ppermute | solution.py:62
  117.1 25.3 %collective-permute-start.12 = (f32[64,2048]{1,0:T(8,128)S(1)}, f32[64,2048]{1,0:T(8,128)S(1)}, u32[]{:S(2)}, u32[]{:S(2)}) collective-permute-start(f32[64,2048]{1,0:T(8,128)S(1)} %dynamic-slice_add_fusion.4), channel_id=1, source_target_pairs={{0,4},{8,0},{16,8},{24,16},{28,24},{20,28},{12,20},{4,12},{1,5},{9... | collective-permute-start | bytes 1572872 | tf_op jit(solution)/shard_map/ppermute | solution.py:63
  140.4 25.3 %collective-permute-start.6 = (f32[64,2048]{1,0:T(8,128)S(1)}, f32[64,2048]{1,0:T(8,128)S(1)}, u32[]{:S(2)}, u32[]{:S(2)}) collective-permute-start(f32[64,2048]{1,0:T(8,128)S(1)} %dynamic-slice_add_fusion.9), channel_id=1, source_target_pairs={{0,8},{8,16},{16,24},{24,28},{28,20},{20,12},{12,4},{4,0},{1,9},{9... | collective-permute-start | bytes 1572872 | tf_op jit(solution)/shard_map/ppermute | solution.py:62
  143.6 25.1 %collective-permute-start.13 = (f32[64,2048]{1,0:T(8,128)S(1)}, f32[64,2048]{1,0:T(8,128)S(1)}, u32[]{:S(2)}, u32[]{:S(2)}) collective-permute-start(f32[64,2048]{1,0:T(8,128)S(1)} %dynamic-slice_add_fusion.3), channel_id=1, source_target_pairs={{0,4},{8,0},{16,8},{24,16},{28,24},{20,28},{12,20},{4,12},{1,5},{9... | collective-permute-start | bytes 1572872 | tf_op jit(solution)/shard_map/ppermute | solution.py:63
  166.8 25.1 %collective-permute-start.7 = (f32[64,2048]{1,0:T(8,128)S(1)}, f32[64,2048]{1,0:T(8,128)S(1)}, u32[]{:S(2)}, u32[]{:S(2)}) collective-permute-start(f32[64,2048]{1,0:T(8,128)S(1)} %dynamic-slice_add_fusion.8), channel_id=1, source_target_pairs={{0,8},{8,16},{16,24},{24,28},{28,20},{20,12},{12,4},{4,0},{1,9},{9... | collective-permute-start | bytes 1572872 | tf_op jit(solution)/shard_map/ppermute | solution.py:62
  169.9 24.9 %collective-permute-start.14 = (f32[64,2048]{1,0:T(8,128)S(1)}, f32[64,2048]{1,0:T(8,128)S(1)}, u32[]{:S(2)}, u32[]{:S(2)}) collective-permute-start(f32[64,2048]{1,0:T(8,128)S(1)} %dynamic-slice_add_fusion.2), channel_id=1, source_target_pairs={{0,4},{8,0},{16,8},{24,16},{28,24},{20,28},{12,20},{4,12},{1,5},{9... | collective-permute-start | bytes 1572872 | tf_op jit(solution)/shard_map/ppermute | solution.py:63
  193.0 24.9 %collective-permute-start.8 = (f32[64,2048]{1,0:T(8,128)S(1)}, f32[64,2048]{1,0:T(8,128)S(1)}, u32[]{:S(2)}, u32[]{:S(2)}) collective-permute-start(f32[64,2048]{1,0:T(8,128)S(1)} %dynamic-slice_add_fusion.7), channel_id=1, source_target_pairs={{0,8},{8,16},{16,24},{24,28},{28,20},{20,12},{12,4},{4,0},{1,9},{9... | collective-permute-start | bytes 1572872 | tf_op jit(solution)/shard_map/ppermute | solution.py:62
  196.0 24.7 %collective-permute-start.15 = (f32[64,2048]{1,0:T(8,128)S(1)}, f32[64,2048]{1,0:T(8,128)S(1)}, u32[]{:S(2)}, u32[]{:S(2)}) collective-permute-start(f32[64,2048]{1,0:T(8,128)S(1)} %dynamic-slice_add_fusion.1), channel_id=1, source_target_pairs={{0,4},{8,0},{16,8},{24,16},{28,24},{20,28},{12,20},{4,12},{1,5},{9... | collective-permute-start | bytes 1572872 | tf_op jit(solution)/shard_map/ppermute | solution.py:63
  219.1 17.4 %collective-permute-start.9 = (f32[64,2048]{1,0:T(8,128)S(1)}, f32[64,2048]{1,0:T(8,128)S(1)}, u32[]{:S(2)}, u32[]{:S(2)}) collective-permute-start(f32[64,2048]{1,0:T(8,128)S(1)} %dynamic-slice_add_fusion.6), channel_id=1, source_target_pairs={{0,8},{8,16},{16,24},{24,28},{28,20},{20,12},{12,4},{4,0},{1,9},{9... | collective-permute-start | bytes 1572872 | tf_op jit(solution)/shard_map/ppermute | solution.py:62
  221.8 15.7 %collective-permute-start.16 = (f32[64,2048]{1,0:T(8,128)S(1)}, f32[64,2048]{1,0:T(8,128)S(1)}, u32[]{:S(2)}, u32[]{:S(2)}) collective-permute-start(f32[64,2048]{1,0:T(8,128)S(1)} %dynamic-slice_add_fusion), channel_id=1, source_target_pairs={{0,4},{8,0},{16,8},{24,16},{28,24},{20,28},{12,20},{4,12},{1,5},{9... | collective-permute-start | bytes 1572872 | tf_op jit(solution)/shard_map/ppermute | solution.py:63
  275.1 43.2 %collective-permute-start = (bf16[896,1024]{1,0:T(8,128)(2,1)}, bf16[896,1024]{1,0:T(8,128)(2,1)}, u32[]{:S(2)}, u32[]{:S(2)}) collective-permute-start(bf16[896,1024]{1,0:T(8,128)(2,1)} %get-tuple-element.27), channel_id=1, source_target_pairs={{0,1},{1,0},{2,3},{3,2},{4,5},{5,4},{6,7},{7,6},{8,9},{9,8},{10,11... | collective-permute-start | bytes 5505032 | tf_op jit(solution)/shard_map/ppermute | solution.py:138
  311.7 43.1 %collective-permute-start.17 = (bf16[896,1024]{1,0:T(8,128)(2,1)}, bf16[896,1024]{1,0:T(8,128)(2,1)S(1)}, u32[]{:S(2)}, u32[]{:S(2)}) collective-permute-start(bf16[896,1024]{1,0:T(8,128)(2,1)} %get-tuple-element.29), channel_id=1, source_target_pairs={{0,1},{1,0},{2,3},{3,2},{4,5},{5,4},{6,7},{7,6},{8,9},{9,8},{10,11... | collective-permute-start | bytes 5505032 | tf_op jit(solution)/shard_map/ppermute | solution.py:138
  354.8 1.3 copy-start.1
Sparse Core Ops, SparseCore 0:
  8.9 223.8 all-gather.2
  239.7 74.2 all-gather.4
